TPU v7x, 512 devices: a whole 4x8x8 slice. The times are simulated.
512 devices in a mesh: section: 8 (over y), expert: 32 (over z, x_hi, core), dp: 2 (over x_lo).
Axes of the slice: x: 4 (x_hi: 2, x_lo: 2; x = x_hi * 2 + x_lo), y: 8, z: 8, core: 2. Of those that a mesh axis runs over, the one named last changes fastest.
Arguments:
- blocks: bfloat16 [8, 512, 7168], P('section', ('expert', 'dp')), may hold values from -6 to 6
- gains: float32 [8, 7168], P('section'), may hold values from 0.1 to 1.9
- w_gate: bfloat16 [8, 7168, 4096], P('section', 'dp', 'expert'), may hold values from -0.0625 to 0.0625
- w_up: bfloat16 [8, 7168, 4096], P('section', 'dp', 'expert'), may hold values from -0.0625 to 0.0625
- w_down: bfloat16 [8, 7168, 4096], P('section', 'dp', 'expert'), may hold values from -0.1875 to 0.1875
- expert_ids: int32 [8, 2, 512, 2], P('section', None, ('expert', 'dp')), may hold values from 0 to 3, all different within a row; in each aligned block of 8 rows (0 to 7, 8 to 15, ..., all dimensions but the last counted through in order) at most 5 rows name the same one
- combine: float32 [8, 2, 512, 2], P('section', None, ('expert', 'dp')), may hold values from 0.2 to 1
Outputs:
- finished: bfloat16 [8, 512, 7168], P('section', ('expert', 'dp'))
Inputs may be any that keep to these rules, and one draw needn't show every extreme that they name: `expert_ids`: each token names 2 different experts; within the 8 tokens of one device (aligned blocks), no expert is named more than 5 times, a bound that some block reaches.
All inputs are finite; a program needn't handle non-finite values.
Results may differ from a plain program's by a relative error of at most 0.0073.
Values may be sent and summed in bfloat16 or wider, within the bound.
No kernel may reach another device: no remote copies, remote signals or barrier semaphores. Data moves between devices by JAX's collectives and lax.ppermute only.
A program may use at most 64 MiB of HBM per device.

v0:
```python
from functools import partial

import jax
import jax.numpy as jnp
from jax import lax
from jax.sharding import PartitionSpec as P


def passed_along(array, axis, by):
    length = lax.axis_size(axis)
    return lax.ppermute(array, axis, [(i, (i + by) % length) for i in range(length)])


def expert_rows(arrived, gate_full, up_full, down_full):
    sources, slot_count, model_width = arrived.shape
    flat_rows = arrived.reshape(sources * slot_count, model_width)
    gate_act = jnp.dot(flat_rows, gate_full, preferred_element_type=jnp.float32)
    upward = jnp.dot(flat_rows, up_full, preferred_element_type=jnp.float32)
    hidden = (jax.nn.silu(gate_act) * upward).astype(jnp.bfloat16)
    output = lax.dot_general(
        hidden, down_full, (((1,), (1,)), ((), ())), preferred_element_type=jnp.float32
    )
    output = output.astype(jnp.bfloat16).reshape(sources, slot_count, model_width)
    return lax.all_to_all(output, "expert", split_axis=0, concat_axis=0, tiled=True)


def moe_layer(stream, gain_row, weights, routes, mixing):
    owners = lax.axis_size("expert")
    experts = max(2, owners // 8)
    span = owners // experts
    tok_rows, model_width = stream.shape
    fan_out = routes.shape[1]
    capacity = min(tok_rows, max(2, 5 * tok_rows * fan_out // (4 * experts)))
    widened = stream.astype(jnp.float32)
    inv_rms = lax.rsqrt(jnp.mean(widened * widened, axis=1, keepdims=True) + 1e-06)
    normed = (widened * inv_rms * gain_row[None, :]).astype(jnp.bfloat16)
    flat_ids = routes.reshape(-1)
    count_all = flat_ids.shape[0]
    chosen = (flat_ids[:, None] == jnp.arange(experts, dtype=jnp.int32)[None, :]).astype(
        jnp.float32
    )
    triangle = (jnp.arange(count_all)[:, None] >= jnp.arange(count_all)[None, :]).astype(
        jnp.float32
    )
    running = jnp.dot(triangle, chosen, preferred_element_type=jnp.float32)
    slot_of = jnp.sum(chosen * (running - 1.0), axis=1).astype(jnp.int32)
    target = flat_ids * capacity + slot_of
    placing = jnp.arange(experts * capacity, dtype=jnp.int32)[:, None] == target[None, :]
    placing = (
        placing.reshape(experts * capacity, tok_rows, fan_out).any(axis=2).astype(jnp.bfloat16)
    )
    outgoing = jnp.dot(placing, normed, preferred_element_type=jnp.float32).astype(jnp.bfloat16)
    outgoing = jnp.repeat(outgoing.reshape(experts, capacity, model_width), span, axis=0)
    gate_full, up_full, down_full = weights
    worker = partial(expert_rows, gate_full=gate_full, up_full=up_full, down_full=down_full)
    returned = worker(lax.all_to_all(outgoing, "expert", split_axis=0, concat_axis=0, tiled=True))
    summed = jnp.sum(
        returned.reshape(experts, span, capacity, model_width).astype(jnp.float32), axis=1
    )
    expert_out = summed.astype(jnp.bfloat16).reshape(experts * capacity, model_width)
    picked = jnp.take(expert_out, target, axis=0)
    picked = picked.reshape(tok_rows, fan_out, model_width)
    mixed_sum = jnp.sum(mixing[:, :, None] * picked.astype(jnp.float32), axis=1)
    return (widened + mixed_sum).astype(jnp.bfloat16)


def on_device(blocks, gains, w_gate, w_up, w_down, expert_ids, combine):
    stream = blocks[0]
    turns = expert_ids.shape[1]
    weights = None
    for layer_turn in range(turns):
        if layer_turn > 0:
            stream = passed_along(stream, "section", 1)
        weights = (
            lax.all_gather(w_gate[0], "dp", axis=0, tiled=True),
            lax.all_gather(w_up[0], "dp", axis=0, tiled=True),
            lax.all_gather(w_down[0], "dp", axis=0, tiled=True),
        )
        stream = moe_layer(
            stream, gains[0], weights, expert_ids[0, layer_turn], combine[0, layer_turn]
        )
    return stream[None]


def solution(mesh):
    in_specs = (
        P("section", ("expert", "dp"), None),
        P("section", None),
        P("section", "dp", "expert"),
        P("section", "dp", "expert"),
        P("section", "dp", "expert"),
        P("section", None, ("expert", "dp"), None),
        P("section", None, ("expert", "dp"), None),
    )
    out_specs = P("section", ("expert", "dp"), None)
    return jax.shard_map(
        on_device, mesh=mesh, in_specs=in_specs, out_specs=out_specs, check_vma=False
    )
```

profile of v0, /device:TPU:1, one launch (start us, length us, event | category | flops | bytes accessed | tf_op | source)
XLA Modules:
  0.0 485.0 jit_solution(11815583365687878870)
XLA Ops:
  6.5 0.7 all-gather.7.cloned.1.call-update
  7.3 0.7 fusion.64
  8.1 0.1 fusion.28
  8.4 0.1 copy.26
  8.6 0.1 fusion.29
  8.9 0.7 bitcast_add_fusion.1
  9.7 1.1 fusion.34
  10.8 1.2 convolution_convert_fusion.3
  12.0 0.1 reshape.113
  12.1 2.3 broadcast_in_dim.15
  14.4 14.5 %all-to-all-start = ((bf16[32,5,7168]{2,1,0:T(8,128)(2,1)}), bf16[32,5,7168]{2,1,0:T(8,128)(2,1)}, u32[]{:S(2)}, u32[]{:S(2)}) async-start(bf16[32,5,7168]{2,1,0:T(8,128)(2,1)} %bitcast.62), calls=%async_computation | async-start | bytes 7340032 | tf_op jit(solution)/shard_map/all_to_all | solution.py:56
  28.9 0.7 all-gather.11.cloned.1.call-update
  29.7 0.7 all-gather.9.cloned.1.call-update
  30.4 81.6 %all-to-all-done = bf16[32,5,7168]{2,1,0:T(8,128)(2,1)} async-done(((bf16[32,5,7168]{2,1,0:T(8,128)(2,1)}), bf16[32,5,7168]{2,1,0:T(8,128)(2,1)}, u32[]{:S(2)}, u32[]{:S(2)}) %all-to-all-start) | async-done | bytes 2293792 | tf_op jit(solution)/shard_map/all_to_all | solution.py:56
  112.0 3.3 reshape.115
  115.3 2.2 fusion.8
  117.5 1.2 all-gather.11.cloned.1.call-done
  118.7 42.0 %all-gather.9.cloned.1.call-done = bf16[1,7168,128]{2,1,0:T(8,128)(2,1)} async-done(((bf16[1,3584,128]{2,1,0:T(8,128)(2,1)}), bf16[1,7168,128]{2,1,0:T(8,128)(2,1)}) %all-gather.9.cloned.1.call-update) | async-done | bytes 1835024 | tf_op jit(solution)/shard_map/all_gather | solution.py:76
  160.8 4.9 %convolution_convert_fusion.1 = bf16[160,7168]{1,0:T(8,128)(2,1)} fusion(bf16[1,7168,128]{2,1,0:T(8,128)(2,1)} %all-gather.11.cloned.1.call-done, bf16[160,7168]{1,0:T(8,128)(2,1)S(1)} %reshape.115, bf16[1,7168,128]{2,1,0:T(8,128)(2,1)} %all-gather.9.cloned.1.call-done, f32[160,128]{1,0:T(8,128)S(1)} %fusion.8), kind=kOutput, calls=%fused_computation.3 | convolution fusion | flops 588472320 | bytes 8339456 | tf_op jit(solution)/shard_map/dot_general | solution.py:20
  165.7 4.6 reshape.116
  170.2 10.7 %all-to-all-start.1 = ((bf16[32,5,7168]{2,1,0:T(8,128)(2,1)}), bf16[32,5,7168]{2,1,0:T(8,128)(2,1)}, u32[]{:S(2)}, u32[]{:S(2)}) async-start(bf16[32,5,7168]{2,1,0:T(8,128)(2,1)} %reshape.116), calls=%async_computation.1 | async-start | bytes 7340032 | tf_op jit(solution)/shard_map/all_to_all | solution.py:24
  181.0 83.0 %all-to-all-done.1 = bf16[32,5,7168]{2,1,0:T(8,128)(2,1)} async-done(((bf16[32,5,7168]{2,1,0:T(8,128)(2,1)}), bf16[32,5,7168]{2,1,0:T(8,128)(2,1)}, u32[]{:S(2)}, u32[]{:S(2)}) %all-to-all-start.1) | async-done | bytes 2293792 | tf_op jit(solution)/shard_map/all_to_all | solution.py:24
  264.0 2.8 bitcast_reduce_fusion.1
  266.8 0.1 reshape.118
  267.0 0.7 gather_fusion
  267.7 0.1 select_convert_fusion.1
  267.8 0.3 reshape.126
  268.1 0.6 multiply_reduce_fusion.1
  268.7 3.1 collective-permute-start
  271.9 3.5 collective-permute-done
  275.5 0.2 fusion.30
  275.7 0.3 convolution_convert_fusion.2
  276.0 0.1 reshape.119
  276.1 0.4 broadcast_in_dim.16
  276.5 92.8 %all_to_all.20 = bf16[32,5,7168]{2,1,0:T(8,128)(2,1)} all-to-all(bf16[32,5,7168]{2,1,0:T(8,128)(2,1)S(1)} %bitcast.63), channel_id=1, replica_groups=mesh['section'=8,'expert'=32,'dp'=2] {'expert'}, dimensions={0} | all-to-all | bytes 4587520 | tf_op jit(solution)/shard_map/all_to_all | solution.py:56
  369.4 3.3 reshape.121
  372.6 2.2 fusion.6
  374.9 4.9 %convolution_convert_fusion = bf16[160,7168]{1,0:T(8,128)(2,1)} fusion(bf16[1,7168,128]{2,1,0:T(8,128)(2,1)} %all-gather.11.cloned.1.call-done, bf16[160,7168]{1,0:T(8,128)(2,1)S(1)} %reshape.121, bf16[1,7168,128]{2,1,0:T(8,128)(2,1)} %all-gather.9.cloned.1.call-done, f32[160,128]{1,0:T(8,128)S(1)} %fusion.6), kind=kOutput, calls=%fused_computation.2 | convolution fusion | flops 588472320 | bytes 8339456 | tf_op jit(solution)/shard_map/dot_general | solution.py:20
  379.8 4.6 reshape.122
  384.3 5.8 %all-to-all-start.3 = ((bf16[32,5,7168]{2,1,0:T(8,128)(2,1)}), bf16[32,5,7168]{2,1,0:T(8,128)(2,1)}, u32[]{:S(2)}, u32[]{:S(2)}) async-start(bf16[32,5,7168]{2,1,0:T(8,128)(2,1)} %reshape.122), calls=%async_computation.3 | async-start | bytes 7340032 | tf_op jit(solution)/shard_map/all_to_all | solution.py:24
  390.2 83.0 %all-to-all-done.3 = bf16[32,5,7168]{2,1,0:T(8,128)(2,1)} async-done(((bf16[32,5,7168]{2,1,0:T(8,128)(2,1)}), bf16[32,5,7168]{2,1,0:T(8,128)(2,1)}, u32[]{:S(2)}, u32[]{:S(2)}) %all-to-all-start.3) | async-done | bytes 2293792 | tf_op jit(solution)/shard_map/all_to_all | solution.py:24
  473.2 2.8 bitcast_reduce_fusion
  476.0 0.1 reshape.124
  476.1 0.7 gather_fusion.1
  476.8 0.1 select_convert_fusion
  476.9 0.3 reshape.127
  477.2 0.6 multiply_reduce_fusion
  477.8 0.7 fusion.39
  (31 shorter events, 1.1 us)
Async XLA Ops:
  6.5 108.7 %all-gather.7.cloned.1.call-start = ((), (), s32[]{:S(2)}) async-start(), calls=%async_computation.4 | async-start | bytes 2752512 | tf_op jit(solution)/shard_map/all_gather | solution.py:75
  14.4 97.6 %all-to-all-start = ((bf16[32,5,7168]{2,1,0:T(8,128)(2,1)}), bf16[32,5,7168]{2,1,0:T(8,128)(2,1)}, u32[]{:S(2)}, u32[]{:S(2)}) async-start(bf16[32,5,7168]{2,1,0:T(8,128)(2,1)} %bitcast.62), calls=%async_computation | async-start | bytes 7340032 | tf_op jit(solution)/shard_map/all_to_all | solution.py:56
  28.9 89.9 %all-gather.11.cloned.1.call-start = ((), (), s32[]{:S(2)}) async-start(), calls=%async_computation.6 | async-start | bytes 2752512 | tf_op jit(solution)/shard_map/all_gather | solution.py:77
  29.6 131.1 %all-gather.9.cloned.1.call-start = ((), (), s32[]{:S(2)}) async-start(), calls=%async_computation.5 | async-start | bytes 2752512 | tf_op jit(solution)/shard_map/all_gather | solution.py:76
  170.2 10.7 %copy-start.2 = (f32[1,2,8,2]{2,3,1,0:T(2,128)S(1)}, f32[1,2,8,2]{2,3,1,0:T(2,128)}, u32[]{:S(2)}) copy-start(f32[1,2,8,2]{2,3,1,0:T(2,128)} %param.15) | copy-start | bytes 388
  170.2 93.8 %all-to-all-start.1 = ((bf16[32,5,7168]{2,1,0:T(8,128)(2,1)}), bf16[32,5,7168]{2,1,0:T(8,128)(2,1)}, u32[]{:S(2)}, u32[]{:S(2)}) async-start(bf16[32,5,7168]{2,1,0:T(8,128)(2,1)} %reshape.116), calls=%async_computation.1 | async-start | bytes 7340032 | tf_op jit(solution)/shard_map/all_to_all | solution.py:24
  266.9 1.7 copy-start
  267.0 8.7 %copy-start.1 = (f32[1,7168]{1,0:T(1,128)S(1)}, f32[1,7168]{1,0:T(1,128)}, u32[]{:S(2)}) copy-start(f32[1,7168]{1,0:T(1,128)} %param.10) | copy-start | bytes 86020
  268.7 6.7 %collective-permute-start = (bf16[8,7168]{1,0:T(8,128)(2,1)S(1)}, bf16[8,7168]{1,0:T(8,128)(2,1)S(1)}, u32[]{:S(2)}, u32[]{:S(2)}) collective-permute-start(bf16[8,7168]{1,0:T(8,128)(2,1)S(1)} %fusion.37), channel_id=1, source_target_pairs={{0,64},{64,128},{128,192},{192,256},{256,320},{320,384},{384,448},... | collective-permute-start | bytes 344072 | tf_op jit(solution)/shard_map/ppermute | solution.py:11
  384.3 88.9 %all-to-all-start.3 = ((bf16[32,5,7168]{2,1,0:T(8,128)(2,1)}), bf16[32,5,7168]{2,1,0:T(8,128)(2,1)}, u32[]{:S(2)}, u32[]{:S(2)}) async-start(bf16[32,5,7168]{2,1,0:T(8,128)(2,1)} %reshape.122), calls=%async_computation.3 | async-start | bytes 7340032 | tf_op jit(solution)/shard_map/all_to_all | solution.py:24
Sparse Core Ops, SparseCore 0:
  9.4 64.4 all-gather.6
  76.0 42.6 all-gather.10
  120.8 39.8 all-gather.8
where the time goes:
time: 487 us; the launch traced here: 485 us
  waiting for transfers between devices  296 us (61%)
  blocking collectives  92.8 us (19%)
  starting transfers between devices  34.2 us (7%)
  local copies, waits for them, and re-layouts  22.2 us (5%)
  matrix products  16 us (3%)
  between operations  13.4 us (3%)
  other arithmetic  9.93 us (2%)
    all_to_all x2, waiting for transfers between devices, expert_rows(): lax.all_to_all(output, 'expert', split_axis=0, concat_axis=0, tiled=True)  166 us
    all_to_all x1, blocking collectives, moe_layer(): lax.all_to_all(outgoing, 'expert', split_axis=0, concat_axis=0, tiled=True)  92.8 us
    all_to_all x1, waiting for transfers between devices, moe_layer(): lax.all_to_all(outgoing, 'expert', split_axis=0, concat_axis=0, tiled=True)  81.6 us
    all_gather x1, waiting for transfers between devices, on_device(): lax.all_gather(w_up[0], 'dp', axis=0, tiled=True)  42 us
    all_to_all x2, starting transfers between devices, expert_rows(): lax.all_to_all(output, 'expert', split_axis=0, concat_axis=0, tiled=True)  16.5 us
    all_to_all x1, starting transfers between devices, moe_layer(): lax.all_to_all(outgoing, 'expert', split_axis=0, concat_axis=0, tiled=True)  14.5 us
    dot_general x2, matrix products, expert_rows(): lax.dot_general(hidden, down_full, (((1,), (1,)), ((), ())), preferred_el...  9.76 us
  transfers between devices with their start and end apart: 7, of which 6 were waited for; matrix products, arithmetic and copies ran while one was open for 3% of the time, Pallas kernels for 0%

commit v1 on v0

v1 whole, which is shorter than its diff:
```python
from functools import partial

import jax
import jax.numpy as jnp
import numpy as np
from jax import lax
from jax.sharding import Mesh
from jax.sharding import PartitionSpec as P

ALL = ("eg", "q", "dp")


def passed_along(array, axis, by):
    length = lax.axis_size(axis)
    return lax.ppermute(array, axis, [(i, (i + by) % length) for i in range(length)])


def route(stream, gain_row, routes, experts, capacity):
    tok_rows, model_width = stream.shape
    fan_out = routes.shape[1]
    widened = stream.astype(jnp.float32)
    inv_rms = lax.rsqrt(jnp.mean(widened * widened, axis=1, keepdims=True) + 1e-06)
    normed = (widened * inv_rms * gain_row[None, :]).astype(jnp.bfloat16)
    flat_ids = routes.reshape(-1)
    count_all = flat_ids.shape[0]
    chosen = (flat_ids[:, None] == jnp.arange(experts, dtype=jnp.int32)[None, :]).astype(
        jnp.float32
    )
    triangle = (jnp.arange(count_all)[:, None] >= jnp.arange(count_all)[None, :]).astype(
        jnp.float32
    )
    running = jnp.dot(triangle, chosen, preferred_element_type=jnp.float32)
    slot_of = jnp.sum(chosen * (running - 1.0), axis=1).astype(jnp.int32)
    target = flat_ids * capacity + slot_of
    placing = jnp.arange(experts * capacity, dtype=jnp.int32)[:, None] == target[None, :]
    placing = (
        placing.reshape(experts * capacity, tok_rows, fan_out).any(axis=2).astype(jnp.bfloat16)
    )
    outgoing = jnp.dot(placing, normed, preferred_element_type=jnp.float32).astype(jnp.bfloat16)
    return widened, outgoing.reshape(experts, capacity, model_width), target


def moe_layer(stream, gain_row, gate_w, up_w, down_mine, routes, mixing):
    experts = lax.axis_size("eg")
    blocks = lax.axis_size("q")
    halves = lax.axis_size("dp")
    tok_rows, model_width = stream.shape
    fan_out = routes.shape[1]
    capacity = min(tok_rows, max(2, 5 * tok_rows * fan_out // (4 * experts)))
    half = model_width // halves
    widened, outgoing, target = route(stream, gain_row, routes, experts, capacity)
    send = outgoing.reshape(experts, 1, capacity, halves, half).transpose(0, 1, 3, 2, 4)
    send = jnp.broadcast_to(send, (experts, blocks, halves, capacity, half))
    send = send.reshape(experts * blocks * halves, capacity, half)
    arrived = lax.all_to_all(send, ALL, split_axis=0, concat_axis=0, tiled=True)
    sources = arrived.shape[0]
    rows = arrived.reshape(sources * capacity, half)
    gate_part = jnp.dot(rows, gate_w, preferred_element_type=jnp.float32)
    up_part = jnp.dot(rows, up_w, preferred_element_type=jnp.float32)
    both = lax.psum(jnp.stack([gate_part, up_part]), "dp")
    hidden = (jax.nn.silu(both[0]) * both[1]).astype(jnp.bfloat16)
    hidden_all = lax.all_gather(hidden, "q", axis=1, tiled=True)
    out = lax.dot_general(
        hidden_all, down_mine, (((1,), (1,)), ((), ())), preferred_element_type=jnp.float32
    ).astype(jnp.bfloat16)
    piece = out.shape[1]
    back = lax.all_to_all(
        out.reshape(sources, capacity, piece), ALL, split_axis=0, concat_axis=0, tiled=True
    )
    back = back.reshape(experts, blocks, halves, capacity, piece).transpose(0, 3, 2, 1, 4)
    expert_out = back.reshape(experts * capacity, model_width)
    picked = jnp.take(expert_out, target, axis=0)
    picked = picked.reshape(tok_rows, fan_out, model_width)
    mixed_sum = jnp.sum(mixing[:, :, None] * picked.astype(jnp.float32), axis=1)
    return (widened + mixed_sum).astype(jnp.bfloat16)


def on_device(blocks, gains, w_gate, w_up, w_down, expert_ids, combine):
    stream = blocks[0]
    turns = expert_ids.shape[1]
    n_blocks = lax.axis_size("q")
    down_local = w_down[0]
    half, width = down_local.shape
    piece = half // n_blocks
    down_mine = lax.all_to_all(
        down_local.reshape(n_blocks, piece, width), "q", split_axis=0, concat_axis=0, tiled=True
    )
    down_mine = down_mine.transpose(1, 0, 2).reshape(piece, n_blocks * width)
    for layer_turn in range(turns):
        if layer_turn > 0:
            stream = passed_along(stream, "section", 1)
        stream = moe_layer(
            stream,
            gains[0],
            w_gate[0],
            w_up[0],
            down_mine,
            expert_ids[0, layer_turn],
            combine[0, layer_turn],
        )
    return stream[None]


def solution(mesh):
    n_section, n_expert, n_dp = (mesh.shape[a] for a in ("section", "expert", "dp"))
    n_q = n_expert // 4
    inner = Mesh(
        np.asarray(mesh.devices).reshape(n_section, n_expert // n_q, n_q, n_dp),
        ("section", "eg", "q", "dp"),
    )
    tok = ("eg", "q", "dp")
    in_specs = (
        P("section", tok, None),
        P("section", None),
        P("section", "dp", ("eg", "q")),
        P("section", "dp", ("eg", "q")),
        P("section", "dp", ("eg", "q")),
        P("section", None, tok, None),
        P("section", None, tok, None),
    )
    out_specs = P("section", tok, None)
    return jax.shard_map(
        on_device, mesh=inner, in_specs=in_specs, out_specs=out_specs, check_vma=False
    )
```

time: 487 us -> 415 us (0.85)
  waiting for transfers between devices: 296 us -> 119 us
  blocking collectives: 92.8 us -> 222 us
  matrix products: 16 us -> 8.22 us
  local copies, waits for them, and re-layouts: 22.2 us -> 15 us
  starting transfers between devices: 34.2 us -> 28.4 us
    all_to_all x3, waiting for transfers between devices: 248 us -> 36 us  [the longest x2 36 us: moe_layer(): lax.all_to_all(out.reshape(sources, capacity, piece), ALL, split_axis=0,...]
    all_to_all x1 -> x2, blocking collectives: 92.8 us -> 188 us  [moe_layer(): arrived = lax.all_to_all(send, ALL, split_axis=0, concat_axis=0, tiled=True)]
    psum x0 -> x2, waiting for transfers between devices: none -> 78.5 us  [moe_layer(): both = lax.psum(jnp.stack([gate_part, up_part]), 'dp')]
    all_gather x3 -> x0, waiting for transfers between devices: 43.3 us -> none  [the longest x1 42 us: on_device(): lax.all_gather(w_up[0], 'dp', axis=0, tiled=True)]
    all_gather x0 -> x2, blocking collectives: none -> 34.2 us  [moe_layer(): hidden_all = lax.all_gather(hidden, 'q', axis=1, tiled=True)]
    dot_general x8 -> x10, matrix products: 16 us -> 8.22 us  [the longest x2 3.42 us: moe_layer(): lax.dot_general(hidden_all, down_mine, (((1,), (1,)), ((), ())), preferre...]
    reshape x8, local copies, waits for them, and re-layouts: 16.1 us -> 9.48 us  [the longest x2 6.39 us: moe_layer(): rows = arrived.reshape(sources * capacity, half)]
    all_to_all x3, starting transfers between devices: 31 us -> 25.3 us  [the longest x2 19 us: moe_layer(): lax.all_to_all(out.reshape(sources, capacity, piece), ALL, split_axis=0,...]
  transfers between devices with their start and end apart: 7 -> 6, of which waited for: 6 -> 5; matrix products, arithmetic and copies ran while one was open for 3% -> 2% of each run, Pallas kernels for 0% -> 0%
where the time goes in v1:
time: 415 us; the launch traced here: 414 us
  blocking collectives  222 us (53%)
  waiting for transfers between devices  119 us (29%)
  starting transfers between devices  28.4 us (7%)
  local copies, waits for them, and re-layouts  15 us (4%)
  between operations  13.7 us (3%)
  matrix products  8.22 us (2%)
  other arithmetic  7.95 us (2%)
    all_to_all x2, blocking collectives, moe_layer(): arrived = lax.all_to_all(send, ALL, split_axis=0, concat_axis=0, tiled=True)  188 us
    psum x2, waiting for transfers between devices, moe_layer(): both = lax.psum(jnp.stack([gate_part, up_part]), 'dp')  78.5 us
    all_to_all x2, waiting for transfers between devices, moe_layer(): lax.all_to_all(out.reshape(sources, capacity, piece), ALL, split_axis=0,...  36 us
    all_gather x2, blocking collectives, moe_layer(): hidden_all = lax.all_gather(hidden, 'q', axis=1, tiled=True)  34.2 us
    all_to_all x2, starting transfers between devices, moe_layer(): lax.all_to_all(out.reshape(sources, capacity, piece), ALL, split_axis=0,...  19 us
  transfers between devices with their start and end apart: 6, of which 5 were waited for; matrix products, arithmetic and copies ran while one was open for 2% of the time, Pallas kernels for 0%

profile of v1, /device:TPU:1, one launch (start us, length us, event | category | flops | bytes accessed | tf_op | source)
XLA Modules:
  0.0 413.9 jit_solution(5506339195129914146)
XLA Ops:
  6.5 0.8 fusion.36
  8.3 0.7 bitcast_add_fusion.1
  9.1 1.1 fusion.16
  10.2 1.2 convolution_convert_fusion.1
  11.6 0.4 broadcast_in_dim.20
  12.0 98.3 %all_to_all.25 = bf16[64,5,3584]{2,1,0:T(8,128)(2,1)} all-to-all(bf16[64,5,3584]{2,1,0:T(8,128)(2,1)S(1)} %bitcast.103), channel_id=1, replica_groups=mesh['section'=8,'eg'=4,'q'=8,'dp'=2] {'eg','q','dp'}, dimensions={0} | all-to-all | bytes 4587520 | tf_op jit(solution)/shard_map/all_to_all | solution.py:55
  110.3 6.3 %all-to-all-start.1 = ((bf16[8,448,128]{2,1,0:T(8,128)(2,1)}), bf16[8,448,128]{2,1,0:T(8,128)(2,1)}, u32[]{:S(2)}, u32[]{:S(2)}) async-start(bf16[8,448,128]{2,1,0:T(8,128)(2,1)} %bitcast.14), calls=%async_computation.1 | async-start | bytes 1835008 | tf_op jit(solution)/shard_map/all_to_all | solution.py:85
  116.6 3.2 reshape.111
  119.8 0.8 convolution_bitcast_fusion.2
  120.5 0.4 copy-done.1
  120.9 0.8 convolution_bitcast_fusion.3
  121.7 0.7 pad_maximum_fusion
  122.5 39.6 %all-reduce.3.cloned.1.call-done = f32[2,320,128]{2,1,0:T(8,128)} async-done(((f32[2,320,128]{2,1,0:T(8,128)}), f32[2,320,128]{2,1,0:T(8,128)}) %all-reduce.3.cloned.1.call-update) | async-done | bytes 327696 | tf_op jit(solution)/shard_map/psum | solution.py:60
  162.1 1.1 fusion.23
  163.2 17.1 %all_gather.6 = bf16[320,1024]{1,0:T(8,128)(2,1)S(1)} all-gather(bf16[320,128]{1,0:T(8,128)(2,1)S(1)} %fusion.23), channel_id=1, replica_groups=mesh['section'=8,'eg'=4,'q'=8,'dp'=2] {'q'}, dimensions={1}, use_global_device_ids=true | all-gather | bytes 737280 | tf_op jit(solution)/shard_map/all_gather | solution.py:62
  180.3 1.7 convolution_convert_fusion.3
  182.0 1.0 reshape.113
  182.9 9.5 %all-to-all-start.2 = ((bf16[64,5,448]{2,1,0:T(8,128)(2,1)}), bf16[64,5,448]{2,1,0:T(8,128)(2,1)S(1)}, u32[]{:S(2)}, u32[]{:S(2)}) async-start(bf16[64,5,448]{2,1,0:T(8,128)(2,1)} %reshape.113), calls=%async_computation.2 | async-start | bytes 1048576 | tf_op jit(solution)/shard_map/all_to_all | solution.py:67
  192.6 18.0 %all-to-all-done.2 = bf16[64,5,448]{2,1,0:T(8,128)(2,1)S(1)} async-done(((bf16[64,5,448]{2,1,0:T(8,128)(2,1)}), bf16[64,5,448]{2,1,0:T(8,128)(2,1)S(1)}, u32[]{:S(2)}, u32[]{:S(2)}) %all-to-all-start.2) | async-done | bytes 286752 | tf_op jit(solution)/shard_map/all_to_all | solution.py:67
  210.6 0.2 copy.69
  210.8 0.4 reshape.115
  211.2 0.7 gather_fusion
  212.0 0.3 reshape.122
  212.3 0.6 multiply_reduce_fusion.1
  213.0 3.1 collective-permute-start
  216.2 4.2 %collective-permute-done = bf16[8,7168]{1,0:T(8,128)(2,1)S(1)} collective-permute-done((bf16[8,7168]{1,0:T(8,128)(2,1)S(1)}, bf16[8,7168]{1,0:T(8,128)(2,1)S(1)}, u32[]{:S(2)}, u32[]{:S(2)}) %collective-permute-start) | collective-permute-done | bytes 114720 | tf_op jit(solution)/shard_map/ppermute | solution.py:15
  220.4 0.2 fusion.12
  220.6 0.3 convolution_convert_fusion
  221.1 0.4 broadcast_in_dim.22
  221.6 89.4 %all_to_all.26 = bf16[64,5,3584]{2,1,0:T(8,128)(2,1)} all-to-all(bf16[64,5,3584]{2,1,0:T(8,128)(2,1)S(1)} %bitcast.104), channel_id=1, replica_groups=mesh['section'=8,'eg'=4,'q'=8,'dp'=2] {'eg','q','dp'}, dimensions={0} | all-to-all | bytes 4587520 | tf_op jit(solution)/shard_map/all_to_all | solution.py:55
  310.9 3.2 reshape.117
  314.1 0.8 convolution_bitcast_fusion
  314.9 0.4 copy-done.2
  315.3 0.8 convolution_bitcast_fusion.1
  316.1 0.7 pad_maximum_fusion.1
  316.8 38.8 %all-reduce.5.cloned.1.call-done = f32[2,320,128]{2,1,0:T(8,128)} async-done(((f32[2,320,128]{2,1,0:T(8,128)}), f32[2,320,128]{2,1,0:T(8,128)}) %all-reduce.5.cloned.1.call-update) | async-done | bytes 327696 | tf_op jit(solution)/shard_map/psum | solution.py:60
  355.6 1.1 fusion.21
  356.7 17.1 %all_gather.7 = bf16[320,1024]{1,0:T(8,128)(2,1)S(1)} all-gather(bf16[320,128]{1,0:T(8,128)(2,1)S(1)} %fusion.21), channel_id=1, replica_groups=mesh['section'=8,'eg'=4,'q'=8,'dp'=2] {'q'}, dimensions={1}, use_global_device_ids=true | all-gather | bytes 737280 | tf_op jit(solution)/shard_map/all_gather | solution.py:62
  373.8 1.7 convolution_convert_fusion.2
  375.5 1.0 reshape.118
  376.5 9.5 %all-to-all-start.4 = ((bf16[64,5,448]{2,1,0:T(8,128)(2,1)}), bf16[64,5,448]{2,1,0:T(8,128)(2,1)S(1)}, u32[]{:S(2)}, u32[]{:S(2)}) async-start(bf16[64,5,448]{2,1,0:T(8,128)(2,1)} %reshape.118), calls=%async_computation.4 | async-start | bytes 1048576 | tf_op jit(solution)/shard_map/all_to_all | solution.py:67
  386.1 18.0 %all-to-all-done.4 = bf16[64,5,448]{2,1,0:T(8,128)(2,1)S(1)} async-done(((bf16[64,5,448]{2,1,0:T(8,128)(2,1)}), bf16[64,5,448]{2,1,0:T(8,128)(2,1)S(1)}, u32[]{:S(2)}, u32[]{:S(2)}) %all-to-all-start.4) | async-done | bytes 286752 | tf_op jit(solution)/shard_map/all_to_all | solution.py:67
  404.1 0.2 copy.68
  404.3 0.4 reshape.120
  404.7 0.7 gather_fusion.1
  405.5 0.3 reshape.123
  405.8 0.6 multiply_reduce_fusion
  406.4 0.7 fusion.25
  (45 shorter events, 2.0 us)
Async XLA Ops:
  6.5 113.2 %copy-start = (bf16[1,3584,128]{2,1,0:T(8,128)(2,1)S(1)}, bf16[1,3584,128]{2,1,0:T(8,128)(2,1)}, u32[]{:S(2)}) copy-start(bf16[1,3584,128]{2,1,0:T(8,128)(2,1)} %param.12) | copy-start | bytes 2752516
  110.3 70.0 %all-to-all-start.1 = ((bf16[8,448,128]{2,1,0:T(8,128)(2,1)}), bf16[8,448,128]{2,1,0:T(8,128)(2,1)}, u32[]{:S(2)}, u32[]{:S(2)}) async-start(bf16[8,448,128]{2,1,0:T(8,128)(2,1)} %bitcast.14), calls=%async_computation.1 | async-start | bytes 1835008 | tf_op jit(solution)/shard_map/all_to_all | solution.py:85
  116.5 45.6 %all-reduce.3.cloned.1.call-start = ((), (), s32[]{:S(2)}) async-start(), calls=%async_computation.5 | async-start | bytes 655360 | tf_op jit(solution)/shard_map/psum | solution.py:60
  119.8 1.2 copy-start.1
  180.3 12.2 %copy-start.5 = (f32[1,2,8,2]{2,3,1,0:T(2,128)S(1)}, f32[1,2,8,2]{2,3,1,0:T(2,128)}, u32[]{:S(2)}) copy-start(f32[1,2,8,2]{2,3,1,0:T(2,128)} %param.15) | copy-start | bytes 388
  182.9 27.7 %all-to-all-start.2 = ((bf16[64,5,448]{2,1,0:T(8,128)(2,1)}), bf16[64,5,448]{2,1,0:T(8,128)(2,1)S(1)}, u32[]{:S(2)}, u32[]{:S(2)}) async-start(bf16[64,5,448]{2,1,0:T(8,128)(2,1)} %reshape.113), calls=%async_computation.2 | async-start | bytes 1048576 | tf_op jit(solution)/shard_map/all_to_all | solution.py:67
  192.5 163.2 %all-reduce.5.cloned.1.call-start = ((), (), s32[]{:S(2)}) async-start(), calls=%async_computation.6 | async-start | bytes 655360 | tf_op jit(solution)/shard_map/psum | solution.py:60
  211.2 1.7 copy-start.3
  211.2 9.4 %copy-start.4 = (f32[1,7168]{1,0:T(1,128)S(1)}, f32[1,7168]{1,0:T(1,128)}, u32[]{:S(2)}) copy-start(f32[1,7168]{1,0:T(1,128)} %param.10) | copy-start | bytes 86020
  213.0 7.4 %collective-permute-start = (bf16[8,7168]{1,0:T(8,128)(2,1)S(1)}, bf16[8,7168]{1,0:T(8,128)(2,1)S(1)}, u32[]{:S(2)}, u32[]{:S(2)}) collective-permute-start(bf16[8,7168]{1,0:T(8,128)(2,1)S(1)} %fusion.19), channel_id=1, source_target_pairs={{0,64},{64,128},{128,192},{192,256},{256,320},{320,384},{384,448},... | collective-permute-start | bytes 344072 | tf_op jit(solution)/shard_map/ppermute | solution.py:15
  314.1 1.2 copy-start.2
  376.5 27.7 %all-to-all-start.4 = ((bf16[64,5,448]{2,1,0:T(8,128)(2,1)}), bf16[64,5,448]{2,1,0:T(8,128)(2,1)S(1)}, u32[]{:S(2)}, u32[]{:S(2)}) async-start(bf16[64,5,448]{2,1,0:T(8,128)(2,1)} %reshape.118), calls=%async_computation.4 | async-start | bytes 1048576 | tf_op jit(solution)/shard_map/all_to_all | solution.py:67
Sparse Core Ops, SparseCore 0:
  122.6 39.4 all-reduce.2
  316.9 38.6 all-reduce.4

commit v2 on v1

--- a/solution.py
+++ b/solution.py
@@ -49,21 +49,23 @@
     capacity = min(tok_rows, max(2, 5 * tok_rows * fan_out // (4 * experts)))
     half = model_width // halves
     widened, outgoing, target = route(stream, gain_row, routes, experts, capacity)
-    send = outgoing.reshape(experts, 1, capacity, halves, half).transpose(0, 1, 3, 2, 4)
-    send = jnp.broadcast_to(send, (experts, blocks, halves, capacity, half))
-    send = send.reshape(experts * blocks * halves, capacity, half)
-    arrived = lax.all_to_all(send, ALL, split_axis=0, concat_axis=0, tiled=True)
-    sources = arrived.shape[0]
+    send = outgoing.reshape(experts, capacity, halves, half).transpose(0, 2, 1, 3)
+    send = send.reshape(experts * halves, capacity, half)
+    arrived = lax.all_to_all(send, ("eg", "dp"), split_axis=0, concat_axis=0, tiled=True)
+    arrived = lax.all_gather(arrived, "q", axis=0, tiled=False)
+    sources = blocks * experts * halves
     rows = arrived.reshape(sources * capacity, half)
     gate_part = jnp.dot(rows, gate_w, preferred_element_type=jnp.float32)
     up_part = jnp.dot(rows, up_w, preferred_element_type=jnp.float32)
-    both = lax.psum(jnp.stack([gate_part, up_part]), "dp")
+    mine = jnp.stack([gate_part, up_part])
+    both = mine + passed_along(mine, "dp", 1)
     hidden = (jax.nn.silu(both[0]) * both[1]).astype(jnp.bfloat16)
     hidden_all = lax.all_gather(hidden, "q", axis=1, tiled=True)
     out = lax.dot_general(
         hidden_all, down_mine, (((1,), (1,)), ((), ())), preferred_element_type=jnp.float32
     ).astype(jnp.bfloat16)
     piece = out.shape[1]
+    out = out.reshape(blocks, experts, halves, capacity, piece).transpose(1, 0, 2, 3, 4)
     back = lax.all_to_all(
         out.reshape(sources, capacity, piece), ALL, split_axis=0, concat_axis=0, tiled=True
     )

time: 415 us -> 274 us (0.66)
  blocking collectives: 222 us -> 72.4 us
  local copies, waits for them, and re-layouts: 15 us -> 25.6 us
    all_to_all x2, blocking collectives: 188 us -> 36.7 us  [moe_layer(): lax.all_to_all(send, ('eg', 'dp'), split_axis=0, concat_axis=0, tiled=True)]
    psum x2 -> x0, waiting for transfers between devices: 78.5 us -> none  [moe_layer(): both = lax.psum(jnp.stack([gate_part, up_part]), 'dp')]
    all_gather x0 -> x2, waiting for transfers between devices: none -> 60.3 us  [moe_layer(): arrived = lax.all_gather(arrived, 'q', axis=0, tiled=False)]
    ppermute x1 -> x3, waiting for transfers between devices: 4.24 us -> 21.6 us  [passed_along(): lax.ppermute(array, axis, [(i, (i + by) % length) for i in range(length)])]
    all_gather x0 -> x2, local copies, waits for them, and re-layouts: none -> 9.47 us  [moe_layer(): arrived = lax.all_gather(arrived, 'q', axis=0, tiled=False)]
    all_to_all x2, starting transfers between devices: 19 us -> 13.9 us  [moe_layer(): lax.all_to_all(out.reshape(sources, capacity, piece), ALL, split_axis=0,...]
    ppermute x1 -> x3, starting transfers between devices: 3.11 us -> 7.46 us  [passed_along(): lax.ppermute(array, axis, [(i, (i + by) % length) for i in range(length)])]
  transfers between devices with their start and end apart: 6 -> 8, of which waited for: 5 -> 7; matrix products, arithmetic and copies ran while one was open for 2% -> 4% of each run, Pallas kernels for 0% -> 0%
where the time goes in v2:
time: 274 us
  waiting for transfers between devices  118 us (43%)
  blocking collectives  72.4 us (26%)
  starting transfers between devices  30.9 us (11%)
  local copies, waits for them, and re-layouts  25.6 us (9%)
  between operations  13.8 us (5%)
  matrix products  8.23 us (3%)
  other arithmetic  4.62 us (2%)
    all_gather x2, waiting for transfers between devices, moe_layer(): arrived = lax.all_gather(arrived, 'q', axis=0, tiled=False)  60.3 us
    all_to_all x2, blocking collectives, moe_layer(): lax.all_to_all(send, ('eg', 'dp'), split_axis=0, concat_axis=0, tiled=True)  36.7 us
    all_to_all x2, waiting for transfers between devices, moe_layer(): lax.all_to_all(out.reshape(sources, capacity, piece), ALL, split_axis=0,...  36 us
    all_gather x2, blocking collectives, moe_layer(): hidden_all = lax.all_gather(hidden, 'q', axis=1, tiled=True)  35.7 us
    ppermute x3, waiting for transfers between devices, passed_along(): lax.ppermute(array, axis, [(i, (i + by) % length) for i in range(length)])  21.6 us
    all_to_all x2, starting transfers between devices, moe_layer(): lax.all_to_all(out.reshape(sources, capacity, piece), ALL, split_axis=0,...  13.9 us
    all_to_all x1, starting transfers between devices, on_device(): lax.all_to_all(down_local.reshape(n_blocks, piece, width), 'q', split_axi...  9.54 us
    all_gather x2, local copies, waits for them, and re-layouts, moe_layer(): arrived = lax.all_gather(arrived, 'q', axis=0, tiled=False)  9.47 us
  transfers between devices with their start and end apart: 8, of which 7 were waited for; matrix products, arithmetic and copies ran while one was open for 4% of the time, Pallas kernels for 0%

profile of v2, /device:TPU:1, one launch (start us, length us, event | category | flops | bytes accessed | tf_op | source)
XLA Modules:
  0.0 273.6 jit_solution(9965028550849177385)
XLA Ops:
  6.5 0.8 fusion.38
  8.3 0.7 bitcast_add_fusion.1
  9.1 1.1 fusion.16
  10.2 1.2 convolution_convert_fusion.1
  11.6 23.1 %all_to_all.25 = bf16[8,5,3584]{2,1,0:T(8,128)(2,1)S(1)} all-to-all(bf16[8,5,3584]{2,1,0:T(8,128)(2,1)S(1)} %bitcast.109), channel_id=1, replica_groups=mesh['section'=8,'eg'=4,'q'=8,'dp'=2] {'eg','dp'}, dimensions={0} | all-to-all | bytes 573440 | tf_op jit(solution)/shard_map/all_to_all | solution.py:54
  34.7 0.8 copy.84
  35.5 9.5 %all-to-all-start.1 = ((bf16[8,448,128]{2,1,0:T(8,128)(2,1)}), bf16[8,448,128]{2,1,0:T(8,128)(2,1)}, u32[]{:S(2)}, u32[]{:S(2)}) async-start(bf16[8,448,128]{2,1,0:T(8,128)(2,1)} %bitcast.13), calls=%async_computation.1 | async-start | bytes 1835008 | tf_op jit(solution)/shard_map/all_to_all | solution.py:87
  45.0 26.5 %all-gather.5.cloned.1.call-done = bf16[64,5,3584]{2,0,1:T(8,128)(2,1)} async-done(((bf16[8,5,3584]{2,0,1:T(8,128)(2,1)}), bf16[64,5,3584]{2,0,1:T(8,128)(2,1)}) %all-gather.5.cloned.1.call-update) | async-done | bytes 2293776 | tf_op jit(solution)/shard_map/all_gather | solution.py:55
  71.5 4.7 %copy.85 = bf16[64,5,3584]{2,1,0:T(8,128)(2,1)} copy(bf16[64,5,3584]{2,0,1:T(8,128)(2,1)} %all-gather.5.cloned.1.call-done) | data formatting | bytes 4587520 | tf_op jit(solution)/shard_map/all_gather | solution.py:55
  76.2 3.2 %reshape.117 = bf16[320,3584]{1,0:T(8,128)(2,1)S(1)} reshape(bf16[64,5,3584]{2,1,0:T(8,128)(2,1)} %copy.85) | data formatting | bytes 4587520 | tf_op jit(solution)/shard_map/reshape | solution.py:57
  79.5 0.8 convolution_bitcast_fusion.2
  80.2 0.4 copy-done.1
  80.6 0.8 convolution_bitcast_fusion.3
  81.4 2.1 collective-permute-start
  83.6 8.7 %collective-permute-done = f32[2,320,128]{2,1,0:T(8,128)S(1)} collective-permute-done((f32[2,320,128]{2,1,0:T(8,128)S(1)}, f32[2,320,128]{2,1,0:T(8,128)S(1)}, u32[]{:S(2)}, u32[]{:S(2)}) %collective-permute-start) | collective-permute-done | bytes 327712 | tf_op jit(solution)/shard_map/ppermute | solution.py:15
  92.4 17.8 %all_gather.20 = bf16[320,1024]{1,0:T(8,128)(2,1)S(1)} all-gather(bf16[320,128]{1,0:T(8,128)(2,1)S(1)} %fusion.23), channel_id=1, replica_groups=mesh['section'=8,'eg'=4,'q'=8,'dp'=2] {'q'}, dimensions={1}, use_global_device_ids=true | all-gather | bytes 737280 | tf_op jit(solution)/shard_map/all_gather | solution.py:63
  110.2 1.7 convolution_convert_fusion.3
  112.1 0.8 copy.103
  112.9 6.1 %all-to-all-start.2 = ((bf16[64,5,448]{2,1,0:T(8,128)(2,1)}), bf16[64,5,448]{2,1,0:T(8,128)(2,1)S(1)}, u32[]{:S(2)}, u32[]{:S(2)}) async-start(bf16[64,5,448]{2,1,0:T(8,128)(2,1)} %bitcast.16), calls=%async_computation.2 | async-start | bytes 1048576 | tf_op jit(solution)/shard_map/all_to_all | solution.py:69
  119.2 18.0 %all-to-all-done.2 = bf16[64,5,448]{2,1,0:T(8,128)(2,1)S(1)} async-done(((bf16[64,5,448]{2,1,0:T(8,128)(2,1)}), bf16[64,5,448]{2,1,0:T(8,128)(2,1)S(1)}, u32[]{:S(2)}, u32[]{:S(2)}) %all-to-all-start.2) | async-done | bytes 286752 | tf_op jit(solution)/shard_map/all_to_all | solution.py:69
  137.2 0.3 copy.124
  137.5 0.4 reshape.122
  137.9 0.7 gather_fusion
  138.7 0.3 reshape.130
  139.0 0.6 multiply_reduce_fusion.1
  139.7 3.1 %collective-permute-start.1 = (bf16[8,7168]{1,0:T(8,128)(2,1)S(1)}, bf16[8,7168]{1,0:T(8,128)(2,1)S(1)}, u32[]{:S(2)}, u32[]{:S(2)}) collective-permute-start(bf16[8,7168]{1,0:T(8,128)(2,1)S(1)} %fusion.19), channel_id=1, source_target_pairs={{0,64},{64,128},{128,192},{192,256},{256,320},{320,384},{384,448},... | collective-permute-start | bytes 344072 | tf_op jit(solution)/shard_map/ppermute | solution.py:15
  142.9 4.2 %collective-permute-done.1 = bf16[8,7168]{1,0:T(8,128)(2,1)S(1)} collective-permute-done((bf16[8,7168]{1,0:T(8,128)(2,1)S(1)}, bf16[8,7168]{1,0:T(8,128)(2,1)S(1)}, u32[]{:S(2)}, u32[]{:S(2)}) %collective-permute-start.1) | collective-permute-done | bytes 114720 | tf_op jit(solution)/shard_map/ppermute | solution.py:15
  147.3 0.3 convolution_convert_fusion
  147.8 13.6 %all_to_all.26 = bf16[8,5,3584]{2,1,0:T(8,128)(2,1)S(1)} all-to-all(bf16[8,5,3584]{2,1,0:T(8,128)(2,1)S(1)} %bitcast.110), channel_id=1, replica_groups=mesh['section'=8,'eg'=4,'q'=8,'dp'=2] {'eg','dp'}, dimensions={0} | all-to-all | bytes 573440 | tf_op jit(solution)/shard_map/all_to_all | solution.py:54
  161.5 0.8 copy.96
  162.3 33.8 %all-gather.7.cloned.1.call-done = bf16[64,5,3584]{2,0,1:T(8,128)(2,1)} async-done(((bf16[8,5,3584]{2,0,1:T(8,128)(2,1)}), bf16[64,5,3584]{2,0,1:T(8,128)(2,1)}) %all-gather.7.cloned.1.call-update) | async-done | bytes 2293776 | tf_op jit(solution)/shard_map/all_gather | solution.py:55
  196.1 4.7 %copy.97 = bf16[64,5,3584]{2,1,0:T(8,128)(2,1)} copy(bf16[64,5,3584]{2,0,1:T(8,128)(2,1)} %all-gather.7.cloned.1.call-done) | data formatting | bytes 4587520 | tf_op jit(solution)/shard_map/all_gather | solution.py:55
  200.9 3.2 %reshape.124 = bf16[320,3584]{1,0:T(8,128)(2,1)S(1)} reshape(bf16[64,5,3584]{2,1,0:T(8,128)(2,1)} %copy.97) | data formatting | bytes 4587520 | tf_op jit(solution)/shard_map/reshape | solution.py:57
  204.1 0.8 convolution_bitcast_fusion
  204.8 0.4 copy-done.2
  205.2 0.8 convolution_bitcast_fusion.1
  206.0 2.2 collective-permute-start.2
  208.2 8.7 %collective-permute-done.2 = f32[2,320,128]{2,1,0:T(8,128)S(1)} collective-permute-done((f32[2,320,128]{2,1,0:T(8,128)S(1)}, f32[2,320,128]{2,1,0:T(8,128)S(1)}, u32[]{:S(2)}, u32[]{:S(2)}) %collective-permute-start.2) | collective-permute-done | bytes 327712 | tf_op jit(solution)/shard_map/ppermute | solution.py:15
  217.0 17.9 %all_gather.23 = bf16[320,1024]{1,0:T(8,128)(2,1)S(1)} all-gather(bf16[320,128]{1,0:T(8,128)(2,1)S(1)} %fusion.21), channel_id=1, replica_groups=mesh['section'=8,'eg'=4,'q'=8,'dp'=2] {'q'}, dimensions={1}, use_global_device_ids=true | all-gather | bytes 737280 | tf_op jit(solution)/shard_map/all_gather | solution.py:63
  234.9 1.7 convolution_convert_fusion.2
  236.8 0.8 copy.106
  237.6 7.8 %all-to-all-start.4 = ((bf16[64,5,448]{2,1,0:T(8,128)(2,1)}), bf16[64,5,448]{2,1,0:T(8,128)(2,1)S(1)}, u32[]{:S(2)}, u32[]{:S(2)}) async-start(bf16[64,5,448]{2,1,0:T(8,128)(2,1)} %bitcast.28), calls=%async_computation.4 | async-start | bytes 1048576 | tf_op jit(solution)/shard_map/all_to_all | solution.py:69
  245.5 18.0 %all-to-all-done.4 = bf16[64,5,448]{2,1,0:T(8,128)(2,1)S(1)} async-done(((bf16[64,5,448]{2,1,0:T(8,128)(2,1)}), bf16[64,5,448]{2,1,0:T(8,128)(2,1)S(1)}, u32[]{:S(2)}, u32[]{:S(2)}) %all-to-all-start.4) | async-done | bytes 286752 | tf_op jit(solution)/shard_map/all_to_all | solution.py:69
  263.6 0.3 copy.123
  263.9 0.4 reshape.128
  264.3 0.7 gather_fusion.1
  265.4 0.6 multiply_reduce_fusion
  266.0 0.7 fusion.25
  (57 shorter events, 3.1 us)
Async XLA Ops:
  6.5 72.9 %copy-start = (bf16[1,3584,128]{2,1,0:T(8,128)(2,1)S(1)}, bf16[1,3584,128]{2,1,0:T(8,128)(2,1)}, u32[]{:S(2)}) copy-start(bf16[1,3584,128]{2,1,0:T(8,128)(2,1)} %param.12) | copy-start | bytes 2752516
  6.5 65.0 %all-gather.5.cloned.1.call-start = ((), (), s32[]{:S(2)}) async-start(), calls=%async_computation.5 | async-start | bytes 2580480 | tf_op jit(solution)/shard_map/all_gather | solution.py:55
  35.5 74.7 %all-to-all-start.1 = ((bf16[8,448,128]{2,1,0:T(8,128)(2,1)}), bf16[8,448,128]{2,1,0:T(8,128)(2,1)}, u32[]{:S(2)}, u32[]{:S(2)}) async-start(bf16[8,448,128]{2,1,0:T(8,128)(2,1)} %bitcast.13), calls=%async_computation.1 | async-start | bytes 1835008 | tf_op jit(solution)/shard_map/all_to_all | solution.py:87
  79.5 1.2 copy-start.1
  81.4 10.9 %collective-permute-start = (f32[2,320,128]{2,1,0:T(8,128)S(1)}, f32[2,320,128]{2,1,0:T(8,128)S(1)}, u32[]{:S(2)}, u32[]{:S(2)}) collective-permute-start(f32[2,320,128]{2,1,0:T(8,128)S(1)} %pad_maximum_fusion), channel_id=1, source_target_pairs={{0,1},{1,0},{2,3},{3,2},{4,5},{5,4},{6,7},{7,6},{8,9},{9,8},{10,11... | collective-permute-start | bytes 983048 | tf_op jit(solution)/shard_map/ppermute | solution.py:15
  110.2 8.9 %copy-start.5 = (f32[1,2,8,2]{2,3,1,0:T(2,128)S(1)}, f32[1,2,8,2]{2,3,1,0:T(2,128)}, u32[]{:S(2)}) copy-start(f32[1,2,8,2]{2,3,1,0:T(2,128)} %param.15) | copy-start | bytes 388
  112.9 24.2 %all-to-all-start.2 = ((bf16[64,5,448]{2,1,0:T(8,128)(2,1)}), bf16[64,5,448]{2,1,0:T(8,128)(2,1)S(1)}, u32[]{:S(2)}, u32[]{:S(2)}) async-start(bf16[64,5,448]{2,1,0:T(8,128)(2,1)} %bitcast.16), calls=%async_computation.2 | async-start | bytes 1048576 | tf_op jit(solution)/shard_map/all_to_all | solution.py:69
  119.0 77.1 %all-gather.7.cloned.1.call-start = ((), (), s32[]{:S(2)}) async-start(), calls=%async_computation.6 | async-start | bytes 2580480 | tf_op jit(solution)/shard_map/all_gather | solution.py:55
  137.9 1.7 copy-start.3
  137.9 9.4 %copy-start.4 = (f32[1,7168]{1,0:T(1,128)S(1)}, f32[1,7168]{1,0:T(1,128)}, u32[]{:S(2)}) copy-start(f32[1,7168]{1,0:T(1,128)} %param.10) | copy-start | bytes 86020
  139.7 7.4 %collective-permute-start.1 = (bf16[8,7168]{1,0:T(8,128)(2,1)S(1)}, bf16[8,7168]{1,0:T(8,128)(2,1)S(1)}, u32[]{:S(2)}, u32[]{:S(2)}) collective-permute-start(bf16[8,7168]{1,0:T(8,128)(2,1)S(1)} %fusion.19), channel_id=1, source_target_pairs={{0,64},{64,128},{128,192},{192,256},{256,320},{320,384},{384,448},... | collective-permute-start | bytes 344072 | tf_op jit(solution)/shard_map/ppermute | solution.py:15
  204.1 1.2 copy-start.2
  206.0 10.9 %collective-permute-start.2 = (f32[2,320,128]{2,1,0:T(8,128)S(1)}, f32[2,320,128]{2,1,0:T(8,128)S(1)}, u32[]{:S(2)}, u32[]{:S(2)}) collective-permute-start(f32[2,320,128]{2,1,0:T(8,128)S(1)} %pad_maximum_fusion.1), channel_id=1, source_target_pairs={{0,1},{1,0},{2,3},{3,2},{4,5},{5,4},{6,7},{7,6},{8,9},{9,8},{10,11... | collective-permute-start | bytes 983048 | tf_op jit(solution)/shard_map/ppermute | solution.py:15
  237.6 26.0 %all-to-all-start.4 = ((bf16[64,5,448]{2,1,0:T(8,128)(2,1)}), bf16[64,5,448]{2,1,0:T(8,128)(2,1)S(1)}, u32[]{:S(2)}, u32[]{:S(2)}) async-start(bf16[64,5,448]{2,1,0:T(8,128)(2,1)} %bitcast.28), calls=%async_computation.4 | async-start | bytes 1048576 | tf_op jit(solution)/shard_map/all_to_all | solution.py:69
Sparse Core Ops, SparseCore 0:
  35.6 35.8 all-gather.4
  162.4 33.6 all-gather.6

commit v3 on v2

--- a/solution.py
+++ b/solution.py
@@ -49,12 +49,15 @@
     capacity = min(tok_rows, max(2, 5 * tok_rows * fan_out // (4 * experts)))
     half = model_width // halves
     widened, outgoing, target = route(stream, gain_row, routes, experts, capacity)
-    send = outgoing.reshape(experts, capacity, halves, half).transpose(0, 2, 1, 3)
-    send = send.reshape(experts * halves, capacity, half)
+    lanes = 128
+    tiles = half // lanes
+    send = outgoing.reshape(experts, capacity, halves, tiles, lanes).transpose(0, 2, 1, 3, 4)
+    send = send.reshape(experts * halves, capacity * tiles, lanes)
     arrived = lax.all_to_all(send, ("eg", "dp"), split_axis=0, concat_axis=0, tiled=True)
-    arrived = lax.all_gather(arrived, "q", axis=0, tiled=False)
+    arrived = arrived.reshape(experts * halves, capacity, half).transpose(1, 0, 2)
+    arrived = lax.all_gather(arrived, "q", axis=1, tiled=True)
     sources = blocks * experts * halves
-    rows = arrived.reshape(sources * capacity, half)
+    rows = arrived.reshape(capacity * sources, half)
     gate_part = jnp.dot(rows, gate_w, preferred_element_type=jnp.float32)
     up_part = jnp.dot(rows, up_w, preferred_element_type=jnp.float32)
     mine = jnp.stack([gate_part, up_part])
@@ -65,7 +68,7 @@
         hidden_all, down_mine, (((1,), (1,)), ((), ())), preferred_element_type=jnp.float32
     ).astype(jnp.bfloat16)
     piece = out.shape[1]
-    out = out.reshape(blocks, experts, halves, capacity, piece).transpose(1, 0, 2, 3, 4)
+    out = out.reshape(capacity, blocks, experts, halves, piece).transpose(2, 1, 3, 0, 4)
     back = lax.all_to_all(
         out.reshape(sources, capacity, piece), ALL, split_axis=0, concat_axis=0, tiled=True
     )

time: 274 us -> 254 us (0.927)
  local copies, waits for them, and re-layouts: 25.6 us -> 10.8 us
  waiting for transfers between devices: 118 us -> 115 us
    all_gather x2 -> x0, local copies, waits for them, and re-layouts: 9.47 us -> none  [moe_layer(): arrived = lax.all_gather(arrived, 'q', axis=0, tiled=False)]
    reshape x6 -> x4, local copies, waits for them, and re-layouts: 6.8 us -> 1.35 us  [the longest x2 1.27 us: moe_layer(): out.reshape(capacity, blocks, experts, halves, piece)]
    dot_general x2, matrix products: 1.51 us -> 5.09 us  [moe_layer(): up_part = jnp.dot(rows, up_w, preferred_element_type=jnp.float32)]
    all_gather x2, waiting for transfers between devices: 60.3 us -> 56.9 us  [moe_layer(): arrived = lax.all_gather(arrived, 'q', axis=1, tiled=True)]
  transfers between devices with their start and end apart: 8 -> 8, of which waited for: 7 -> 7; matrix products, arithmetic and copies ran while one was open for 4% -> 1% of each run, Pallas kernels for 0% -> 0%
where the time goes in v3:
time: 254 us
  waiting for transfers between devices  115 us (45%)
  blocking collectives  70 us (28%)
  starting transfers between devices  29.7 us (12%)
  between operations  13.8 us (5%)
  local copies, waits for them, and re-layouts  10.8 us (4%)
  matrix products  10.2 us (4%)
  other arithmetic  4.62 us (2%)
    all_gather x2, waiting for transfers between devices, moe_layer(): arrived = lax.all_gather(arrived, 'q', axis=1, tiled=True)  56.9 us
    all_to_all x2, waiting for transfers between devices, moe_layer(): lax.all_to_all(out.reshape(sources, capacity, piece), ALL, split_axis=0,...  36 us
    all_gather x2, blocking collectives, moe_layer(): hidden_all = lax.all_gather(hidden, 'q', axis=1, tiled=True)  35.4 us
    all_to_all x2, blocking collectives, moe_layer(): lax.all_to_all(send, ('eg', 'dp'), split_axis=0, concat_axis=0, tiled=True)  34.7 us
    ppermute x3, waiting for transfers between devices, passed_along(): lax.ppermute(array, axis, [(i, (i + by) % length) for i in range(length)])  21.7 us
    all_to_all x2, starting transfers between devices, moe_layer(): lax.all_to_all(out.reshape(sources, capacity, piece), ALL, split_axis=0,...  13.9 us
    all_to_all x1, starting transfers between devices, on_device(): lax.all_to_all(down_local.reshape(n_blocks, piece, width), 'q', split_axi...  8.24 us
    ppermute x3, starting transfers between devices, passed_along(): lax.ppermute(array, axis, [(i, (i + by) % length) for i in range(length)])  7.5 us
  transfers between devices with their start and end apart: 8, of which 7 were waited for; matrix products, arithmetic and copies ran while one was open for 1% of the time, Pallas kernels for 0%

profile of v3, /device:TPU:1, one launch (start us, length us, event | category | flops | bytes accessed | tf_op | source)
XLA Modules:
  0.0 253.7 jit_solution(13206537707520882643)
XLA Ops:
  6.5 0.8 fusion.38
  8.3 0.7 bitcast_add_fusion.1
  9.1 1.1 fusion.16
  10.2 1.2 convolution_convert_fusion.1
  11.4 0.2 reshape_reshape.6
  11.6 0.2 copy.57
  11.9 21.8 %all_to_all.25 = bf16[8,140,128]{2,1,0:T(8,128)(2,1)S(1)} all-to-all(bf16[8,140,128]{2,1,0:T(8,128)(2,1)S(1)} %copy.58), channel_id=1, replica_groups=mesh['section'=8,'eg'=4,'q'=8,'dp'=2] {'eg','dp'}, dimensions={0} | all-to-all | bytes 573440 | tf_op jit(solution)/shard_map/all_to_all | solution.py:56
  33.7 0.8 copy.59
  34.5 8.2 %all-to-all-start.1 = ((bf16[8,448,128]{2,1,0:T(8,128)(2,1)}), bf16[8,448,128]{2,1,0:T(8,128)(2,1)S(1)}, u32[]{:S(2)}, u32[]{:S(2)}) async-start(bf16[8,448,128]{2,1,0:T(8,128)(2,1)} %bitcast.16), calls=%async_computation.1 | async-start | bytes 1835008 | tf_op jit(solution)/shard_map/all_to_all | solution.py:90
  42.7 25.7 %all-gather.3.cloned.1.call-done = bf16[5,64,3584]{2,1,0:T(8,128)(2,1)} async-done(((bf16[5,8,3584]{2,1,0:T(8,128)(2,1)}), bf16[5,64,3584]{2,1,0:T(8,128)(2,1)}) %all-gather.3.cloned.1.call-update) | async-done | bytes 2293776 | tf_op jit(solution)/shard_map/all_gather | solution.py:58
  68.5 2.5 %convolution_bitcast_fusion.2 = f32[1,320,128]{2,1,0:T(8,128)S(1)} fusion(bf16[320,3584]{1,0:T(8,128)(2,1)} %bitcast.113, bf16[1,3584,128]{2,1,0:T(8,128)(2,1)S(1)} %copy-done), kind=kOutput, calls=%fused_computation.8 | convolution fusion | flops 293601280 | bytes 3375104 | tf_op jit(solution)/shard_map/dot_general | solution.py:62
  71.0 0.8 convolution_bitcast_fusion.3
  71.8 2.1 collective-permute-start
  73.9 8.8 %collective-permute-done = f32[2,320,128]{2,1,0:T(8,128)S(1)} collective-permute-done((f32[2,320,128]{2,1,0:T(8,128)S(1)}, f32[2,320,128]{2,1,0:T(8,128)S(1)}, u32[]{:S(2)}, u32[]{:S(2)}) %collective-permute-start) | collective-permute-done | bytes 327712 | tf_op jit(solution)/shard_map/ppermute | solution.py:15
  82.8 17.7 %all_gather.13 = bf16[320,1024]{1,0:T(8,128)(2,1)S(1)} all-gather(bf16[320,128]{1,0:T(8,128)(2,1)S(1)} %fusion.23), channel_id=1, replica_groups=mesh['section'=8,'eg'=4,'q'=8,'dp'=2] {'q'}, dimensions={1}, use_global_device_ids=true | all-gather | bytes 737280 | tf_op jit(solution)/shard_map/all_gather | solution.py:66
  100.5 1.3 convolution_convert_fusion.3
  101.7 1.1 reshape.126
  102.9 1.0 copy.75
  103.8 6.1 %all-to-all-start.2 = ((bf16[64,5,448]{2,1,0:T(8,128)(2,1)}), bf16[64,5,448]{2,1,0:T(8,128)(2,1)S(1)}, u32[]{:S(2)}, u32[]{:S(2)}) async-start(bf16[64,5,448]{2,1,0:T(8,128)(2,1)} %bitcast.19), calls=%async_computation.2 | async-start | bytes 1048576 | tf_op jit(solution)/shard_map/all_to_all | solution.py:72
  110.1 18.0 %all-to-all-done.2 = bf16[64,5,448]{2,1,0:T(8,128)(2,1)S(1)} async-done(((bf16[64,5,448]{2,1,0:T(8,128)(2,1)}), bf16[64,5,448]{2,1,0:T(8,128)(2,1)S(1)}, u32[]{:S(2)}, u32[]{:S(2)}) %all-to-all-start.2) | async-done | bytes 286752 | tf_op jit(solution)/shard_map/all_to_all | solution.py:72
  128.1 0.3 copy.93
  128.5 0.4 reshape.129
  128.9 0.7 gather_fusion
  129.7 0.3 reshape.138
  130.0 0.6 multiply_reduce_fusion.1
  130.6 3.1 %collective-permute-start.1 = (bf16[8,7168]{1,0:T(8,128)(2,1)S(1)}, bf16[8,7168]{1,0:T(8,128)(2,1)S(1)}, u32[]{:S(2)}, u32[]{:S(2)}) collective-permute-start(bf16[8,7168]{1,0:T(8,128)(2,1)S(1)} %fusion.19), channel_id=1, source_target_pairs={{0,64},{64,128},{128,192},{192,256},{256,320},{320,384},{384,448},... | collective-permute-start | bytes 344072 | tf_op jit(solution)/shard_map/ppermute | solution.py:15
  133.8 4.2 %collective-permute-done.1 = bf16[8,7168]{1,0:T(8,128)(2,1)S(1)} collective-permute-done((bf16[8,7168]{1,0:T(8,128)(2,1)S(1)}, bf16[8,7168]{1,0:T(8,128)(2,1)S(1)}, u32[]{:S(2)}, u32[]{:S(2)}) %collective-permute-start.1) | collective-permute-done | bytes 114720 | tf_op jit(solution)/shard_map/ppermute | solution.py:15
  138.3 0.3 convolution_convert_fusion
  138.6 0.2 reshape_reshape.7
  138.8 0.2 copy.68
  139.1 12.9 %all_to_all.26 = bf16[8,140,128]{2,1,0:T(8,128)(2,1)S(1)} all-to-all(bf16[8,140,128]{2,1,0:T(8,128)(2,1)S(1)} %copy.69), channel_id=1, replica_groups=mesh['section'=8,'eg'=4,'q'=8,'dp'=2] {'eg','dp'}, dimensions={0} | all-to-all | bytes 573440 | tf_op jit(solution)/shard_map/all_to_all | solution.py:56
  152.0 0.8 copy.70
  152.8 31.2 %all-gather.5.cloned.1.call-done = bf16[5,64,3584]{2,1,0:T(8,128)(2,1)} async-done(((bf16[5,8,3584]{2,1,0:T(8,128)(2,1)}), bf16[5,64,3584]{2,1,0:T(8,128)(2,1)}) %all-gather.5.cloned.1.call-update) | async-done | bytes 2293776 | tf_op jit(solution)/shard_map/all_gather | solution.py:58
  184.0 2.5 %convolution_bitcast_fusion = f32[1,320,128]{2,1,0:T(8,128)S(1)} fusion(bf16[320,3584]{1,0:T(8,128)(2,1)} %bitcast.115, bf16[1,3584,128]{2,1,0:T(8,128)(2,1)S(1)} %copy-done), kind=kOutput, calls=%fused_computation.6 | convolution fusion | flops 293601280 | bytes 3375104 | tf_op jit(solution)/shard_map/dot_general | solution.py:62
  186.5 0.8 convolution_bitcast_fusion.1
  187.3 2.3 collective-permute-start.2
  189.7 8.7 %collective-permute-done.2 = f32[2,320,128]{2,1,0:T(8,128)S(1)} collective-permute-done((f32[2,320,128]{2,1,0:T(8,128)S(1)}, f32[2,320,128]{2,1,0:T(8,128)S(1)}, u32[]{:S(2)}, u32[]{:S(2)}) %collective-permute-start.2) | collective-permute-done | bytes 327712 | tf_op jit(solution)/shard_map/ppermute | solution.py:15
  198.4 17.7 %all_gather.15 = bf16[320,1024]{1,0:T(8,128)(2,1)S(1)} all-gather(bf16[320,128]{1,0:T(8,128)(2,1)S(1)} %fusion.21), channel_id=1, replica_groups=mesh['section'=8,'eg'=4,'q'=8,'dp'=2] {'q'}, dimensions={1}, use_global_device_ids=true | all-gather | bytes 737280 | tf_op jit(solution)/shard_map/all_gather | solution.py:66
  216.2 0.5 convolution_convert_fusion.2
  216.8 1.0 copy.77
  217.8 7.8 %all-to-all-start.4 = ((bf16[64,5,448]{2,1,0:T(8,128)(2,1)}), bf16[64,5,448]{2,1,0:T(8,128)(2,1)S(1)}, u32[]{:S(2)}, u32[]{:S(2)}) async-start(bf16[64,5,448]{2,1,0:T(8,128)(2,1)} %bitcast.34), calls=%async_computation.4 | async-start | bytes 1048576 | tf_op jit(solution)/shard_map/all_to_all | solution.py:72
  225.7 18.0 %all-to-all-done.4 = bf16[64,5,448]{2,1,0:T(8,128)(2,1)S(1)} async-done(((bf16[64,5,448]{2,1,0:T(8,128)(2,1)}), bf16[64,5,448]{2,1,0:T(8,128)(2,1)S(1)}, u32[]{:S(2)}, u32[]{:S(2)}) %all-to-all-start.4) | async-done | bytes 286752 | tf_op jit(solution)/shard_map/all_to_all | solution.py:72
  243.8 0.3 copy.92
  244.1 0.4 reshape.136
  244.5 0.7 gather_fusion.1
  245.3 0.3 reshape.139
  245.6 0.6 multiply_reduce_fusion
  246.2 0.7 fusion.25
  (61 shorter events, 2.4 us)
Async XLA Ops:
  6.5 61.9 %copy-start = (bf16[1,3584,128]{2,1,0:T(8,128)(2,1)S(1)}, bf16[1,3584,128]{2,1,0:T(8,128)(2,1)}, u32[]{:S(2)}) copy-start(bf16[1,3584,128]{2,1,0:T(8,128)(2,1)} %param.12) | copy-start | bytes 2752516
  6.5 61.9 %all-gather.3.cloned.1.call-start = ((), (), s32[]{:S(2)}) async-start(), calls=%async_computation.5 | async-start | bytes 2580480 | tf_op jit(solution)/shard_map/all_gather | solution.py:58
  34.5 66.0 %all-to-all-start.1 = ((bf16[8,448,128]{2,1,0:T(8,128)(2,1)}), bf16[8,448,128]{2,1,0:T(8,128)(2,1)S(1)}, u32[]{:S(2)}, u32[]{:S(2)}) async-start(bf16[8,448,128]{2,1,0:T(8,128)(2,1)} %bitcast.16), calls=%async_computation.1 | async-start | bytes 1835008 | tf_op jit(solution)/shard_map/all_to_all | solution.py:90
  42.7 28.3 %copy-start.3 = (bf16[1,3584,128]{2,1,0:T(8,128)(2,1)S(1)}, bf16[1,3584,128]{2,1,0:T(8,128)(2,1)}, u32[]{:S(2)}) copy-start(bf16[1,3584,128]{2,1,0:T(8,128)(2,1)} %param.11) | copy-start | bytes 2752516
  68.5 2.6 %copy-start.1 = (bf16[5,64,3584]{2,1,0:T(8,128)(2,1)S(1)}, bf16[5,64,3584]{2,1,0:T(8,128)(2,1)}, u32[]{:S(2)}) copy-start(bf16[5,64,3584]{2,1,0:T(8,128)(2,1)} %all-gather.3.cloned.1.call-done) | copy-start | bytes 6881284
  71.8 10.9 %collective-permute-start = (f32[2,320,128]{2,1,0:T(8,128)S(1)}, f32[2,320,128]{2,1,0:T(8,128)S(1)}, u32[]{:S(2)}, u32[]{:S(2)}) collective-permute-start(f32[2,320,128]{2,1,0:T(8,128)S(1)} %pad_maximum_fusion), channel_id=1, source_target_pairs={{0,1},{1,0},{2,3},{3,2},{4,5},{5,4},{6,7},{7,6},{8,9},{9,8},{10,11... | collective-permute-start | bytes 983048 | tf_op jit(solution)/shard_map/ppermute | solution.py:15
  100.5 9.5 %copy-start.8 = (f32[1,2,8,2]{2,3,1,0:T(2,128)S(1)}, f32[1,2,8,2]{2,3,1,0:T(2,128)}, u32[]{:S(2)}) copy-start(f32[1,2,8,2]{2,3,1,0:T(2,128)} %param.15) | copy-start | bytes 388
  100.5 3.4 %copy-start.5 = (bf16[8,448,128]{2,1,0:T(8,128)(2,1)}, bf16[8,448,128]{2,1,0:T(8,128)(2,1)S(1)}, u32[]{:S(2)}) copy-start(bf16[8,448,128]{2,1,0:T(8,128)(2,1)S(1)} %all-to-all-done.1) | copy-start | bytes 2752516
  103.8 24.3 %all-to-all-start.2 = ((bf16[64,5,448]{2,1,0:T(8,128)(2,1)}), bf16[64,5,448]{2,1,0:T(8,128)(2,1)S(1)}, u32[]{:S(2)}, u32[]{:S(2)}) async-start(bf16[64,5,448]{2,1,0:T(8,128)(2,1)} %bitcast.19), calls=%async_computation.2 | async-start | bytes 1048576 | tf_op jit(solution)/shard_map/all_to_all | solution.py:72
  110.0 74.0 %all-gather.5.cloned.1.call-start = ((), (), s32[]{:S(2)}) async-start(), calls=%async_computation.6 | async-start | bytes 2580480 | tf_op jit(solution)/shard_map/all_gather | solution.py:58
  128.9 1.7 copy-start.4
  128.9 9.4 %copy-start.7 = (f32[1,7168]{1,0:T(1,128)S(1)}, f32[1,7168]{1,0:T(1,128)}, u32[]{:S(2)}) copy-start(f32[1,7168]{1,0:T(1,128)} %param.10) | copy-start | bytes 86020
  130.6 7.4 %collective-permute-start.1 = (bf16[8,7168]{1,0:T(8,128)(2,1)S(1)}, bf16[8,7168]{1,0:T(8,128)(2,1)S(1)}, u32[]{:S(2)}, u32[]{:S(2)}) collective-permute-start(bf16[8,7168]{1,0:T(8,128)(2,1)S(1)} %fusion.19), channel_id=1, source_target_pairs={{0,64},{64,128},{128,192},{192,256},{256,320},{320,384},{384,448},... | collective-permute-start | bytes 344072 | tf_op jit(solution)/shard_map/ppermute | solution.py:15
  184.0 2.6 %copy-start.2 = (bf16[5,64,3584]{2,1,0:T(8,128)(2,1)S(1)}, bf16[5,64,3584]{2,1,0:T(8,128)(2,1)}, u32[]{:S(2)}) copy-start(bf16[5,64,3584]{2,1,0:T(8,128)(2,1)} %all-gather.5.cloned.1.call-done) | copy-start | bytes 6881284
  187.3 28.9 %copy-start.6 = (bf16[8,448,128]{2,1,0:T(8,128)(2,1)S(1)}, bf16[8,448,128]{2,1,0:T(8,128)(2,1)}, u32[]{:S(2)}) copy-start(bf16[8,448,128]{2,1,0:T(8,128)(2,1)} %copy-done.5) | copy-start | bytes 2752516
  187.3 11.0 %collective-permute-start.2 = (f32[2,320,128]{2,1,0:T(8,128)S(1)}, f32[2,320,128]{2,1,0:T(8,128)S(1)}, u32[]{:S(2)}, u32[]{:S(2)}) collective-permute-start(f32[2,320,128]{2,1,0:T(8,128)S(1)} %pad_maximum_fusion.1), channel_id=1, source_target_pairs={{0,1},{1,0},{2,3},{3,2},{4,5},{5,4},{6,7},{7,6},{8,9},{9,8},{10,11... | collective-permute-start | bytes 983048 | tf_op jit(solution)/shard_map/ppermute | solution.py:15
  217.8 26.0 %all-to-all-start.4 = ((bf16[64,5,448]{2,1,0:T(8,128)(2,1)}), bf16[64,5,448]{2,1,0:T(8,128)(2,1)S(1)}, u32[]{:S(2)}, u32[]{:S(2)}) async-start(bf16[64,5,448]{2,1,0:T(8,128)(2,1)} %bitcast.34), calls=%async_computation.4 | async-start | bytes 1048576 | tf_op jit(solution)/shard_map/all_to_all | solution.py:72
Sparse Core Ops, SparseCore 0:
  34.6 33.8 all-gather.2
  152.9 31.0 all-gather.4

commit v4 on v3

--- a/solution.py
+++ b/solution.py
@@ -70,7 +70,7 @@
     piece = out.shape[1]
     out = out.reshape(capacity, blocks, experts, halves, piece).transpose(2, 1, 3, 0, 4)
     back = lax.all_to_all(
-        out.reshape(sources, capacity, piece), ALL, split_axis=0, concat_axis=0, tiled=True
+        out.reshape(sources, capacity * piece), ALL, split_axis=0, concat_axis=0, tiled=True
     )
     back = back.reshape(experts, blocks, halves, capacity, piece).transpose(0, 3, 2, 1, 4)
     expert_out = back.reshape(experts * capacity, model_width)

time: 254 us -> 258 us (1.016)
  waiting for transfers between devices: 115 us -> 106 us
  other arithmetic: 4.62 us -> 13.2 us
  local copies, waits for them, and re-layouts: 10.8 us -> 14.6 us
    all_to_all x0 -> x4, other arithmetic: none -> 8.58 us  [moe_layer(): lax.all_to_all(out.reshape(sources, capacity * piece), ALL, split_axis=0,...]
    all_to_all x2, waiting for transfers between devices: 36 us -> 27.6 us  [moe_layer(): lax.all_to_all(out.reshape(sources, capacity * piece), ALL, split_axis=0,...]
    unnamed x18 -> x22, local copies, waits for them, and re-layouts: 0.04 us -> 2.92 us
where the time goes in v4:
time: 258 us; the launch traced here: 257 us
  waiting for transfers between devices  106 us (41%)
  blocking collectives  69.7 us (27%)
  starting transfers between devices  29.8 us (12%)
  local copies, waits for them, and re-layouts  14.6 us (6%)
  between operations  13.9 us (5%)
  other arithmetic  13.2 us (5%)
  matrix products  10.2 us (4%)
    all_gather x2, waiting for transfers between devices, moe_layer(): arrived = lax.all_gather(arrived, 'q', axis=1, tiled=True)  56.3 us
    all_gather x2, blocking collectives, moe_layer(): hidden_all = lax.all_gather(hidden, 'q', axis=1, tiled=True)  35.4 us
    all_to_all x2, blocking collectives, moe_layer(): lax.all_to_all(send, ('eg', 'dp'), split_axis=0, concat_axis=0, tiled=True)  34.3 us
    all_to_all x2, waiting for transfers between devices, moe_layer(): lax.all_to_all(out.reshape(sources, capacity * piece), ALL, split_axis=0,...  27.6 us
    ppermute x3, waiting for transfers between devices, passed_along(): lax.ppermute(array, axis, [(i, (i + by) % length) for i in range(length)])  22 us
    all_to_all x2, starting transfers between devices, moe_layer(): lax.all_to_all(out.reshape(sources, capacity * piece), ALL, split_axis=0,...  13.9 us
    all_to_all x4, other arithmetic, moe_layer(): lax.all_to_all(out.reshape(sources, capacity * piece), ALL, split_axis=0,...  8.58 us
    all_to_all x1, starting transfers between devices, on_device(): lax.all_to_all(down_local.reshape(n_blocks, piece, width), 'q', split_axi...  8.2 us
  transfers between devices with their start and end apart: 8, of which 7 were waited for; matrix products, arithmetic and copies ran while one was open for 1% of the time, Pallas kernels for 0%

profile of v4, /device:TPU:1, one launch (start us, length us, event | category | flops | bytes accessed | tf_op | source)
XLA Modules:
  0.0 257.2 jit_solution(10725979228858116910)
XLA Ops:
  6.5 0.8 fusion.38
  8.3 0.7 bitcast_add_fusion.1
  9.1 1.1 fusion.16
  10.2 1.2 convolution_convert_fusion.1
  11.9 21.8 %all_to_all.35 = bf16[8,140,128]{2,1,0:T(8,128)(2,1)S(1)} all-to-all(bf16[8,140,128]{2,1,0:T(8,128)(2,1)S(1)} %copy.56), channel_id=1, replica_groups=mesh['section'=8,'eg'=4,'q'=8,'dp'=2] {'eg','dp'}, dimensions={0} | all-to-all | bytes 573440 | tf_op jit(solution)/shard_map/all_to_all | solution.py:56
  33.7 0.8 copy.57
  34.5 8.2 %all-to-all-start.1 = ((bf16[8,448,128]{2,1,0:T(8,128)(2,1)}), bf16[8,448,128]{2,1,0:T(8,128)(2,1)S(1)}, u32[]{:S(2)}, u32[]{:S(2)}) async-start(bf16[8,448,128]{2,1,0:T(8,128)(2,1)} %bitcast.16), calls=%async_computation.1 | async-start | bytes 1835008 | tf_op jit(solution)/shard_map/all_to_all | solution.py:90
  42.7 25.7 %all-gather.3.cloned.1.call-done = bf16[5,64,3584]{2,1,0:T(8,128)(2,1)} async-done(((bf16[5,8,3584]{2,1,0:T(8,128)(2,1)}), bf16[5,64,3584]{2,1,0:T(8,128)(2,1)}) %all-gather.3.cloned.1.call-update) | async-done | bytes 2293776 | tf_op jit(solution)/shard_map/all_gather | solution.py:58
  68.5 2.5 convolution_bitcast_fusion.2
  71.0 0.8 convolution_bitcast_fusion.3
  71.8 2.1 collective-permute-start
  73.9 8.8 %collective-permute-done = f32[2,320,128]{2,1,0:T(8,128)S(1)} collective-permute-done((f32[2,320,128]{2,1,0:T(8,128)S(1)}, f32[2,320,128]{2,1,0:T(8,128)S(1)}, u32[]{:S(2)}, u32[]{:S(2)}) %collective-permute-start) | collective-permute-done | bytes 327712 | tf_op jit(solution)/shard_map/ppermute | solution.py:15
  82.8 17.7 %all_gather.13 = bf16[320,1024]{1,0:T(8,128)(2,1)S(1)} all-gather(bf16[320,128]{1,0:T(8,128)(2,1)S(1)} %fusion.23), channel_id=1, replica_groups=mesh['section'=8,'eg'=4,'q'=8,'dp'=2] {'q'}, dimensions={1}, use_global_device_ids=true | all-gather | bytes 737280 | tf_op jit(solution)/shard_map/all_gather | solution.py:66
  100.5 1.2 convolution_convert_fusion.3
  101.7 1.1 reshape.130
  103.1 0.6 all_to_all.28
  103.6 0.5 broadcast.130
  104.1 2.5 reduce.2
  106.6 1.0 reshape.166
  107.6 6.1 %all-to-all-start.2 = ((bf16[64,2,1120]{2,1,0:T(2,128)(2,1)}), bf16[64,2,1120]{2,1,0:T(2,128)(2,1)S(1)}, u32[]{:S(2)}, u32[]{:S(2)}) async-start(bf16[64,2,1120]{2,1,0:T(2,128)(2,1)} %reshape.166), calls=%async_computation.2 | async-start | bytes 589824 | tf_op jit(solution)/shard_map/all_to_all | solution.py:72
  113.9 13.8 %all-to-all-done.2 = bf16[64,2,1120]{2,1,0:T(2,128)(2,1)S(1)} async-done(((bf16[64,2,1120]{2,1,0:T(2,128)(2,1)}), bf16[64,2,1120]{2,1,0:T(2,128)(2,1)S(1)}, u32[]{:S(2)}, u32[]{:S(2)}) %all-to-all-start.2) | async-done | bytes 286752 | tf_op jit(solution)/shard_map/all_to_all | solution.py:72
  127.6 0.4 reshape.167
  128.1 1.8 reduce
  129.9 0.6 reshape.131
  131.1 0.7 gather_fusion
  132.2 0.6 multiply_reduce_fusion.1
  132.9 3.3 %collective-permute-start.1 = (bf16[8,7168]{1,0:T(8,128)(2,1)S(1)}, bf16[8,7168]{1,0:T(8,128)(2,1)S(1)}, u32[]{:S(2)}, u32[]{:S(2)}) collective-permute-start(bf16[8,7168]{1,0:T(8,128)(2,1)S(1)} %fusion.19), channel_id=1, source_target_pairs={{0,64},{64,128},{128,192},{192,256},{256,320},{320,384},{384,448},... | collective-permute-start | bytes 344072 | tf_op jit(solution)/shard_map/ppermute | solution.py:15
  136.3 4.5 %collective-permute-done.1 = bf16[8,7168]{1,0:T(8,128)(2,1)S(1)} collective-permute-done((bf16[8,7168]{1,0:T(8,128)(2,1)S(1)}, bf16[8,7168]{1,0:T(8,128)(2,1)S(1)}, u32[]{:S(2)}, u32[]{:S(2)}) %collective-permute-start.1) | collective-permute-done | bytes 114720 | tf_op jit(solution)/shard_map/ppermute | solution.py:15
  141.8 12.5 %all_to_all.36 = bf16[8,140,128]{2,1,0:T(8,128)(2,1)S(1)} all-to-all(bf16[8,140,128]{2,1,0:T(8,128)(2,1)S(1)} %copy.66), channel_id=1, replica_groups=mesh['section'=8,'eg'=4,'q'=8,'dp'=2] {'eg','dp'}, dimensions={0} | all-to-all | bytes 573440 | tf_op jit(solution)/shard_map/all_to_all | solution.py:56
  154.3 0.8 copy.67
  155.1 30.6 %all-gather.5.cloned.1.call-done = bf16[5,64,3584]{2,1,0:T(8,128)(2,1)} async-done(((bf16[5,8,3584]{2,1,0:T(8,128)(2,1)}), bf16[5,64,3584]{2,1,0:T(8,128)(2,1)}) %all-gather.5.cloned.1.call-update) | async-done | bytes 2293776 | tf_op jit(solution)/shard_map/all_gather | solution.py:58
  185.7 2.5 convolution_bitcast_fusion
  188.2 0.8 convolution_bitcast_fusion.1
  189.0 2.3 collective-permute-start.2
  191.4 8.7 %collective-permute-done.2 = f32[2,320,128]{2,1,0:T(8,128)S(1)} collective-permute-done((f32[2,320,128]{2,1,0:T(8,128)S(1)}, f32[2,320,128]{2,1,0:T(8,128)S(1)}, u32[]{:S(2)}, u32[]{:S(2)}) %collective-permute-start.2) | collective-permute-done | bytes 327712 | tf_op jit(solution)/shard_map/ppermute | solution.py:15
  200.2 17.7 %all_gather.15 = bf16[320,1024]{1,0:T(8,128)(2,1)S(1)} all-gather(bf16[320,128]{1,0:T(8,128)(2,1)S(1)} %fusion.21), channel_id=1, replica_groups=mesh['section'=8,'eg'=4,'q'=8,'dp'=2] {'q'}, dimensions={1}, use_global_device_ids=true | all-gather | bytes 737280 | tf_op jit(solution)/shard_map/all_gather | solution.py:66
  217.9 0.5 convolution_convert_fusion.2
  218.8 0.6 all_to_all.29
  219.3 2.5 reduce.3
  221.8 1.0 reshape.168
  222.8 7.8 %all-to-all-start.4 = ((bf16[64,2,1120]{2,1,0:T(2,128)(2,1)}), bf16[64,2,1120]{2,1,0:T(2,128)(2,1)S(1)}, u32[]{:S(2)}, u32[]{:S(2)}) async-start(bf16[64,2,1120]{2,1,0:T(2,128)(2,1)} %reshape.168), calls=%async_computation.4 | async-start | bytes 589824 | tf_op jit(solution)/shard_map/all_to_all | solution.py:72
  230.7 13.8 %all-to-all-done.4 = bf16[64,2,1120]{2,1,0:T(2,128)(2,1)S(1)} async-done(((bf16[64,2,1120]{2,1,0:T(2,128)(2,1)}), bf16[64,2,1120]{2,1,0:T(2,128)(2,1)S(1)}, u32[]{:S(2)}, u32[]{:S(2)}) %all-to-all-start.4) | async-done | bytes 286752 | tf_op jit(solution)/shard_map/all_to_all | solution.py:72
  244.5 0.4 reshape.169
  245.0 1.8 reduce.1
  246.8 0.6 reshape.137
  248.0 0.7 gather_fusion.1
  249.1 0.6 multiply_reduce_fusion
  249.7 0.7 fusion.25
  (72 shorter events, 5.6 us)
Async XLA Ops:
  6.5 61.9 %copy-start = (bf16[1,3584,128]{2,1,0:T(8,128)(2,1)S(1)}, bf16[1,3584,128]{2,1,0:T(8,128)(2,1)}, u32[]{:S(2)}) copy-start(bf16[1,3584,128]{2,1,0:T(8,128)(2,1)} %param.12) | copy-start | bytes 2752516
  6.5 61.9 %all-gather.3.cloned.1.call-start = ((), (), s32[]{:S(2)}) async-start(), calls=%async_computation.5 | async-start | bytes 2580480 | tf_op jit(solution)/shard_map/all_gather | solution.py:58
  34.5 66.0 %all-to-all-start.1 = ((bf16[8,448,128]{2,1,0:T(8,128)(2,1)}), bf16[8,448,128]{2,1,0:T(8,128)(2,1)S(1)}, u32[]{:S(2)}, u32[]{:S(2)}) async-start(bf16[8,448,128]{2,1,0:T(8,128)(2,1)} %bitcast.16), calls=%async_computation.1 | async-start | bytes 1835008 | tf_op jit(solution)/shard_map/all_to_all | solution.py:90
  42.7 28.3 %copy-start.3 = (bf16[1,3584,128]{2,1,0:T(8,128)(2,1)S(1)}, bf16[1,3584,128]{2,1,0:T(8,128)(2,1)}, u32[]{:S(2)}) copy-start(bf16[1,3584,128]{2,1,0:T(8,128)(2,1)} %param.11) | copy-start | bytes 2752516
  68.4 2.6 copy-start.1
  71.8 10.9 %collective-permute-start = (f32[2,320,128]{2,1,0:T(8,128)S(1)}, f32[2,320,128]{2,1,0:T(8,128)S(1)}, u32[]{:S(2)}, u32[]{:S(2)}) collective-permute-start(f32[2,320,128]{2,1,0:T(8,128)S(1)} %pad_maximum_fusion), channel_id=1, source_target_pairs={{0,1},{1,0},{2,3},{3,2},{4,5},{5,4},{6,7},{7,6},{8,9},{9,8},{10,11... | collective-permute-start | bytes 983048 | tf_op jit(solution)/shard_map/ppermute | solution.py:15
  100.5 1.2 copy-start.5
  101.7 12.0 %copy-start.8 = (f32[1,2,8,2]{2,3,1,0:T(2,128)S(1)}, f32[1,2,8,2]{2,3,1,0:T(2,128)}, u32[]{:S(2)}) copy-start(f32[1,2,8,2]{2,3,1,0:T(2,128)} %param.15) | copy-start | bytes 388
  107.6 20.0 %all-to-all-start.2 = ((bf16[64,2,1120]{2,1,0:T(2,128)(2,1)}), bf16[64,2,1120]{2,1,0:T(2,128)(2,1)S(1)}, u32[]{:S(2)}, u32[]{:S(2)}) async-start(bf16[64,2,1120]{2,1,0:T(2,128)(2,1)} %reshape.166), calls=%async_computation.2 | async-start | bytes 589824 | tf_op jit(solution)/shard_map/all_to_all | solution.py:72
  113.7 72.0 %all-gather.5.cloned.1.call-start = ((), (), s32[]{:S(2)}) async-start(), calls=%async_computation.6 | async-start | bytes 2580480 | tf_op jit(solution)/shard_map/all_gather | solution.py:58
  131.1 1.7 copy-start.4
  131.1 9.8 %copy-start.7 = (f32[1,7168]{1,0:T(1,128)S(1)}, f32[1,7168]{1,0:T(1,128)}, u32[]{:S(2)}) copy-start(f32[1,7168]{1,0:T(1,128)} %param.10) | copy-start | bytes 86020
  132.9 7.9 %collective-permute-start.1 = (bf16[8,7168]{1,0:T(8,128)(2,1)S(1)}, bf16[8,7168]{1,0:T(8,128)(2,1)S(1)}, u32[]{:S(2)}, u32[]{:S(2)}) collective-permute-start(bf16[8,7168]{1,0:T(8,128)(2,1)S(1)} %fusion.19), channel_id=1, source_target_pairs={{0,64},{64,128},{128,192},{192,256},{256,320},{320,384},{384,448},... | collective-permute-start | bytes 344072 | tf_op jit(solution)/shard_map/ppermute | solution.py:15
  185.7 2.6 copy-start.2
  189.0 28.9 %copy-start.6 = (bf16[8,448,128]{2,1,0:T(8,128)(2,1)S(1)}, bf16[8,448,128]{2,1,0:T(8,128)(2,1)}, u32[]{:S(2)}) copy-start(bf16[8,448,128]{2,1,0:T(8,128)(2,1)} %copy-done.5) | copy-start | bytes 2752516
  189.0 11.0 %collective-permute-start.2 = (f32[2,320,128]{2,1,0:T(8,128)S(1)}, f32[2,320,128]{2,1,0:T(8,128)S(1)}, u32[]{:S(2)}, u32[]{:S(2)}) collective-permute-start(f32[2,320,128]{2,1,0:T(8,128)S(1)} %pad_maximum_fusion.1), channel_id=1, source_target_pairs={{0,1},{1,0},{2,3},{3,2},{4,5},{5,4},{6,7},{7,6},{8,9},{9,8},{10,11... | collective-permute-start | bytes 983048 | tf_op jit(solution)/shard_map/ppermute | solution.py:15
  222.8 21.7 %all-to-all-start.4 = ((bf16[64,2,1120]{2,1,0:T(2,128)(2,1)}), bf16[64,2,1120]{2,1,0:T(2,128)(2,1)S(1)}, u32[]{:S(2)}, u32[]{:S(2)}) async-start(bf16[64,2,1120]{2,1,0:T(2,128)(2,1)} %reshape.168), calls=%async_computation.4 | async-start | bytes 589824 | tf_op jit(solution)/shard_map/all_to_all | solution.py:72
Sparse Core Ops, SparseCore 0:
  34.6 33.7 all-gather.2
  155.2 30.4 all-gather.4

commit v5 on v3

--- a/solution.py
+++ b/solution.py
@@ -7,7 +7,7 @@
 from jax.sharding import Mesh
 from jax.sharding import PartitionSpec as P
 
-ALL = ("eg", "q", "dp")
+ALL = ("eg", "qa", "c", "dp")
 
 
 def passed_along(array, axis, by):
@@ -42,7 +42,7 @@
 
 def moe_layer(stream, gain_row, gate_w, up_w, down_mine, routes, mixing):
     experts = lax.axis_size("eg")
-    blocks = lax.axis_size("q")
+    blocks = lax.axis_size("qa") * lax.axis_size("c")
     halves = lax.axis_size("dp")
     tok_rows, model_width = stream.shape
     fan_out = routes.shape[1]
@@ -55,7 +55,8 @@
     send = send.reshape(experts * halves, capacity * tiles, lanes)
     arrived = lax.all_to_all(send, ("eg", "dp"), split_axis=0, concat_axis=0, tiled=True)
     arrived = arrived.reshape(experts * halves, capacity, half).transpose(1, 0, 2)
-    arrived = lax.all_gather(arrived, "q", axis=1, tiled=True)
+    arrived = lax.all_gather(arrived, "qa", axis=1, tiled=True)
+    arrived = lax.all_gather(arrived, "c", axis=1, tiled=True)
     sources = blocks * experts * halves
     rows = arrived.reshape(capacity * sources, half)
     gate_part = jnp.dot(rows, gate_w, preferred_element_type=jnp.float32)
@@ -63,12 +64,14 @@
     mine = jnp.stack([gate_part, up_part])
     both = mine + passed_along(mine, "dp", 1)
     hidden = (jax.nn.silu(both[0]) * both[1]).astype(jnp.bfloat16)
-    hidden_all = lax.all_gather(hidden, "q", axis=1, tiled=True)
+    hidden_all = lax.all_gather(hidden, ("qa", "c"), axis=1, tiled=True)
     out = lax.dot_general(
         hidden_all, down_mine, (((1,), (1,)), ((), ())), preferred_element_type=jnp.float32
     ).astype(jnp.bfloat16)
     piece = out.shape[1]
-    out = out.reshape(capacity, blocks, experts, halves, piece).transpose(2, 1, 3, 0, 4)
+    cores = lax.axis_size("c")
+    out = out.reshape(capacity, cores, blocks // cores, experts, halves, piece)
+    out = out.transpose(3, 2, 1, 4, 0, 5)
     back = lax.all_to_all(
         out.reshape(sources, capacity, piece), ALL, split_axis=0, concat_axis=0, tiled=True
     )
@@ -83,12 +86,12 @@
 def on_device(blocks, gains, w_gate, w_up, w_down, expert_ids, combine):
     stream = blocks[0]
     turns = expert_ids.shape[1]
-    n_blocks = lax.axis_size("q")
+    n_blocks = lax.axis_size("qa") * lax.axis_size("c")
     down_local = w_down[0]
     half, width = down_local.shape
     piece = half // n_blocks
     down_mine = lax.all_to_all(
-        down_local.reshape(n_blocks, piece, width), "q", split_axis=0, concat_axis=0, tiled=True
+        down_local.reshape(n_blocks, piece, width), ("qa", "c"), split_axis=0, concat_axis=0, tiled=True
     )
     down_mine = down_mine.transpose(1, 0, 2).reshape(piece, n_blocks * width)
     for layer_turn in range(turns):
@@ -109,17 +112,18 @@
 def solution(mesh):
     n_section, n_expert, n_dp = (mesh.shape[a] for a in ("section", "expert", "dp"))
     n_q = n_expert // 4
+    n_core = 2
     inner = Mesh(
-        np.asarray(mesh.devices).reshape(n_section, n_expert // n_q, n_q, n_dp),
-        ("section", "eg", "q", "dp"),
+        np.asarray(mesh.devices).reshape(n_section, n_expert // n_q, n_q // n_core, n_core, n_dp),
+        ("section", "eg", "qa", "c", "dp"),
     )
-    tok = ("eg", "q", "dp")
+    tok = ("eg", "qa", "c", "dp")
     in_specs = (
         P("section", tok, None),
         P("section", None),
-        P("section", "dp", ("eg", "q")),
-        P("section", "dp", ("eg", "q")),
-        P("section", "dp", ("eg", "q")),
+        P("section", "dp", ("eg", "qa", "c")),
+        P("section", "dp", ("eg", "qa", "c")),
+        P("section", "dp", ("eg", "qa", "c")),
         P("section", None, tok, None),
         P("section", None, tok, None),
     )

time: 254 us -> 313 us (1.23)
  waiting for transfers between devices: 115 us -> 173 us
    all_gather x2 -> x4, waiting for transfers between devices: 56.9 us -> 115 us  [the longest x2 73.6 us: moe_layer(): arrived = lax.all_gather(arrived, 'qa', axis=1, tiled=True)]
    all_to_all x2, starting transfers between devices: 13.9 us -> 19.6 us  [moe_layer(): lax.all_to_all(out.reshape(sources, capacity, piece), ALL, split_axis=0,...]
    all_to_all x1, starting transfers between devices: 8.24 us -> 5.09 us  [on_device(): lax.all_to_all(down_local.reshape(n_blocks, piece, width), ('qa', 'c'), s...]
  transfers between devices with their start and end apart: 8 -> 10, of which waited for: 7 -> 9; matrix products, arithmetic and copies ran while one was open for 1% -> 1% of each run, Pallas kernels for 0% -> 0%
where the time goes in v5:
time: 313 us; the launch traced here: 312 us
  waiting for transfers between devices  173 us (55%)
  blocking collectives  67.5 us (22%)
  starting transfers between devices  32.3 us (10%)
  between operations  13.5 us (4%)
  local copies, waits for them, and re-layouts  10.8 us (3%)
  matrix products  10.2 us (3%)
  other arithmetic  4.62 us (1%)
    all_gather x2, waiting for transfers between devices, moe_layer(): arrived = lax.all_gather(arrived, 'qa', axis=1, tiled=True)  73.6 us
    all_gather x2, waiting for transfers between devices, moe_layer(): arrived = lax.all_gather(arrived, 'c', axis=1, tiled=True)  41.6 us
    all_to_all x2, waiting for transfers between devices, moe_layer(): lax.all_to_all(out.reshape(sources, capacity, piece), ALL, split_axis=0,...  36 us
    all_to_all x2, blocking collectives, moe_layer(): lax.all_to_all(send, ('eg', 'dp'), split_axis=0, concat_axis=0, tiled=True)  34.7 us
    all_gather x2, blocking collectives, moe_layer(): hidden_all = lax.all_gather(hidden, ('qa', 'c'), axis=1, tiled=True)  32.8 us
    ppermute x3, waiting for transfers between devices, passed_along(): lax.ppermute(array, axis, [(i, (i + by) % length) for i in range(length)])  21.9 us
    all_to_all x2, starting transfers between devices, moe_layer(): lax.all_to_all(out.reshape(sources, capacity, piece), ALL, split_axis=0,...  19.6 us
    ppermute x3, starting transfers between devices, passed_along(): lax.ppermute(array, axis, [(i, (i + by) % length) for i in range(length)])  7.45 us
  transfers between devices with their start and end apart: 10, of which 9 were waited for; matrix products, arithmetic and copies ran while one was open for 1% of the time, Pallas kernels for 0%

profile of v5, /device:TPU:1, one launch (start us, length us, event | category | flops | bytes accessed | tf_op | source)
XLA Modules:
  0.0 312.0 jit_solution(17558430432211738097)
XLA Ops:
  6.5 0.8 fusion.38
  8.3 0.7 bitcast_add_fusion.1
  9.1 1.1 fusion.16
  10.2 1.2 convolution_convert_fusion.1
  11.4 0.2 reshape_reshape.6
  11.9 21.8 %all_to_all.25 = bf16[8,140,128]{2,1,0:T(8,128)(2,1)S(1)} all-to-all(bf16[8,140,128]{2,1,0:T(8,128)(2,1)S(1)} %copy.58), channel_id=1, replica_groups=mesh['section'=8,'eg'=4,'qa'=4,'c'=2,'dp'=2] {'eg','dp'}, dimensions={0} | all-to-all | bytes 573440 | tf_op jit(solution)/shard_map/all_to_all | solution.py:56
  33.7 0.8 copy.59
  34.5 37.3 %all-gather.5.cloned.1.call-done = bf16[5,32,3584]{2,1,0:T(8,128)(2,1)} async-done(((bf16[5,8,3584]{2,1,0:T(8,128)(2,1)}), bf16[5,32,3584]{2,1,0:T(8,128)(2,1)}) %all-gather.5.cloned.1.call-update) | async-done | bytes 1146896 | tf_op jit(solution)/shard_map/all_gather | solution.py:58
  71.9 5.1 %all-to-all-start.1 = ((bf16[8,448,128]{2,1,0:T(8,128)(2,1)}), bf16[8,448,128]{2,1,0:T(8,128)(2,1)S(1)}, u32[]{:S(2)}, u32[]{:S(2)}) async-start(bf16[8,448,128]{2,1,0:T(8,128)(2,1)} %bitcast.16), calls=%async_computation.1 | async-start | bytes 1835008 | tf_op jit(solution)/shard_map/all_to_all | solution.py:93
  77.0 18.3 %all-gather.7.cloned.1.call-done = bf16[5,64,3584]{2,1,0:T(8,128)(2,1)} async-done(((bf16[5,32,3584]{2,1,0:T(8,128)(2,1)}), bf16[5,64,3584]{2,1,0:T(8,128)(2,1)}) %all-gather.7.cloned.1.call-update) | async-done | bytes 2293776 | tf_op jit(solution)/shard_map/all_gather | solution.py:59
  95.3 2.5 convolution_bitcast_fusion.2
  97.9 0.8 convolution_bitcast_fusion.3
  98.7 2.1 collective-permute-start
  100.8 8.8 %collective-permute-done = f32[2,320,128]{2,1,0:T(8,128)S(1)} collective-permute-done((f32[2,320,128]{2,1,0:T(8,128)S(1)}, f32[2,320,128]{2,1,0:T(8,128)S(1)}, u32[]{:S(2)}, u32[]{:S(2)}) %collective-permute-start) | collective-permute-done | bytes 327712 | tf_op jit(solution)/shard_map/ppermute | solution.py:15
  109.7 16.4 %all_gather.20 = bf16[320,1024]{1,0:T(8,128)(2,1)S(1)} all-gather(bf16[320,128]{1,0:T(8,128)(2,1)S(1)} %fusion.23), channel_id=1, replica_groups=mesh['section'=8,'eg'=4,'qa'=4,'c'=2,'dp'=2] {'qa','c'}, dimensions={1}, use_global_device_ids=true | all-gather | bytes 737280 | tf_op jit(solution)/shard_map/all_gather | solution.py:67
  126.1 1.3 convolution_convert_fusion.3
  127.4 1.1 reshape.126
  128.5 1.0 copy.75
  129.5 9.8 %all-to-all-start.2 = ((bf16[64,5,448]{2,1,0:T(8,128)(2,1)}), bf16[64,5,448]{2,1,0:T(8,128)(2,1)S(1)}, u32[]{:S(2)}, u32[]{:S(2)}) async-start(bf16[64,5,448]{2,1,0:T(8,128)(2,1)} %bitcast.19), calls=%async_computation.2 | async-start | bytes 1048576 | tf_op jit(solution)/shard_map/all_to_all | solution.py:75
  139.5 18.0 %all-to-all-done.2 = bf16[64,5,448]{2,1,0:T(8,128)(2,1)S(1)} async-done(((bf16[64,5,448]{2,1,0:T(8,128)(2,1)}), bf16[64,5,448]{2,1,0:T(8,128)(2,1)S(1)}, u32[]{:S(2)}, u32[]{:S(2)}) %all-to-all-start.2) | async-done | bytes 286752 | tf_op jit(solution)/shard_map/all_to_all | solution.py:75
  157.4 0.3 copy.93
  157.8 0.4 reshape.129
  158.2 0.7 gather_fusion
  159.0 0.3 reshape.138
  159.3 0.6 multiply_reduce_fusion.1
  160.0 3.1 collective-permute-start.1
  163.2 4.2 %collective-permute-done.1 = bf16[8,7168]{1,0:T(8,128)(2,1)S(1)} collective-permute-done((bf16[8,7168]{1,0:T(8,128)(2,1)S(1)}, bf16[8,7168]{1,0:T(8,128)(2,1)S(1)}, u32[]{:S(2)}, u32[]{:S(2)}) %collective-permute-start.1) | collective-permute-done | bytes 114720 | tf_op jit(solution)/shard_map/ppermute | solution.py:15
  167.6 0.3 convolution_convert_fusion
  167.9 0.2 reshape_reshape.7
  168.4 12.9 %all_to_all.26 = bf16[8,140,128]{2,1,0:T(8,128)(2,1)S(1)} all-to-all(bf16[8,140,128]{2,1,0:T(8,128)(2,1)S(1)} %copy.69), channel_id=1, replica_groups=mesh['section'=8,'eg'=4,'qa'=4,'c'=2,'dp'=2] {'eg','dp'}, dimensions={0} | all-to-all | bytes 573440 | tf_op jit(solution)/shard_map/all_to_all | solution.py:56
  181.3 0.8 copy.70
  182.2 36.3 %all-gather.9.cloned.1.call-done = bf16[5,32,3584]{2,1,0:T(8,128)(2,1)} async-done(((bf16[5,8,3584]{2,1,0:T(8,128)(2,1)}), bf16[5,32,3584]{2,1,0:T(8,128)(2,1)}) %all-gather.9.cloned.1.call-update) | async-done | bytes 1146896 | tf_op jit(solution)/shard_map/all_gather | solution.py:58
  218.5 23.3 %all-gather.11.cloned.1.call-done = bf16[5,64,3584]{2,1,0:T(8,128)(2,1)} async-done(((bf16[5,32,3584]{2,1,0:T(8,128)(2,1)}), bf16[5,64,3584]{2,1,0:T(8,128)(2,1)}) %all-gather.11.cloned.1.call-update) | async-done | bytes 2293776 | tf_op jit(solution)/shard_map/all_gather | solution.py:59
  241.7 2.5 convolution_bitcast_fusion
  244.3 0.8 convolution_bitcast_fusion.1
  245.1 2.2 collective-permute-start.2
  247.3 8.8 %collective-permute-done.2 = f32[2,320,128]{2,1,0:T(8,128)S(1)} collective-permute-done((f32[2,320,128]{2,1,0:T(8,128)S(1)}, f32[2,320,128]{2,1,0:T(8,128)S(1)}, u32[]{:S(2)}, u32[]{:S(2)}) %collective-permute-start.2) | collective-permute-done | bytes 327712 | tf_op jit(solution)/shard_map/ppermute | solution.py:15
  256.3 16.4 %all_gather.23 = bf16[320,1024]{1,0:T(8,128)(2,1)S(1)} all-gather(bf16[320,128]{1,0:T(8,128)(2,1)S(1)} %fusion.21), channel_id=1, replica_groups=mesh['section'=8,'eg'=4,'qa'=4,'c'=2,'dp'=2] {'qa','c'}, dimensions={1}, use_global_device_ids=true | all-gather | bytes 737280 | tf_op jit(solution)/shard_map/all_gather | solution.py:67
  272.7 0.5 convolution_convert_fusion.2
  273.4 1.0 copy.77
  274.3 9.8 %all-to-all-start.4 = ((bf16[64,5,448]{2,1,0:T(8,128)(2,1)}), bf16[64,5,448]{2,1,0:T(8,128)(2,1)S(1)}, u32[]{:S(2)}, u32[]{:S(2)}) async-start(bf16[64,5,448]{2,1,0:T(8,128)(2,1)} %bitcast.34), calls=%async_computation.4 | async-start | bytes 1048576 | tf_op jit(solution)/shard_map/all_to_all | solution.py:75
  284.3 18.0 %all-to-all-done.4 = bf16[64,5,448]{2,1,0:T(8,128)(2,1)S(1)} async-done(((bf16[64,5,448]{2,1,0:T(8,128)(2,1)}), bf16[64,5,448]{2,1,0:T(8,128)(2,1)S(1)}, u32[]{:S(2)}, u32[]{:S(2)}) %all-to-all-start.4) | async-done | bytes 286752 | tf_op jit(solution)/shard_map/all_to_all | solution.py:75
  302.3 0.3 copy.92
  302.7 0.4 reshape.136
  303.0 0.7 gather_fusion.1
  303.9 0.3 reshape.139
  304.1 0.6 multiply_reduce_fusion
  304.8 0.7 fusion.25
  (67 shorter events, 3.0 us)
Async XLA Ops:
  6.5 88.8 %copy-start = (bf16[1,3584,128]{2,1,0:T(8,128)(2,1)S(1)}, bf16[1,3584,128]{2,1,0:T(8,128)(2,1)}, u32[]{:S(2)}) copy-start(bf16[1,3584,128]{2,1,0:T(8,128)(2,1)} %param.12) | copy-start | bytes 2752516
  6.5 65.3 %all-gather.5.cloned.1.call-start = ((), (), s32[]{:S(2)}) async-start(), calls=%async_computation.5 | async-start | bytes 1433600 | tf_op jit(solution)/shard_map/all_gather | solution.py:58
  34.5 60.8 %all-gather.7.cloned.1.call-start = ((), (), s32[]{:S(2)}) async-start(), calls=%async_computation.6 | async-start | bytes 3440640 | tf_op jit(solution)/shard_map/all_gather | solution.py:59
  71.9 54.2 %all-to-all-start.1 = ((bf16[8,448,128]{2,1,0:T(8,128)(2,1)}), bf16[8,448,128]{2,1,0:T(8,128)(2,1)S(1)}, u32[]{:S(2)}, u32[]{:S(2)}) async-start(bf16[8,448,128]{2,1,0:T(8,128)(2,1)} %bitcast.16), calls=%async_computation.1 | async-start | bytes 1835008 | tf_op jit(solution)/shard_map/all_to_all | solution.py:93
  77.0 20.9 %copy-start.3 = (bf16[1,3584,128]{2,1,0:T(8,128)(2,1)S(1)}, bf16[1,3584,128]{2,1,0:T(8,128)(2,1)}, u32[]{:S(2)}) copy-start(bf16[1,3584,128]{2,1,0:T(8,128)(2,1)} %param.11) | copy-start | bytes 2752516
  95.3 2.6 copy-start.1
  98.7 10.9 %collective-permute-start = (f32[2,320,128]{2,1,0:T(8,128)S(1)}, f32[2,320,128]{2,1,0:T(8,128)S(1)}, u32[]{:S(2)}, u32[]{:S(2)}) collective-permute-start(f32[2,320,128]{2,1,0:T(8,128)S(1)} %pad_maximum_fusion), channel_id=1, source_target_pairs={{0,1},{1,0},{2,3},{3,2},{4,5},{5,4},{6,7},{7,6},{8,9},{9,8},{10,11... | collective-permute-start | bytes 983048 | tf_op jit(solution)/shard_map/ppermute | solution.py:15
  126.1 13.2 %copy-start.8 = (f32[1,2,8,2]{2,3,1,0:T(2,128)S(1)}, f32[1,2,8,2]{2,3,1,0:T(2,128)}, u32[]{:S(2)}) copy-start(f32[1,2,8,2]{2,3,1,0:T(2,128)} %param.15) | copy-start | bytes 388
  126.1 3.4 %copy-start.5 = (bf16[8,448,128]{2,1,0:T(8,128)(2,1)}, bf16[8,448,128]{2,1,0:T(8,128)(2,1)S(1)}, u32[]{:S(2)}) copy-start(bf16[8,448,128]{2,1,0:T(8,128)(2,1)S(1)} %all-to-all-done.1) | copy-start | bytes 2752516
  129.5 27.9 %all-to-all-start.2 = ((bf16[64,5,448]{2,1,0:T(8,128)(2,1)}), bf16[64,5,448]{2,1,0:T(8,128)(2,1)S(1)}, u32[]{:S(2)}, u32[]{:S(2)}) async-start(bf16[64,5,448]{2,1,0:T(8,128)(2,1)} %bitcast.19), calls=%async_computation.2 | async-start | bytes 1048576 | tf_op jit(solution)/shard_map/all_to_all | solution.py:75
  139.3 79.1 %all-gather.9.cloned.1.call-start = ((), (), s32[]{:S(2)}) async-start(), calls=%async_computation.7 | async-start | bytes 1433600 | tf_op jit(solution)/shard_map/all_gather | solution.py:58
  158.2 1.7 copy-start.4
  158.2 9.4 %copy-start.7 = (f32[1,7168]{1,0:T(1,128)S(1)}, f32[1,7168]{1,0:T(1,128)}, u32[]{:S(2)}) copy-start(f32[1,7168]{1,0:T(1,128)} %param.10) | copy-start | bytes 86020
  160.0 7.4 %collective-permute-start.1 = (bf16[8,7168]{1,0:T(8,128)(2,1)S(1)}, bf16[8,7168]{1,0:T(8,128)(2,1)S(1)}, u32[]{:S(2)}, u32[]{:S(2)}) collective-permute-start(bf16[8,7168]{1,0:T(8,128)(2,1)S(1)} %fusion.19), channel_id=1, source_target_pairs={{0,64},{64,128},{128,192},{192,256},{256,320},{320,384},{384,448},... | collective-permute-start | bytes 344072 | tf_op jit(solution)/shard_map/ppermute | solution.py:15
  182.1 59.6 %all-gather.11.cloned.1.call-start = ((), (), s32[]{:S(2)}) async-start(), calls=%async_computation.8 | async-start | bytes 3440640 | tf_op jit(solution)/shard_map/all_gather | solution.py:59
  241.7 2.6 copy-start.2
  245.1 27.6 %copy-start.6 = (bf16[8,448,128]{2,1,0:T(8,128)(2,1)S(1)}, bf16[8,448,128]{2,1,0:T(8,128)(2,1)}, u32[]{:S(2)}) copy-start(bf16[8,448,128]{2,1,0:T(8,128)(2,1)} %copy-done.5) | copy-start | bytes 2752516
  245.1 11.1 %collective-permute-start.2 = (f32[2,320,128]{2,1,0:T(8,128)S(1)}, f32[2,320,128]{2,1,0:T(8,128)S(1)}, u32[]{:S(2)}, u32[]{:S(2)}) collective-permute-start(f32[2,320,128]{2,1,0:T(8,128)S(1)} %pad_maximum_fusion.1), channel_id=1, source_target_pairs={{0,1},{1,0},{2,3},{3,2},{4,5},{5,4},{6,7},{7,6},{8,9},{9,8},{10,11... | collective-permute-start | bytes 983048 | tf_op jit(solution)/shard_map/ppermute | solution.py:15
  274.3 28.0 %all-to-all-start.4 = ((bf16[64,5,448]{2,1,0:T(8,128)(2,1)}), bf16[64,5,448]{2,1,0:T(8,128)(2,1)S(1)}, u32[]{:S(2)}, u32[]{:S(2)}) async-start(bf16[64,5,448]{2,1,0:T(8,128)(2,1)} %bitcast.34), calls=%async_computation.4 | async-start | bytes 1048576 | tf_op jit(solution)/shard_map/all_to_all | solution.py:75
Sparse Core Ops, SparseCore 0:
  34.6 37.2 all-gather.4
  73.9 21.3 all-gather.6
  182.2 36.1 all-gather.8
  220.4 21.3 all-gather.10

commit v6 on v3

--- a/solution.py
+++ b/solution.py
@@ -40,15 +40,12 @@
     return widened, outgoing.reshape(experts, capacity, model_width), target
 
 
-def moe_layer(stream, gain_row, gate_w, up_w, down_mine, routes, mixing):
+def expert_rows(outgoing, gate_w, up_w, down_mine):
     experts = lax.axis_size("eg")
     blocks = lax.axis_size("q")
     halves = lax.axis_size("dp")
-    tok_rows, model_width = stream.shape
-    fan_out = routes.shape[1]
-    capacity = min(tok_rows, max(2, 5 * tok_rows * fan_out // (4 * experts)))
+    _, capacity, model_width = outgoing.shape
     half = model_width // halves
-    widened, outgoing, target = route(stream, gain_row, routes, experts, capacity)
     lanes = 128
     tiles = half // lanes
     send = outgoing.reshape(experts, capacity, halves, tiles, lanes).transpose(0, 2, 1, 3, 4)
@@ -73,7 +70,21 @@
         out.reshape(sources, capacity, piece), ALL, split_axis=0, concat_axis=0, tiled=True
     )
     back = back.reshape(experts, blocks, halves, capacity, piece).transpose(0, 3, 2, 1, 4)
-    expert_out = back.reshape(experts * capacity, model_width)
+    return back.reshape(experts, capacity, model_width)
+
+
+def moe_layer(stream, gain_row, gate_w, up_w, down_mine, routes, mixing):
+    experts = lax.axis_size("eg")
+    tok_rows, model_width = stream.shape
+    fan_out = routes.shape[1]
+    capacity = min(tok_rows, max(2, 5 * tok_rows * fan_out // (4 * experts)))
+    widened, outgoing, target = route(stream, gain_row, routes, experts, capacity)
+    cut = (capacity + 1) // 2
+    parts = [
+        expert_rows(outgoing[:, :cut], gate_w, up_w, down_mine),
+        expert_rows(outgoing[:, cut:], gate_w, up_w, down_mine),
+    ]
+    expert_out = jnp.concatenate(parts, axis=1).reshape(experts * capacity, model_width)
     picked = jnp.take(expert_out, target, axis=0)
     picked = picked.reshape(tok_rows, fan_out, model_width)
     mixed_sum = jnp.sum(mixing[:, :, None] * picked.astype(jnp.float32), axis=1)

time: 254 us -> 303 us (1.19)
  blocking collectives: 70 us -> 169 us
  waiting for transfers between devices: 115 us -> 39.1 us
  starting transfers between devices: 29.7 us -> 50.1 us
    all_gather x2 -> x6, blocking collectives: 35.4 us -> 115 us  [the longest x4 65.8 us: expert_rows(): hidden_all = lax.all_gather(hidden, 'q', axis=1, tiled=True)]
    all_gather x2, waiting for transfers between devices: 56.9 us -> 0.01 us  [expert_rows(): arrived = lax.all_gather(arrived, 'q', axis=1, tiled=True)]
    all_to_all x2 -> x4, blocking collectives: 34.7 us -> 53.9 us  [expert_rows(): lax.all_to_all(send, ('eg', 'dp'), split_axis=0, concat_axis=0, tiled=True)]
    all_to_all x2 -> x4, starting transfers between devices: 13.9 us -> 29.3 us  [expert_rows(): lax.all_to_all(out.reshape(sources, capacity, piece), ALL, split_axis=0,...]
    all_to_all x2 -> x4, waiting for transfers between devices: 36 us -> 26.2 us  [expert_rows(): lax.all_to_all(out.reshape(sources, capacity, piece), ALL, split_axis=0,...]
    ppermute x3 -> x5, waiting for transfers between devices: 21.7 us -> 12.9 us  [passed_along(): lax.ppermute(array, axis, [(i, (i + by) % length) for i in range(length)])]
    ppermute x3 -> x5, starting transfers between devices: 7.5 us -> 13.8 us  [passed_along(): lax.ppermute(array, axis, [(i, (i + by) % length) for i in range(length)])]
    transpose x4 -> x12, local copies, waits for them, and re-layouts: 0.52 us -> 3.56 us  [the longest x2 1.6 us: expert_rows(): out.reshape(capacity, blocks, experts, halves, piece)]
  transfers between devices with their start and end apart: 8 -> 12, of which waited for: 7 -> 5; matrix products, arithmetic and copies ran while one was open for 1% -> 4% of each run, Pallas kernels for 0% -> 0%
where the time goes in v6:
time: 303 us; the launch traced here: 302 us
  blocking collectives  169 us (56%)
  starting transfers between devices  50.1 us (17%)
  waiting for transfers between devices  39.1 us (13%)
  between operations  14.2 us (5%)
  local copies, waits for them, and re-layouts  13.6 us (4%)
  matrix products  10 us (3%)
  other arithmetic  6.01 us (2%)
    all_gather x4, blocking collectives, expert_rows(): hidden_all = lax.all_gather(hidden, 'q', axis=1, tiled=True)  65.8 us
    all_to_all x4, blocking collectives, expert_rows(): lax.all_to_all(send, ('eg', 'dp'), split_axis=0, concat_axis=0, tiled=True)  53.9 us
    all_gather x2, blocking collectives, expert_rows(): arrived = lax.all_gather(arrived, 'q', axis=1, tiled=True)  49 us
    all_to_all x4, starting transfers between devices, expert_rows(): lax.all_to_all(out.reshape(sources, capacity, piece), ALL, split_axis=0,...  29.3 us
    all_to_all x4, waiting for transfers between devices, expert_rows(): lax.all_to_all(out.reshape(sources, capacity, piece), ALL, split_axis=0,...  26.2 us
    ppermute x5, starting transfers between devices, passed_along(): lax.ppermute(array, axis, [(i, (i + by) % length) for i in range(length)])  13.8 us
    ppermute x5, waiting for transfers between devices, passed_along(): lax.ppermute(array, axis, [(i, (i + by) % length) for i in range(length)])  12.9 us
    all_to_all x1, starting transfers between devices, on_device(): lax.all_to_all(down_local.reshape(n_blocks, piece, width), 'q', split_axi...  6.9 us
  transfers between devices with their start and end apart: 12, of which 5 were waited for; matrix products, arithmetic and copies ran while one was open for 4% of the time, Pallas kernels for 0%

profile of v6, /device:TPU:1, one launch (start us, length us, event | category | flops | bytes accessed | tf_op | source)
XLA Modules:
  0.0 301.6 jit_solution(14203075975411045662)
XLA Ops:
  6.5 1.1 fusion.24
  7.7 0.7 fusion.52
  9.4 0.7 bitcast_add_fusion.1
  10.2 1.2 convolution_convert_fusion.1
  12.0 19.4 %all_to_all.45 = bf16[8,84,128]{2,1,0:T(8,128)(2,1)S(1)} all-to-all(bf16[8,84,128]{2,1,0:T(8,128)(2,1)S(1)} %copy.167), channel_id=1, replica_groups=mesh['section'=8,'eg'=4,'q'=8,'dp'=2] {'eg','dp'}, dimensions={0} | all-to-all | bytes 344064 | tf_op jit(solution)/shard_map/all_to_all | solution.py:53
  31.5 0.7 copy.168
  32.5 12.4 %all_to_all.46 = bf16[8,56,128]{2,1,0:T(8,128)(2,1)S(1)} all-to-all(bf16[8,56,128]{2,1,0:T(8,128)(2,1)S(1)} %copy.175), channel_id=1, replica_groups=mesh['section'=8,'eg'=4,'q'=8,'dp'=2] {'eg','dp'}, dimensions={0} | all-to-all | bytes 229376 | tf_op jit(solution)/shard_map/all_to_all | solution.py:53
  44.9 6.9 %all-to-all-start.1 = ((bf16[8,448,128]{2,1,0:T(8,128)(2,1)}), bf16[8,448,128]{2,1,0:T(8,128)(2,1)S(1)}, u32[]{:S(2)}, u32[]{:S(2)}) async-start(bf16[8,448,128]{2,1,0:T(8,128)(2,1)} %bitcast.16), calls=%async_computation.1 | async-start | bytes 1835008 | tf_op jit(solution)/shard_map/all_to_all | solution.py:101
  51.9 28.1 %all_gather.26 = bf16[2,64,3584]{2,0,1:T(2,128)(2,1)S(1)} all-gather(bf16[2,8,3584]{2,0,1:T(2,128)(2,1)S(1)} %bitcast.221), channel_id=1, replica_groups=mesh['section'=8,'eg'=4,'q'=8,'dp'=2] {'q'}, dimensions={1}, use_global_device_ids=true | all-gather | bytes 1032192 | tf_op jit(solution)/shard_map/all_gather | solution.py:55
  80.5 0.8 copy-done.1
  81.7 2.4 collective-permute-start.1
  84.0 4.4 %collective-permute-done.1 = f32[2,128,128]{2,1,0:T(8,128)S(1)} collective-permute-done((f32[2,128,128]{2,1,0:T(8,128)S(1)}, f32[2,128,128]{2,1,0:T(8,128)S(1)}, u32[]{:S(2)}, u32[]{:S(2)}) %collective-permute-start.1) | collective-permute-done | bytes 131104 | tf_op jit(solution)/shard_map/ppermute | solution.py:15
  88.5 15.9 %all_gather.27 = bf16[128,1024]{1,0:T(8,128)(2,1)S(1)} all-gather(bf16[128,128]{1,0:T(8,128)(2,1)S(1)} %fusion.43), channel_id=1, replica_groups=mesh['section'=8,'eg'=4,'q'=8,'dp'=2] {'q'}, dimensions={1}, use_global_device_ids=true | all-gather | bytes 294912 | tf_op jit(solution)/shard_map/all_gather | solution.py:63
  104.4 2.0 convolution_bitcast_fusion.2
  106.4 0.5 convolution_bitcast_fusion.3
  106.9 2.4 collective-permute-start
  109.9 0.8 copy.178
  110.7 8.3 %all-to-all-start.4 = ((bf16[64,2,448]{2,1,0:T(2,128)(2,1)}), bf16[64,2,448]{2,1,0:T(2,128)(2,1)S(1)}, u32[]{:S(2)}, u32[]{:S(2)}) async-start(bf16[64,2,448]{2,1,0:T(2,128)(2,1)} %bitcast.31), calls=%async_computation.4 | async-start | bytes 262144 | tf_op jit(solution)/shard_map/all_to_all | solution.py:69
  119.1 0.9 fusion.51
  120.1 16.9 %all_gather.25 = bf16[192,1024]{1,0:T(8,128)(2,1)S(1)} all-gather(bf16[192,128]{1,0:T(8,128)(2,1)S(1)} %fusion.39), channel_id=1, replica_groups=mesh['section'=8,'eg'=4,'q'=8,'dp'=2] {'q'}, dimensions={1}, use_global_device_ids=true | all-gather | bytes 442368 | tf_op jit(solution)/shard_map/all_gather | solution.py:63
  137.0 0.4 convolution_convert_fusion.3
  137.5 0.9 copy.201
  138.4 8.3 %all-to-all-start.2 = ((bf16[64,3,448]{2,1,0:T(4,128)(2,1)}), bf16[64,3,448]{2,1,0:T(4,128)(2,1)S(1)}, u32[]{:S(2)}, u32[]{:S(2)}) async-start(bf16[64,3,448]{2,1,0:T(4,128)(2,1)} %bitcast.19), calls=%async_computation.2 | async-start | bytes 524288 | tf_op jit(solution)/shard_map/all_to_all | solution.py:69
  147.1 13.0 %all-to-all-done.2 = bf16[64,3,448]{2,1,0:T(4,128)(2,1)S(1)} async-done(((bf16[64,3,448]{2,1,0:T(4,128)(2,1)}), bf16[64,3,448]{2,1,0:T(4,128)(2,1)S(1)}, u32[]{:S(2)}, u32[]{:S(2)}) %all-to-all-start.2) | async-done | bytes 172064 | tf_op jit(solution)/shard_map/all_to_all | solution.py:69
  161.1 0.7 gather_fusion
  162.2 0.6 multiply_reduce_fusion.1
  162.9 3.2 %collective-permute-start.2 = (bf16[8,7168]{1,0:T(8,128)(2,1)S(1)}, bf16[8,7168]{1,0:T(8,128)(2,1)S(1)}, u32[]{:S(2)}, u32[]{:S(2)}) collective-permute-start(bf16[8,7168]{1,0:T(8,128)(2,1)S(1)} %fusion.27), channel_id=1, source_target_pairs={{0,64},{64,128},{128,192},{192,256},{256,320},{320,384},{384,448},... | collective-permute-start | bytes 344072 | tf_op jit(solution)/shard_map/ppermute | solution.py:15
  166.2 4.7 %collective-permute-done.2 = bf16[8,7168]{1,0:T(8,128)(2,1)S(1)} collective-permute-done((bf16[8,7168]{1,0:T(8,128)(2,1)S(1)}, bf16[8,7168]{1,0:T(8,128)(2,1)S(1)}, u32[]{:S(2)}, u32[]{:S(2)}) %collective-permute-start.2) | collective-permute-done | bytes 114720 | tf_op jit(solution)/shard_map/ppermute | solution.py:15
  172.1 10.4 %all_to_all.47 = bf16[8,84,128]{2,1,0:T(8,128)(2,1)S(1)} all-to-all(bf16[8,84,128]{2,1,0:T(8,128)(2,1)S(1)} %copy.186), channel_id=1, replica_groups=mesh['section'=8,'eg'=4,'q'=8,'dp'=2] {'eg','dp'}, dimensions={0} | all-to-all | bytes 344064 | tf_op jit(solution)/shard_map/all_to_all | solution.py:53
  182.5 0.7 copy.187
  183.6 11.8 %all_to_all.48 = bf16[8,56,128]{2,1,0:T(8,128)(2,1)S(1)} all-to-all(bf16[8,56,128]{2,1,0:T(8,128)(2,1)S(1)} %copy.193), channel_id=1, replica_groups=mesh['section'=8,'eg'=4,'q'=8,'dp'=2] {'eg','dp'}, dimensions={0} | all-to-all | bytes 229376 | tf_op jit(solution)/shard_map/all_to_all | solution.py:53
  195.4 20.8 %all_gather.30 = bf16[2,64,3584]{2,0,1:T(2,128)(2,1)S(1)} all-gather(bf16[2,8,3584]{2,0,1:T(2,128)(2,1)S(1)} %bitcast.222), channel_id=1, replica_groups=mesh['section'=8,'eg'=4,'q'=8,'dp'=2] {'q'}, dimensions={1}, use_global_device_ids=true | all-gather | bytes 1032192 | tf_op jit(solution)/shard_map/all_gather | solution.py:55
  217.2 3.0 collective-permute-start.4
  220.2 3.8 %collective-permute-done.4 = f32[2,128,128]{2,1,0:T(8,128)S(1)} collective-permute-done((f32[2,128,128]{2,1,0:T(8,128)S(1)}, f32[2,128,128]{2,1,0:T(8,128)S(1)}, u32[]{:S(2)}, u32[]{:S(2)}) %collective-permute-start.4) | collective-permute-done | bytes 131104 | tf_op jit(solution)/shard_map/ppermute | solution.py:15
  224.0 15.9 %all_gather.31 = bf16[128,1024]{1,0:T(8,128)(2,1)S(1)} all-gather(bf16[128,128]{1,0:T(8,128)(2,1)S(1)} %fusion.41), channel_id=1, replica_groups=mesh['section'=8,'eg'=4,'q'=8,'dp'=2] {'q'}, dimensions={1}, use_global_device_ids=true | all-gather | bytes 294912 | tf_op jit(solution)/shard_map/all_gather | solution.py:63
  239.9 2.0 convolution_bitcast_fusion
  241.9 0.5 convolution_bitcast_fusion.1
  242.5 2.9 collective-permute-start.3
  246.0 0.8 copy.196
  246.8 4.5 %all-to-all-start.8 = ((bf16[64,2,448]{2,1,0:T(2,128)(2,1)}), bf16[64,2,448]{2,1,0:T(2,128)(2,1)S(1)}, u32[]{:S(2)}, u32[]{:S(2)}) async-start(bf16[64,2,448]{2,1,0:T(2,128)(2,1)} %bitcast.58), calls=%async_computation.8 | async-start | bytes 262144 | tf_op jit(solution)/shard_map/all_to_all | solution.py:69
  251.4 17.1 %all_gather.29 = bf16[192,1024]{1,0:T(8,128)(2,1)S(1)} all-gather(bf16[192,128]{1,0:T(8,128)(2,1)S(1)} %fusion.37), channel_id=1, replica_groups=mesh['section'=8,'eg'=4,'q'=8,'dp'=2] {'q'}, dimensions={1}, use_global_device_ids=true | all-gather | bytes 442368 | tf_op jit(solution)/shard_map/all_gather | solution.py:63
  268.5 0.4 convolution_convert_fusion.2
  269.1 0.9 copy.205
  269.9 8.1 %all-to-all-start.6 = ((bf16[64,3,448]{2,1,0:T(4,128)(2,1)}), bf16[64,3,448]{2,1,0:T(4,128)(2,1)S(1)}, u32[]{:S(2)}, u32[]{:S(2)}) async-start(bf16[64,3,448]{2,1,0:T(4,128)(2,1)} %bitcast.46), calls=%async_computation.6 | async-start | bytes 524288 | tf_op jit(solution)/shard_map/all_to_all | solution.py:69
  278.4 13.1 %all-to-all-done.6 = bf16[64,3,448]{2,1,0:T(4,128)(2,1)S(1)} async-done(((bf16[64,3,448]{2,1,0:T(4,128)(2,1)}), bf16[64,3,448]{2,1,0:T(4,128)(2,1)S(1)}, u32[]{:S(2)}, u32[]{:S(2)}) %all-to-all-start.6) | async-done | bytes 172064 | tf_op jit(solution)/shard_map/all_to_all | solution.py:69
  292.4 0.7 gather_fusion.1
  293.5 0.6 multiply_reduce_fusion
  294.1 0.7 fusion.29
  (123 shorter events, 10.3 us)
Async XLA Ops:
  6.5 73.6 %copy-start = (bf16[1,3584,128]{2,1,0:T(8,128)(2,1)S(1)}, bf16[1,3584,128]{2,1,0:T(8,128)(2,1)}, u32[]{:S(2)}) copy-start(bf16[1,3584,128]{2,1,0:T(8,128)(2,1)} %param.12) | copy-start | bytes 2752516
  6.5 97.9 %all-gather.3.cloned.1.call-start = ((), (), s32[]{:S(2)}) async-start(), calls=%async_computation.9 | async-start | bytes 1548288 | tf_op jit(solution)/shard_map/all_gather | solution.py:55
  44.9 64.4 %all-to-all-start.1 = ((bf16[8,448,128]{2,1,0:T(8,128)(2,1)}), bf16[8,448,128]{2,1,0:T(8,128)(2,1)S(1)}, u32[]{:S(2)}, u32[]{:S(2)}) async-start(bf16[8,448,128]{2,1,0:T(8,128)(2,1)} %bitcast.16), calls=%async_computation.1 | async-start | bytes 1835008 | tf_op jit(solution)/shard_map/all_to_all | solution.py:101
  80.1 1.2 copy-start.1
  81.7 6.8 %collective-permute-start.1 = (f32[2,128,128]{2,1,0:T(8,128)S(1)}, f32[2,128,128]{2,1,0:T(8,128)S(1)}, u32[]{:S(2)}, u32[]{:S(2)}) collective-permute-start(f32[2,128,128]{2,1,0:T(8,128)S(1)} %pad_maximum_fusion.4), channel_id=1, source_target_pairs={{0,1},{1,0},{2,3},{3,2},{4,5},{5,4},{6,7},{7,6},{8,9},{9,8},{10,11... | collective-permute-start | bytes 393224 | tf_op jit(solution)/shard_map/ppermute | solution.py:15
  104.4 2.0 copy-start.2
  106.9 12.2 %collective-permute-start = (f32[2,192,128]{2,1,0:T(8,128)S(1)}, f32[2,192,128]{2,1,0:T(8,128)}, u32[]{:S(2)}, u32[]{:S(2)}) collective-permute-start(f32[2,192,128]{2,1,0:T(8,128)S(1)} %pad_maximum_fusion.2), channel_id=1, source_target_pairs={{0,1},{1,0},{2,3},{3,2},{4,5},{5,4},{6,7},{7,6},{8,9},{9,8},{10,11... | collective-permute-start | bytes 589832 | tf_op jit(solution)/shard_map/ppermute | solution.py:15
  109.3 27.6 %copy-start.5 = (bf16[8,448,128]{2,1,0:T(8,128)(2,1)}, bf16[8,448,128]{2,1,0:T(8,128)(2,1)S(1)}, u32[]{:S(2)}) copy-start(bf16[8,448,128]{2,1,0:T(8,128)(2,1)S(1)} %all-to-all-done.1) | copy-start | bytes 2752516
  110.7 27.7 %all-to-all-start.4 = ((bf16[64,2,448]{2,1,0:T(2,128)(2,1)}), bf16[64,2,448]{2,1,0:T(2,128)(2,1)S(1)}, u32[]{:S(2)}, u32[]{:S(2)}) async-start(bf16[64,2,448]{2,1,0:T(2,128)(2,1)} %bitcast.31), calls=%async_computation.4 | async-start | bytes 262144 | tf_op jit(solution)/shard_map/all_to_all | solution.py:69
  137.0 9.8 %copy-start.9 = (f32[1,2,8,2]{2,3,1,0:T(2,128)S(1)}, f32[1,2,8,2]{2,3,1,0:T(2,128)}, u32[]{:S(2)}) copy-start(f32[1,2,8,2]{2,3,1,0:T(2,128)} %param.15) | copy-start | bytes 388
  138.4 21.8 %all-to-all-start.2 = ((bf16[64,3,448]{2,1,0:T(4,128)(2,1)}), bf16[64,3,448]{2,1,0:T(4,128)(2,1)S(1)}, u32[]{:S(2)}, u32[]{:S(2)}) async-start(bf16[64,3,448]{2,1,0:T(4,128)(2,1)} %bitcast.19), calls=%async_computation.2 | async-start | bytes 524288 | tf_op jit(solution)/shard_map/all_to_all | solution.py:69
  146.7 93.2 %all-gather.5.cloned.1.call-start = ((), (), s32[]{:S(2)}) async-start(), calls=%async_computation.10 | async-start | bytes 1548288 | tf_op jit(solution)/shard_map/all_gather | solution.py:55
  161.8 1.1 copy-start.4
  161.8 9.3 %copy-start.8 = (f32[1,7168]{1,0:T(1,128)S(1)}, f32[1,7168]{1,0:T(1,128)}, u32[]{:S(2)}) copy-start(f32[1,7168]{1,0:T(1,128)} %param.10) | copy-start | bytes 86020
  162.9 8.0 %collective-permute-start.2 = (bf16[8,7168]{1,0:T(8,128)(2,1)S(1)}, bf16[8,7168]{1,0:T(8,128)(2,1)S(1)}, u32[]{:S(2)}, u32[]{:S(2)}) collective-permute-start(bf16[8,7168]{1,0:T(8,128)(2,1)S(1)} %fusion.27), channel_id=1, source_target_pairs={{0,64},{64,128},{128,192},{192,256},{256,320},{320,384},{384,448},... | collective-permute-start | bytes 344072 | tf_op jit(solution)/shard_map/ppermute | solution.py:15
  217.2 6.8 %collective-permute-start.4 = (f32[2,128,128]{2,1,0:T(8,128)S(1)}, f32[2,128,128]{2,1,0:T(8,128)S(1)}, u32[]{:S(2)}, u32[]{:S(2)}) collective-permute-start(f32[2,128,128]{2,1,0:T(8,128)S(1)} %pad_maximum_fusion.5), channel_id=1, source_target_pairs={{0,1},{1,0},{2,3},{3,2},{4,5},{5,4},{6,7},{7,6},{8,9},{9,8},{10,11... | collective-permute-start | bytes 393224 | tf_op jit(solution)/shard_map/ppermute | solution.py:15
  239.9 2.0 copy-start.3
  241.9 3.5 %copy-start.6 = (bf16[8,448,128]{2,1,0:T(8,128)(2,1)S(1)}, bf16[8,448,128]{2,1,0:T(8,128)(2,1)}, u32[]{:S(2)}) copy-start(bf16[8,448,128]{2,1,0:T(8,128)(2,1)} %copy-done.5) | copy-start | bytes 2752516
  242.5 8.8 %collective-permute-start.3 = (f32[2,192,128]{2,1,0:T(8,128)S(1)}, f32[2,192,128]{2,1,0:T(8,128)S(1)}, u32[]{:S(2)}, u32[]{:S(2)}) collective-permute-start(f32[2,192,128]{2,1,0:T(8,128)S(1)} %pad_maximum_fusion.3), channel_id=1, source_target_pairs={{0,1},{1,0},{2,3},{3,2},{4,5},{5,4},{6,7},{7,6},{8,9},{9,8},{10,11... | collective-permute-start | bytes 589832 | tf_op jit(solution)/shard_map/ppermute | solution.py:15
  245.8 22.7 %copy-start.7 = (bf16[8,448,128]{2,1,0:T(8,128)(2,1)S(1)}, bf16[8,448,128]{2,1,0:T(8,128)(2,1)}, u32[]{:S(2)}) copy-start(bf16[8,448,128]{2,1,0:T(8,128)(2,1)} %copy-done.5) | copy-start | bytes 2752516
  246.8 23.2 %all-to-all-start.8 = ((bf16[64,2,448]{2,1,0:T(2,128)(2,1)}), bf16[64,2,448]{2,1,0:T(2,128)(2,1)S(1)}, u32[]{:S(2)}, u32[]{:S(2)}) async-start(bf16[64,2,448]{2,1,0:T(2,128)(2,1)} %bitcast.58), calls=%async_computation.8 | async-start | bytes 262144 | tf_op jit(solution)/shard_map/all_to_all | solution.py:69
  269.9 21.5 %all-to-all-start.6 = ((bf16[64,3,448]{2,1,0:T(4,128)(2,1)}), bf16[64,3,448]{2,1,0:T(4,128)(2,1)S(1)}, u32[]{:S(2)}, u32[]{:S(2)}) async-start(bf16[64,3,448]{2,1,0:T(4,128)(2,1)} %bitcast.46), calls=%async_computation.6 | async-start | bytes 524288 | tf_op jit(solution)/shard_map/all_to_all | solution.py:69
Sparse Core Ops, SparseCore 0:
  32.3 36.3 all-gather.2
  183.4 30.9 all-gather.4

commit v7 on v3

--- a/solution.py
+++ b/solution.py
@@ -61,9 +61,16 @@
     gate_part = jnp.dot(rows, gate_w, preferred_element_type=jnp.float32)
     up_part = jnp.dot(rows, up_w, preferred_element_type=jnp.float32)
     mine = jnp.stack([gate_part, up_part])
-    both = mine + passed_along(mine, "dp", 1)
+    share = mine.shape[1] // halves
+    side = lax.axis_index("dp")
+    keep = lax.dynamic_slice_in_dim(mine, side * share, share, axis=1)
+    give = lax.dynamic_slice_in_dim(mine, (1 - side) * share, share, axis=1)
+    both = keep + passed_along(give, "dp", 1)
     hidden = (jax.nn.silu(both[0]) * both[1]).astype(jnp.bfloat16)
-    hidden_all = lax.all_gather(hidden, "q", axis=1, tiled=True)
+    units = hidden.shape[1]
+    hidden_all = lax.all_gather(hidden, ("q", "dp"), axis=0, tiled=False)
+    hidden_all = hidden_all.reshape(blocks, halves, share, units).transpose(1, 2, 0, 3)
+    hidden_all = hidden_all.reshape(halves * share, blocks * units)
     out = lax.dot_general(
         hidden_all, down_mine, (((1,), (1,)), ((), ())), preferred_element_type=jnp.float32
     ).astype(jnp.bfloat16)

time: 254 us -> 278 us (1.094)
  blocking collectives: 70 us -> 94.6 us
  waiting for transfers between devices: 115 us -> 108 us
  starting transfers between devices: 29.7 us -> 34.7 us
    all_gather x2, blocking collectives: 35.4 us -> 59.9 us  [moe_layer(): hidden_all = lax.all_gather(hidden, ('q', 'dp'), axis=0, tiled=False)]
    ppermute x3, waiting for transfers between devices: 21.7 us -> 14.7 us  [passed_along(): lax.ppermute(array, axis, [(i, (i + by) % length) for i in range(length)])]
    all_to_all x2, starting transfers between devices: 13.9 us -> 18.9 us  [moe_layer(): lax.all_to_all(out.reshape(sources, capacity, piece), ALL, split_axis=0,...]
where the time goes in v7:
time: 278 us; the launch traced here: 277 us
  waiting for transfers between devices  108 us (39%)
  blocking collectives  94.6 us (34%)
  starting transfers between devices  34.7 us (12%)
  between operations  13.8 us (5%)
  local copies, waits for them, and re-layouts  11.6 us (4%)
  matrix products  10.2 us (4%)
  other arithmetic  4.49 us (2%)
    all_gather x2, blocking collectives, moe_layer(): hidden_all = lax.all_gather(hidden, ('q', 'dp'), axis=0, tiled=False)  59.9 us
    all_gather x2, waiting for transfers between devices, moe_layer(): arrived = lax.all_gather(arrived, 'q', axis=1, tiled=True)  56.9 us
    all_to_all x2, waiting for transfers between devices, moe_layer(): lax.all_to_all(out.reshape(sources, capacity, piece), ALL, split_axis=0,...  36 us
    all_to_all x2, blocking collectives, moe_layer(): lax.all_to_all(send, ('eg', 'dp'), split_axis=0, concat_axis=0, tiled=True)  34.7 us
    all_to_all x2, starting transfers between devices, moe_layer(): lax.all_to_all(out.reshape(sources, capacity, piece), ALL, split_axis=0,...  18.9 us
    ppermute x3, waiting for transfers between devices, passed_along(): lax.ppermute(array, axis, [(i, (i + by) % length) for i in range(length)])  14.7 us
    all_to_all x1, starting transfers between devices, on_device(): lax.all_to_all(down_local.reshape(n_blocks, piece, width), 'q', split_axi...  8.24 us
    ppermute x3, starting transfers between devices, passed_along(): lax.ppermute(array, axis, [(i, (i + by) % length) for i in range(length)])  7.5 us
  transfers between devices with their start and end apart: 8, of which 7 were waited for; matrix products, arithmetic and copies ran while one was open for 1% of the time, Pallas kernels for 0%

profile of v7, /device:TPU:1, one launch (start us, length us, event | category | flops | bytes accessed | tf_op | source)
XLA Modules:
  0.0 277.1 jit_solution(16902286631560705264)
XLA Ops:
  6.5 0.8 fusion.44
  8.3 0.7 bitcast_add_fusion.1
  9.1 1.1 fusion.20
  10.2 1.2 convolution_convert_fusion.1
  11.4 0.2 reshape_reshape.6
  11.9 21.8 %all_to_all.25 = bf16[8,140,128]{2,1,0:T(8,128)(2,1)S(1)} all-to-all(bf16[8,140,128]{2,1,0:T(8,128)(2,1)S(1)} %copy.62), channel_id=1, replica_groups=mesh['section'=8,'eg'=4,'q'=8,'dp'=2] {'eg','dp'}, dimensions={0} | all-to-all | bytes 573440 | tf_op jit(solution)/shard_map/all_to_all | solution.py:56
  33.7 0.8 copy.63
  34.5 8.2 %all-to-all-start.1 = ((bf16[8,448,128]{2,1,0:T(8,128)(2,1)}), bf16[8,448,128]{2,1,0:T(8,128)(2,1)S(1)}, u32[]{:S(2)}, u32[]{:S(2)}) async-start(bf16[8,448,128]{2,1,0:T(8,128)(2,1)} %bitcast.16), calls=%async_computation.1 | async-start | bytes 1835008 | tf_op jit(solution)/shard_map/all_to_all | solution.py:97
  42.7 25.7 %all-gather.3.cloned.1.call-done = bf16[5,64,3584]{2,1,0:T(8,128)(2,1)} async-done(((bf16[5,8,3584]{2,1,0:T(8,128)(2,1)}), bf16[5,64,3584]{2,1,0:T(8,128)(2,1)}) %all-gather.3.cloned.1.call-update) | async-done | bytes 2293776 | tf_op jit(solution)/shard_map/all_gather | solution.py:58
  68.5 2.5 convolution_bitcast_fusion.2
  71.0 0.8 convolution_bitcast_fusion.3
  71.8 2.1 collective-permute-start
  73.9 5.3 %collective-permute-done = f32[2,160,128]{2,1,0:T(8,128)S(1)} collective-permute-done((f32[2,160,128]{2,1,0:T(8,128)S(1)}, f32[2,160,128]{2,1,0:T(8,128)S(1)}, u32[]{:S(2)}, u32[]{:S(2)}) %collective-permute-start) | collective-permute-done | bytes 163872 | tf_op jit(solution)/shard_map/ppermute | solution.py:15
  79.3 30.0 %all_gather.15 = bf16[16,160,128]{2,1,0:T(8,128)(2,1)S(1)} all-gather(bf16[1,160,128]{2,1,0:T(8,128)(2,1)S(1)} %fusion.39), channel_id=1, replica_groups=mesh['section'=8,'eg'=4,'q'=8,'dp'=2] {'q','dp'}, dimensions={0}, use_global_device_ids=true | all-gather | bytes 696320 | tf_op jit(solution)/shard_map/all_gather | solution.py:71
  109.3 0.4 copy.64
  109.7 1.2 convolution_convert_fusion.3
  111.0 1.1 reshape.140
  112.1 1.0 copy.81
  113.1 8.5 %all-to-all-start.2 = ((bf16[64,5,448]{2,1,0:T(8,128)(2,1)}), bf16[64,5,448]{2,1,0:T(8,128)(2,1)S(1)}, u32[]{:S(2)}, u32[]{:S(2)}) async-start(bf16[64,5,448]{2,1,0:T(8,128)(2,1)} %bitcast.19), calls=%async_computation.2 | async-start | bytes 1048576 | tf_op jit(solution)/shard_map/all_to_all | solution.py:79
  121.8 18.0 %all-to-all-done.2 = bf16[64,5,448]{2,1,0:T(8,128)(2,1)S(1)} async-done(((bf16[64,5,448]{2,1,0:T(8,128)(2,1)}), bf16[64,5,448]{2,1,0:T(8,128)(2,1)S(1)}, u32[]{:S(2)}, u32[]{:S(2)}) %all-to-all-start.2) | async-done | bytes 286752 | tf_op jit(solution)/shard_map/all_to_all | solution.py:79
  139.8 0.3 copy.109
  140.1 0.4 reshape.143
  140.5 0.7 gather_fusion
  141.4 0.3 reshape.154
  141.6 0.6 multiply_reduce_fusion.1
  142.3 3.1 %collective-permute-start.1 = (bf16[8,7168]{1,0:T(8,128)(2,1)S(1)}, bf16[8,7168]{1,0:T(8,128)(2,1)S(1)}, u32[]{:S(2)}, u32[]{:S(2)}) collective-permute-start(bf16[8,7168]{1,0:T(8,128)(2,1)S(1)} %fusion.23), channel_id=1, source_target_pairs={{0,64},{64,128},{128,192},{192,256},{256,320},{320,384},{384,448},... | collective-permute-start | bytes 344072 | tf_op jit(solution)/shard_map/ppermute | solution.py:15
  145.5 4.2 %collective-permute-done.1 = bf16[8,7168]{1,0:T(8,128)(2,1)S(1)} collective-permute-done((bf16[8,7168]{1,0:T(8,128)(2,1)S(1)}, bf16[8,7168]{1,0:T(8,128)(2,1)S(1)}, u32[]{:S(2)}, u32[]{:S(2)}) %collective-permute-start.1) | collective-permute-done | bytes 114720 | tf_op jit(solution)/shard_map/ppermute | solution.py:15
  149.9 0.3 convolution_convert_fusion
  150.2 0.2 reshape_reshape.7
  150.8 12.9 %all_to_all.26 = bf16[8,140,128]{2,1,0:T(8,128)(2,1)S(1)} all-to-all(bf16[8,140,128]{2,1,0:T(8,128)(2,1)S(1)} %copy.74), channel_id=1, replica_groups=mesh['section'=8,'eg'=4,'q'=8,'dp'=2] {'eg','dp'}, dimensions={0} | all-to-all | bytes 573440 | tf_op jit(solution)/shard_map/all_to_all | solution.py:56
  163.7 0.8 copy.75
  164.5 31.2 %all-gather.5.cloned.1.call-done = bf16[5,64,3584]{2,1,0:T(8,128)(2,1)} async-done(((bf16[5,8,3584]{2,1,0:T(8,128)(2,1)}), bf16[5,64,3584]{2,1,0:T(8,128)(2,1)}) %all-gather.5.cloned.1.call-update) | async-done | bytes 2293776 | tf_op jit(solution)/shard_map/all_gather | solution.py:58
  195.6 2.5 convolution_bitcast_fusion
  198.2 0.8 convolution_bitcast_fusion.1
  199.0 2.3 collective-permute-start.2
  201.3 5.2 %collective-permute-done.2 = f32[2,160,128]{2,1,0:T(8,128)S(1)} collective-permute-done((f32[2,160,128]{2,1,0:T(8,128)S(1)}, f32[2,160,128]{2,1,0:T(8,128)S(1)}, u32[]{:S(2)}, u32[]{:S(2)}) %collective-permute-start.2) | collective-permute-done | bytes 163872 | tf_op jit(solution)/shard_map/ppermute | solution.py:15
  206.6 29.9 %all_gather.17 = bf16[16,160,128]{2,1,0:T(8,128)(2,1)S(1)} all-gather(bf16[1,160,128]{2,1,0:T(8,128)(2,1)S(1)} %fusion.38), channel_id=1, replica_groups=mesh['section'=8,'eg'=4,'q'=8,'dp'=2] {'q','dp'}, dimensions={0}, use_global_device_ids=true | all-gather | bytes 696320 | tf_op jit(solution)/shard_map/all_gather | solution.py:71
  236.5 0.4 copy.76
  236.9 0.5 convolution_convert_fusion.2
  237.6 1.0 copy.83
  238.6 10.4 %all-to-all-start.4 = ((bf16[64,5,448]{2,1,0:T(8,128)(2,1)}), bf16[64,5,448]{2,1,0:T(8,128)(2,1)S(1)}, u32[]{:S(2)}, u32[]{:S(2)}) async-start(bf16[64,5,448]{2,1,0:T(8,128)(2,1)} %bitcast.34), calls=%async_computation.4 | async-start | bytes 1048576 | tf_op jit(solution)/shard_map/all_to_all | solution.py:79
  249.1 18.1 %all-to-all-done.4 = bf16[64,5,448]{2,1,0:T(8,128)(2,1)S(1)} async-done(((bf16[64,5,448]{2,1,0:T(8,128)(2,1)}), bf16[64,5,448]{2,1,0:T(8,128)(2,1)S(1)}, u32[]{:S(2)}, u32[]{:S(2)}) %all-to-all-start.4) | async-done | bytes 286752 | tf_op jit(solution)/shard_map/all_to_all | solution.py:79
  267.1 0.3 copy.108
  267.5 0.4 reshape.152
  267.9 0.7 gather_fusion.1
  268.7 0.3 reshape.155
  268.9 0.6 multiply_reduce_fusion
  269.6 0.7 fusion.31
  (62 shorter events, 2.7 us)
Async XLA Ops:
  6.5 61.9 %copy-start = (bf16[1,3584,128]{2,1,0:T(8,128)(2,1)S(1)}, bf16[1,3584,128]{2,1,0:T(8,128)(2,1)}, u32[]{:S(2)}) copy-start(bf16[1,3584,128]{2,1,0:T(8,128)(2,1)} %param.12) | copy-start | bytes 2752516
  6.5 61.9 %all-gather.3.cloned.1.call-start = ((), (), s32[]{:S(2)}) async-start(), calls=%async_computation.5 | async-start | bytes 2580480 | tf_op jit(solution)/shard_map/all_gather | solution.py:58
  34.5 75.2 %all-to-all-start.1 = ((bf16[8,448,128]{2,1,0:T(8,128)(2,1)}), bf16[8,448,128]{2,1,0:T(8,128)(2,1)S(1)}, u32[]{:S(2)}, u32[]{:S(2)}) async-start(bf16[8,448,128]{2,1,0:T(8,128)(2,1)} %bitcast.16), calls=%async_computation.1 | async-start | bytes 1835008 | tf_op jit(solution)/shard_map/all_to_all | solution.py:97
  42.7 28.3 %copy-start.3 = (bf16[1,3584,128]{2,1,0:T(8,128)(2,1)S(1)}, bf16[1,3584,128]{2,1,0:T(8,128)(2,1)}, u32[]{:S(2)}) copy-start(bf16[1,3584,128]{2,1,0:T(8,128)(2,1)} %param.11) | copy-start | bytes 2752516
  68.5 2.6 copy-start.1
  71.8 7.4 %collective-permute-start = (f32[2,160,128]{2,1,0:T(8,128)S(1)}, f32[2,160,128]{2,1,0:T(8,128)S(1)}, u32[]{:S(2)}, u32[]{:S(2)}) collective-permute-start(f32[2,160,128]{2,1,0:T(8,128)S(1)} %fusion.27), channel_id=1, source_target_pairs={{0,1},{1,0},{2,3},{3,2},{4,5},{5,4},{6,7},{7,6},{8,9},{9,8},{10,11... | collective-permute-start | bytes 491528 | tf_op jit(solution)/shard_map/ppermute | solution.py:15
  109.7 3.4 %copy-start.5 = (bf16[8,448,128]{2,1,0:T(8,128)(2,1)}, bf16[8,448,128]{2,1,0:T(8,128)(2,1)S(1)}, u32[]{:S(2)}) copy-start(bf16[8,448,128]{2,1,0:T(8,128)(2,1)S(1)} %all-to-all-done.1) | copy-start | bytes 2752516
  109.7 12.0 %copy-start.8 = (f32[1,2,8,2]{2,3,1,0:T(2,128)S(1)}, f32[1,2,8,2]{2,3,1,0:T(2,128)}, u32[]{:S(2)}) copy-start(f32[1,2,8,2]{2,3,1,0:T(2,128)} %param.15) | copy-start | bytes 388
  113.1 26.7 %all-to-all-start.2 = ((bf16[64,5,448]{2,1,0:T(8,128)(2,1)}), bf16[64,5,448]{2,1,0:T(8,128)(2,1)S(1)}, u32[]{:S(2)}, u32[]{:S(2)}) async-start(bf16[64,5,448]{2,1,0:T(8,128)(2,1)} %bitcast.19), calls=%async_computation.2 | async-start | bytes 1048576 | tf_op jit(solution)/shard_map/all_to_all | solution.py:79
  121.6 74.0 %all-gather.5.cloned.1.call-start = ((), (), s32[]{:S(2)}) async-start(), calls=%async_computation.6 | async-start | bytes 2580480 | tf_op jit(solution)/shard_map/all_gather | solution.py:58
  140.5 1.7 copy-start.4
  140.5 9.4 %copy-start.7 = (f32[1,7168]{1,0:T(1,128)S(1)}, f32[1,7168]{1,0:T(1,128)}, u32[]{:S(2)}) copy-start(f32[1,7168]{1,0:T(1,128)} %param.10) | copy-start | bytes 86020
  142.3 7.4 %collective-permute-start.1 = (bf16[8,7168]{1,0:T(8,128)(2,1)S(1)}, bf16[8,7168]{1,0:T(8,128)(2,1)S(1)}, u32[]{:S(2)}, u32[]{:S(2)}) collective-permute-start(bf16[8,7168]{1,0:T(8,128)(2,1)S(1)} %fusion.23), channel_id=1, source_target_pairs={{0,64},{64,128},{128,192},{192,256},{256,320},{320,384},{384,448},... | collective-permute-start | bytes 344072 | tf_op jit(solution)/shard_map/ppermute | solution.py:15
  195.6 2.6 copy-start.2
  199.0 38.0 %copy-start.6 = (bf16[8,448,128]{2,1,0:T(8,128)(2,1)S(1)}, bf16[8,448,128]{2,1,0:T(8,128)(2,1)}, u32[]{:S(2)}) copy-start(bf16[8,448,128]{2,1,0:T(8,128)(2,1)} %copy-done.5) | copy-start | bytes 2752516
  199.0 7.5 %collective-permute-start.2 = (f32[2,160,128]{2,1,0:T(8,128)S(1)}, f32[2,160,128]{2,1,0:T(8,128)S(1)}, u32[]{:S(2)}, u32[]{:S(2)}) collective-permute-start(f32[2,160,128]{2,1,0:T(8,128)S(1)} %fusion.24), channel_id=1, source_target_pairs={{0,1},{1,0},{2,3},{3,2},{4,5},{5,4},{6,7},{7,6},{8,9},{9,8},{10,11... | collective-permute-start | bytes 491528 | tf_op jit(solution)/shard_map/ppermute | solution.py:15
  238.6 28.5 %all-to-all-start.4 = ((bf16[64,5,448]{2,1,0:T(8,128)(2,1)}), bf16[64,5,448]{2,1,0:T(8,128)(2,1)S(1)}, u32[]{:S(2)}, u32[]{:S(2)}) async-start(bf16[64,5,448]{2,1,0:T(8,128)(2,1)} %bitcast.34), calls=%async_computation.4 | async-start | bytes 1048576 | tf_op jit(solution)/shard_map/all_to_all | solution.py:79
Sparse Core Ops, SparseCore 0:
  34.6 33.8 all-gather.2
  164.6 31.0 all-gather.4

commit v8 on v4

--- a/solution.py
+++ b/solution.py
@@ -70,7 +70,7 @@
     piece = out.shape[1]
     out = out.reshape(capacity, blocks, experts, halves, piece).transpose(2, 1, 3, 0, 4)
     back = lax.all_to_all(
-        out.reshape(sources, capacity * piece), ALL, split_axis=0, concat_axis=0, tiled=True
+        out.reshape(sources, 2, capacity * piece // 2), ALL, split_axis=0, concat_axis=0, tiled=True
     )
     back = back.reshape(experts, blocks, halves, capacity, piece).transpose(0, 3, 2, 1, 4)
     expert_out = back.reshape(experts * capacity, model_width)

time: 258 us -> 248 us (0.961)
  other arithmetic: 13.2 us -> 4.62 us
    all_to_all x4 -> x0, other arithmetic: 8.58 us -> none  [moe_layer(): lax.all_to_all(out.reshape(sources, capacity * piece), ALL, split_axis=0,...]
    unnamed x22 -> x18, local copies, waits for them, and re-layouts: 2.92 us -> 0.04 us
    reshape x0 -> x2, local copies, waits for them, and re-layouts: none -> 2.74 us  [moe_layer(): out.reshape(sources, 2, capacity * piece // 2)]
where the time goes in v8:
time: 248 us; the launch traced here: 247 us
  waiting for transfers between devices  106 us (43%)
  blocking collectives  69.7 us (28%)
  starting transfers between devices  29.8 us (12%)
  between operations  13.8 us (6%)
  local copies, waits for them, and re-layouts  12.9 us (5%)
  matrix products  10.2 us (4%)
  other arithmetic  4.62 us (2%)
    all_gather x2, waiting for transfers between devices, moe_layer(): arrived = lax.all_gather(arrived, 'q', axis=1, tiled=True)  56.3 us
    all_gather x2, blocking collectives, moe_layer(): hidden_all = lax.all_gather(hidden, 'q', axis=1, tiled=True)  35.4 us
    all_to_all x2, blocking collectives, moe_layer(): lax.all_to_all(send, ('eg', 'dp'), split_axis=0, concat_axis=0, tiled=True)  34.3 us
    all_to_all x2, waiting for transfers between devices, moe_layer(): lax.all_to_all(out.reshape(sources, 2, capacity * piece // 2), ALL, split...  27.6 us
    ppermute x3, waiting for transfers between devices, passed_along(): lax.ppermute(array, axis, [(i, (i + by) % length) for i in range(length)])  22.1 us
    all_to_all x2, starting transfers between devices, moe_layer(): lax.all_to_all(out.reshape(sources, 2, capacity * piece // 2), ALL, split...  14.1 us
    all_to_all x1, starting transfers between devices, on_device(): lax.all_to_all(down_local.reshape(n_blocks, piece, width), 'q', split_axi...  8.2 us
    ppermute x3, starting transfers between devices, passed_along(): lax.ppermute(array, axis, [(i, (i + by) % length) for i in range(length)])  7.5 us
  transfers between devices with their start and end apart: 8, of which 7 were waited for; matrix products, arithmetic and copies ran while one was open for 1% of the time, Pallas kernels for 0%

profile of v8, /device:TPU:1, one launch (start us, length us, event | category | flops | bytes accessed | tf_op | source)
XLA Modules:
  0.0 247.1 jit_solution(13979369895368437544)
XLA Ops:
  6.5 0.8 fusion.38
  8.3 0.7 bitcast_add_fusion.1
  9.1 1.1 fusion.16
  10.2 1.2 convolution_convert_fusion.1
  11.4 0.2 reshape_reshape.6
  11.9 21.8 %all_to_all.25 = bf16[8,140,128]{2,1,0:T(8,128)(2,1)S(1)} all-to-all(bf16[8,140,128]{2,1,0:T(8,128)(2,1)S(1)} %copy.54), channel_id=1, replica_groups=mesh['section'=8,'eg'=4,'q'=8,'dp'=2] {'eg','dp'}, dimensions={0} | all-to-all | bytes 573440 | tf_op jit(solution)/shard_map/all_to_all | solution.py:56
  33.7 0.8 copy.55
  34.5 8.2 %all-to-all-start.1 = ((bf16[8,448,128]{2,1,0:T(8,128)(2,1)}), bf16[8,448,128]{2,1,0:T(8,128)(2,1)S(1)}, u32[]{:S(2)}, u32[]{:S(2)}) async-start(bf16[8,448,128]{2,1,0:T(8,128)(2,1)} %bitcast.16), calls=%async_computation.1 | async-start | bytes 1835008 | tf_op jit(solution)/shard_map/all_to_all | solution.py:90
  42.7 25.7 %all-gather.3.cloned.1.call-done = bf16[5,64,3584]{2,1,0:T(8,128)(2,1)} async-done(((bf16[5,8,3584]{2,1,0:T(8,128)(2,1)}), bf16[5,64,3584]{2,1,0:T(8,128)(2,1)}) %all-gather.3.cloned.1.call-update) | async-done | bytes 2293776 | tf_op jit(solution)/shard_map/all_gather | solution.py:58
  68.5 2.5 %convolution_bitcast_fusion.2 = f32[1,320,128]{2,1,0:T(8,128)S(1)} fusion(bf16[320,3584]{1,0:T(8,128)(2,1)} %bitcast.107, bf16[1,3584,128]{2,1,0:T(8,128)(2,1)S(1)} %copy-done), kind=kOutput, calls=%fused_computation.8 | convolution fusion | flops 293601280 | bytes 3375104 | tf_op jit(solution)/shard_map/dot_general | solution.py:62
  71.0 0.8 convolution_bitcast_fusion.3
  71.8 2.1 collective-permute-start
  73.9 8.8 %collective-permute-done = f32[2,320,128]{2,1,0:T(8,128)S(1)} collective-permute-done((f32[2,320,128]{2,1,0:T(8,128)S(1)}, f32[2,320,128]{2,1,0:T(8,128)S(1)}, u32[]{:S(2)}, u32[]{:S(2)}) %collective-permute-start) | collective-permute-done | bytes 327712 | tf_op jit(solution)/shard_map/ppermute | solution.py:15
  82.8 17.7 %all_gather.13 = bf16[320,1024]{1,0:T(8,128)(2,1)S(1)} all-gather(bf16[320,128]{1,0:T(8,128)(2,1)S(1)} %fusion.23), channel_id=1, replica_groups=mesh['section'=8,'eg'=4,'q'=8,'dp'=2] {'q'}, dimensions={1}, use_global_device_ids=true | all-gather | bytes 737280 | tf_op jit(solution)/shard_map/all_gather | solution.py:66
  100.5 1.3 convolution_convert_fusion.3
  101.7 1.1 reshape.126
  103.1 1.4 reshape.127
  104.4 6.1 %all-to-all-start.2 = ((bf16[64,2,1120]{2,1,0:T(2,128)(2,1)}), bf16[64,2,1120]{2,1,0:T(2,128)(2,1)S(1)}, u32[]{:S(2)}, u32[]{:S(2)}) async-start(bf16[64,2,1120]{2,1,0:T(2,128)(2,1)} %reshape.127), calls=%async_computation.2 | async-start | bytes 589824 | tf_op jit(solution)/shard_map/all_to_all | solution.py:72
  110.7 13.8 %all-to-all-done.2 = bf16[64,2,1120]{2,1,0:T(2,128)(2,1)S(1)} async-done(((bf16[64,2,1120]{2,1,0:T(2,128)(2,1)}), bf16[64,2,1120]{2,1,0:T(2,128)(2,1)S(1)}, u32[]{:S(2)}, u32[]{:S(2)}) %all-to-all-start.2) | async-done | bytes 286752 | tf_op jit(solution)/shard_map/all_to_all | solution.py:72
  124.5 0.6 reshape.128
  125.1 0.2 copy.58
  125.3 0.4 reshape.129
  125.7 0.7 gather_fusion
  126.5 0.3 reshape.138
  126.8 0.6 multiply_reduce_fusion.1
  127.5 3.1 %collective-permute-start.1 = (bf16[8,7168]{1,0:T(8,128)(2,1)S(1)}, bf16[8,7168]{1,0:T(8,128)(2,1)S(1)}, u32[]{:S(2)}, u32[]{:S(2)}) collective-permute-start(bf16[8,7168]{1,0:T(8,128)(2,1)S(1)} %fusion.19), channel_id=1, source_target_pairs={{0,64},{64,128},{128,192},{192,256},{256,320},{320,384},{384,448},... | collective-permute-start | bytes 344072 | tf_op jit(solution)/shard_map/ppermute | solution.py:15
  130.7 4.7 %collective-permute-done.1 = bf16[8,7168]{1,0:T(8,128)(2,1)S(1)} collective-permute-done((bf16[8,7168]{1,0:T(8,128)(2,1)S(1)}, bf16[8,7168]{1,0:T(8,128)(2,1)S(1)}, u32[]{:S(2)}, u32[]{:S(2)}) %collective-permute-start.1) | collective-permute-done | bytes 114720 | tf_op jit(solution)/shard_map/ppermute | solution.py:15
  135.5 0.3 convolution_convert_fusion
  135.8 0.2 reshape_reshape.7
  136.4 12.5 %all_to_all.26 = bf16[8,140,128]{2,1,0:T(8,128)(2,1)S(1)} all-to-all(bf16[8,140,128]{2,1,0:T(8,128)(2,1)S(1)} %copy.63), channel_id=1, replica_groups=mesh['section'=8,'eg'=4,'q'=8,'dp'=2] {'eg','dp'}, dimensions={0} | all-to-all | bytes 573440 | tf_op jit(solution)/shard_map/all_to_all | solution.py:56
  148.9 0.8 copy.64
  149.7 30.6 %all-gather.5.cloned.1.call-done = bf16[5,64,3584]{2,1,0:T(8,128)(2,1)} async-done(((bf16[5,8,3584]{2,1,0:T(8,128)(2,1)}), bf16[5,64,3584]{2,1,0:T(8,128)(2,1)}) %all-gather.5.cloned.1.call-update) | async-done | bytes 2293776 | tf_op jit(solution)/shard_map/all_gather | solution.py:58
  180.3 2.5 %convolution_bitcast_fusion = f32[1,320,128]{2,1,0:T(8,128)S(1)} fusion(bf16[320,3584]{1,0:T(8,128)(2,1)} %bitcast.109, bf16[1,3584,128]{2,1,0:T(8,128)(2,1)S(1)} %copy-done), kind=kOutput, calls=%fused_computation.6 | convolution fusion | flops 293601280 | bytes 3375104 | tf_op jit(solution)/shard_map/dot_general | solution.py:62
  182.8 0.8 convolution_bitcast_fusion.1
  183.6 2.3 collective-permute-start.2
  186.0 8.7 %collective-permute-done.2 = f32[2,320,128]{2,1,0:T(8,128)S(1)} collective-permute-done((f32[2,320,128]{2,1,0:T(8,128)S(1)}, f32[2,320,128]{2,1,0:T(8,128)S(1)}, u32[]{:S(2)}, u32[]{:S(2)}) %collective-permute-start.2) | collective-permute-done | bytes 327712 | tf_op jit(solution)/shard_map/ppermute | solution.py:15
  194.8 17.7 %all_gather.15 = bf16[320,1024]{1,0:T(8,128)(2,1)S(1)} all-gather(bf16[320,128]{1,0:T(8,128)(2,1)S(1)} %fusion.21), channel_id=1, replica_groups=mesh['section'=8,'eg'=4,'q'=8,'dp'=2] {'q'}, dimensions={1}, use_global_device_ids=true | all-gather | bytes 737280 | tf_op jit(solution)/shard_map/all_gather | solution.py:66
  212.5 0.5 convolution_convert_fusion.2
  213.3 1.4 reshape.134
  214.7 8.0 %all-to-all-start.4 = ((bf16[64,2,1120]{2,1,0:T(2,128)(2,1)}), bf16[64,2,1120]{2,1,0:T(2,128)(2,1)S(1)}, u32[]{:S(2)}, u32[]{:S(2)}) async-start(bf16[64,2,1120]{2,1,0:T(2,128)(2,1)} %reshape.134), calls=%async_computation.4 | async-start | bytes 589824 | tf_op jit(solution)/shard_map/all_to_all | solution.py:72
  222.8 13.8 %all-to-all-done.4 = bf16[64,2,1120]{2,1,0:T(2,128)(2,1)S(1)} async-done(((bf16[64,2,1120]{2,1,0:T(2,128)(2,1)}), bf16[64,2,1120]{2,1,0:T(2,128)(2,1)S(1)}, u32[]{:S(2)}, u32[]{:S(2)}) %all-to-all-start.4) | async-done | bytes 286752 | tf_op jit(solution)/shard_map/all_to_all | solution.py:72
  236.6 0.6 reshape.135
  237.3 0.2 copy.66
  237.5 0.4 reshape.136
  237.9 0.7 gather_fusion.1
  238.7 0.3 reshape.139
  238.9 0.6 multiply_reduce_fusion
  239.6 0.7 fusion.25
  (63 shorter events, 3.2 us)
Async XLA Ops:
  6.5 61.9 %copy-start = (bf16[1,3584,128]{2,1,0:T(8,128)(2,1)S(1)}, bf16[1,3584,128]{2,1,0:T(8,128)(2,1)}, u32[]{:S(2)}) copy-start(bf16[1,3584,128]{2,1,0:T(8,128)(2,1)} %param.12) | copy-start | bytes 2752516
  6.5 61.9 %all-gather.3.cloned.1.call-start = ((), (), s32[]{:S(2)}) async-start(), calls=%async_computation.5 | async-start | bytes 2580480 | tf_op jit(solution)/shard_map/all_gather | solution.py:58
  34.5 66.0 %all-to-all-start.1 = ((bf16[8,448,128]{2,1,0:T(8,128)(2,1)}), bf16[8,448,128]{2,1,0:T(8,128)(2,1)S(1)}, u32[]{:S(2)}, u32[]{:S(2)}) async-start(bf16[8,448,128]{2,1,0:T(8,128)(2,1)} %bitcast.16), calls=%async_computation.1 | async-start | bytes 1835008 | tf_op jit(solution)/shard_map/all_to_all | solution.py:90
  42.7 28.3 %copy-start.3 = (bf16[1,3584,128]{2,1,0:T(8,128)(2,1)S(1)}, bf16[1,3584,128]{2,1,0:T(8,128)(2,1)}, u32[]{:S(2)}) copy-start(bf16[1,3584,128]{2,1,0:T(8,128)(2,1)} %param.11) | copy-start | bytes 2752516
  68.5 2.6 %copy-start.1 = (bf16[5,64,3584]{2,1,0:T(8,128)(2,1)S(1)}, bf16[5,64,3584]{2,1,0:T(8,128)(2,1)}, u32[]{:S(2)}) copy-start(bf16[5,64,3584]{2,1,0:T(8,128)(2,1)} %all-gather.3.cloned.1.call-done) | copy-start | bytes 6881284
  71.8 10.9 %collective-permute-start = (f32[2,320,128]{2,1,0:T(8,128)S(1)}, f32[2,320,128]{2,1,0:T(8,128)S(1)}, u32[]{:S(2)}, u32[]{:S(2)}) collective-permute-start(f32[2,320,128]{2,1,0:T(8,128)S(1)} %pad_maximum_fusion), channel_id=1, source_target_pairs={{0,1},{1,0},{2,3},{3,2},{4,5},{5,4},{6,7},{7,6},{8,9},{9,8},{10,11... | collective-permute-start | bytes 983048 | tf_op jit(solution)/shard_map/ppermute | solution.py:15
  100.5 10.1 %copy-start.8 = (f32[1,2,8,2]{2,3,1,0:T(2,128)S(1)}, f32[1,2,8,2]{2,3,1,0:T(2,128)}, u32[]{:S(2)}) copy-start(f32[1,2,8,2]{2,3,1,0:T(2,128)} %param.15) | copy-start | bytes 388
  100.5 1.3 copy-start.5
  104.4 20.0 %all-to-all-start.2 = ((bf16[64,2,1120]{2,1,0:T(2,128)(2,1)}), bf16[64,2,1120]{2,1,0:T(2,128)(2,1)S(1)}, u32[]{:S(2)}, u32[]{:S(2)}) async-start(bf16[64,2,1120]{2,1,0:T(2,128)(2,1)} %reshape.127), calls=%async_computation.2 | async-start | bytes 589824 | tf_op jit(solution)/shard_map/all_to_all | solution.py:72
  110.6 69.7 %all-gather.5.cloned.1.call-start = ((), (), s32[]{:S(2)}) async-start(), calls=%async_computation.6 | async-start | bytes 2580480 | tf_op jit(solution)/shard_map/all_gather | solution.py:58
  125.7 1.7 copy-start.4
  125.7 9.8 %copy-start.7 = (f32[1,7168]{1,0:T(1,128)S(1)}, f32[1,7168]{1,0:T(1,128)}, u32[]{:S(2)}) copy-start(f32[1,7168]{1,0:T(1,128)} %param.10) | copy-start | bytes 86020
  127.5 7.9 %collective-permute-start.1 = (bf16[8,7168]{1,0:T(8,128)(2,1)S(1)}, bf16[8,7168]{1,0:T(8,128)(2,1)S(1)}, u32[]{:S(2)}, u32[]{:S(2)}) collective-permute-start(bf16[8,7168]{1,0:T(8,128)(2,1)S(1)} %fusion.19), channel_id=1, source_target_pairs={{0,64},{64,128},{128,192},{192,256},{256,320},{320,384},{384,448},... | collective-permute-start | bytes 344072 | tf_op jit(solution)/shard_map/ppermute | solution.py:15
  180.3 2.6 %copy-start.2 = (bf16[5,64,3584]{2,1,0:T(8,128)(2,1)S(1)}, bf16[5,64,3584]{2,1,0:T(8,128)(2,1)}, u32[]{:S(2)}) copy-start(bf16[5,64,3584]{2,1,0:T(8,128)(2,1)} %all-gather.5.cloned.1.call-done) | copy-start | bytes 6881284
  183.6 28.9 %copy-start.6 = (bf16[8,448,128]{2,1,0:T(8,128)(2,1)S(1)}, bf16[8,448,128]{2,1,0:T(8,128)(2,1)}, u32[]{:S(2)}) copy-start(bf16[8,448,128]{2,1,0:T(8,128)(2,1)} %copy-done.5) | copy-start | bytes 2752516
  183.6 11.0 %collective-permute-start.2 = (f32[2,320,128]{2,1,0:T(8,128)S(1)}, f32[2,320,128]{2,1,0:T(8,128)S(1)}, u32[]{:S(2)}, u32[]{:S(2)}) collective-permute-start(f32[2,320,128]{2,1,0:T(8,128)S(1)} %pad_maximum_fusion.1), channel_id=1, source_target_pairs={{0,1},{1,0},{2,3},{3,2},{4,5},{5,4},{6,7},{7,6},{8,9},{9,8},{10,11... | collective-permute-start | bytes 983048 | tf_op jit(solution)/shard_map/ppermute | solution.py:15
  214.7 21.9 %all-to-all-start.4 = ((bf16[64,2,1120]{2,1,0:T(2,128)(2,1)}), bf16[64,2,1120]{2,1,0:T(2,128)(2,1)S(1)}, u32[]{:S(2)}, u32[]{:S(2)}) async-start(bf16[64,2,1120]{2,1,0:T(2,128)(2,1)} %reshape.134), calls=%async_computation.4 | async-start | bytes 589824 | tf_op jit(solution)/shard_map/all_to_all | solution.py:72
Sparse Core Ops, SparseCore 0:
  34.6 33.7 all-gather.2
  149.8 30.4 all-gather.4

commit v9 on v8

--- a/solution.py
+++ b/solution.py
@@ -80,6 +80,48 @@
     return (widened + mixed_sum).astype(jnp.bfloat16)
 
 
+def moe_layer_rows(stream, gain_row, gate_full, up_full, down_rows, routes, mixing):
+    experts = lax.axis_size("eg")
+    blocks = lax.axis_size("q")
+    halves = lax.axis_size("dp")
+    tok_rows, model_width = stream.shape
+    fan_out = routes.shape[1]
+    capacity = min(tok_rows, max(2, 5 * tok_rows * fan_out // (4 * experts)))
+    widened, outgoing, target = route(stream, gain_row, routes, experts, capacity)
+    lanes = 128
+    tiles = model_width // lanes
+    send = outgoing.reshape(experts, capacity * tiles, lanes)
+    arrived = lax.all_to_all(send, "eg", split_axis=0, concat_axis=0, tiled=True)
+    arrived = arrived.reshape(experts, capacity, model_width).transpose(1, 0, 2)
+    arrived = lax.all_gather(arrived, "q", axis=1, tiled=True)
+    sources = blocks * experts
+    rows = arrived.reshape(capacity * sources, model_width)
+    gate_act = jnp.dot(rows, gate_full, preferred_element_type=jnp.float32)
+    upward = jnp.dot(rows, up_full, preferred_element_type=jnp.float32)
+    hidden = (jax.nn.silu(gate_act) * upward).astype(jnp.bfloat16)
+    hidden_all = lax.all_gather(hidden, "q", axis=1, tiled=True)
+    out = lax.dot_general(
+        hidden_all, down_rows, (((1,), (1,)), ((), ())), preferred_element_type=jnp.float32
+    ).astype(jnp.bfloat16)
+    piece = out.shape[1]
+    out = out.reshape(capacity, blocks, experts, piece).transpose(2, 1, 0, 3)
+    back = lax.all_to_all(
+        out.reshape(sources, 2, capacity * piece // 2), ("eg", "q"), split_axis=0, concat_axis=0,
+        tiled=True,
+    )
+    sub = piece // halves
+    back = back.reshape(experts, blocks, capacity, halves, sub).transpose(0, 2, 3, 1, 4)
+    expert_out = back.reshape(experts * capacity, model_width)
+    picked = jnp.take(expert_out, target, axis=0)
+    picked = picked.reshape(tok_rows, fan_out, model_width)
+    mixed_sum = jnp.sum(mixing[:, :, None] * picked.astype(jnp.float32), axis=1)
+    return (widened + mixed_sum).astype(jnp.bfloat16)
+
+
+def in_order(first, mine, other):
+    return jnp.where(first, jnp.concatenate([mine, other]), jnp.concatenate([other, mine]))
+
+
 def on_device(blocks, gains, w_gate, w_up, w_down, expert_ids, combine):
     stream = blocks[0]
     turns = expert_ids.shape[1]
@@ -91,9 +133,23 @@
         down_local.reshape(n_blocks, piece, width), "q", split_axis=0, concat_axis=0, tiled=True
     )
     down_mine = down_mine.transpose(1, 0, 2).reshape(piece, n_blocks * width)
+    first = lax.axis_index("dp") == 0
+    other = passed_along(jnp.stack([w_gate[0], w_up[0]]), "dp", 1)
+    other_down = passed_along(down_mine, "dp", 1)
     for layer_turn in range(turns):
         if layer_turn > 0:
+            stream, other, other_down = lax.optimization_barrier((stream, other, other_down))
             stream = passed_along(stream, "section", 1)
+            stream = moe_layer_rows(
+                stream,
+                gains[0],
+                in_order(first, w_gate[0], other[0]),
+                in_order(first, w_up[0], other[1]),
+                in_order(first, down_mine, other_down),
+                expert_ids[0, layer_turn],
+                combine[0, layer_turn],
+            )
+            continue
         stream = moe_layer(
             stream,
             gains[0],

time: 248 us -> 290 us (1.17)
  blocking collectives: 69.7 us -> 102 us
  local copies, waits for them, and re-layouts: 12.9 us -> 21 us
  waiting for transfers between devices: 106 us -> 101 us
  starting transfers between devices: 29.8 us -> 33.7 us
    all_gather x0 -> x1, waiting for transfers between devices: none -> 34.4 us  [moe_layer_rows(): arrived = lax.all_gather(arrived, 'q', axis=1, tiled=True)]
    all_gather x2 -> x1, waiting for transfers between devices: 56.3 us -> 25.7 us  [moe_layer(): arrived = lax.all_gather(arrived, 'q', axis=1, tiled=True)]
    all_to_all x2 -> x1, waiting for transfers between devices: 27.6 us -> 9.51 us  [moe_layer(): lax.all_to_all(out.reshape(sources, 2, capacity * piece // 2), ALL, split...]
    all_gather x0 -> x1, blocking collectives: none -> 15.8 us  [moe_layer_rows(): hidden_all = lax.all_gather(hidden, 'q', axis=1, tiled=True)]
    all_gather x2 -> x1, blocking collectives: 35.4 us -> 50.8 us  [moe_layer(): hidden_all = lax.all_gather(hidden, 'q', axis=1, tiled=True)]
    all_to_all x0 -> x1, blocking collectives: none -> 14 us  [moe_layer_rows(): lax.all_to_all(send, 'eg', split_axis=0, concat_axis=0, tiled=True)]
    all_to_all x0 -> x1, waiting for transfers between devices: none -> 13.4 us  [moe_layer_rows(): lax.all_to_all(out.reshape(sources, 2, capacity * piece // 2), ('eg', 'q'...]
    all_to_all x2 -> x1, blocking collectives: 34.3 us -> 21.8 us  [moe_layer(): lax.all_to_all(send, ('eg', 'dp'), split_axis=0, concat_axis=0, tiled=True)]
  transfers between devices with their start and end apart: 8 -> 9, of which waited for: 7 -> 7; matrix products, arithmetic and copies ran while one was open for 1% -> 6% of each run, Pallas kernels for 0% -> 0%
where the time goes in v9:
time: 290 us
  blocking collectives  102 us (35%)
  waiting for transfers between devices  101 us (35%)
  starting transfers between devices  33.7 us (12%)
  local copies, waits for them, and re-layouts  21 us (7%)
  between operations  13.8 us (5%)
  matrix products  10.9 us (4%)
  other arithmetic  6.85 us (2%)
    all_gather x1, blocking collectives, moe_layer(): hidden_all = lax.all_gather(hidden, 'q', axis=1, tiled=True)  50.8 us
    all_gather x1, waiting for transfers between devices, moe_layer_rows(): arrived = lax.all_gather(arrived, 'q', axis=1, tiled=True)  34.4 us
    all_gather x1, waiting for transfers between devices, moe_layer(): arrived = lax.all_gather(arrived, 'q', axis=1, tiled=True)  25.7 us
    all_to_all x1, blocking collectives, moe_layer(): lax.all_to_all(send, ('eg', 'dp'), split_axis=0, concat_axis=0, tiled=True)  21.8 us
    ppermute x4, waiting for transfers between devices, passed_along(): lax.ppermute(array, axis, [(i, (i + by) % length) for i in range(length)])  17.9 us
    all_gather x1, blocking collectives, moe_layer_rows(): hidden_all = lax.all_gather(hidden, 'q', axis=1, tiled=True)  15.8 us
    all_to_all x1, blocking collectives, moe_layer_rows(): lax.all_to_all(send, 'eg', split_axis=0, concat_axis=0, tiled=True)  14 us
    all_to_all x1, waiting for transfers between devices, moe_layer_rows(): lax.all_to_all(out.reshape(sources, 2, capacity * piece // 2), ('eg', 'q'...  13.4 us
  transfers between devices with their start and end apart: 9, of which 7 were waited for; matrix products, arithmetic and copies ran while one was open for 6% of the time, Pallas kernels for 0%

profile of v9, /device:TPU:1, one launch (start us, length us, event | category | flops | bytes accessed | tf_op | source)
XLA Modules:
  0.0 289.6 jit_solution(3827913335025722129)
XLA Ops:
  6.5 0.7 fusion.56
  8.2 0.7 bitcast_add_fusion.1
  9.0 1.1 fusion.32
  10.1 1.2 convolution_convert_fusion.1
  11.8 21.8 %all_to_all.25 = bf16[8,140,128]{2,1,0:T(8,128)(2,1)S(1)} all-to-all(bf16[8,140,128]{2,1,0:T(8,128)(2,1)S(1)} %copy.52), channel_id=1, replica_groups=mesh['section'=8,'eg'=4,'q'=8,'dp'=2] {'eg','dp'}, dimensions={0} | all-to-all | bytes 573440 | tf_op jit(solution)/shard_map/all_to_all | solution.py:56
  33.6 0.8 copy.53
  34.4 8.2 %all-to-all-start.1 = ((bf16[8,448,128]{2,1,0:T(8,128)(2,1)}), bf16[8,448,128]{2,1,0:T(8,128)(2,1)S(1)}, u32[]{:S(2)}, u32[]{:S(2)}) async-start(bf16[8,448,128]{2,1,0:T(8,128)(2,1)} %bitcast.100), calls=%async_computation.1 | async-start | bytes 1835008 | tf_op jit(solution)/shard_map/all_to_all | solution.py:132
  42.6 25.7 %all-gather.3.cloned.1.call-done = bf16[5,64,3584]{2,1,0:T(8,128)(2,1)} async-done(((bf16[5,8,3584]{2,1,0:T(8,128)(2,1)}), bf16[5,64,3584]{2,1,0:T(8,128)(2,1)}) %all-gather.3.cloned.1.call-update) | async-done | bytes 2293776 | tf_op jit(solution)/shard_map/all_gather | solution.py:58
  68.4 2.5 convolution_bitcast_fusion
  71.0 0.8 convolution_bitcast_fusion.1
  71.8 2.1 collective-permute-start
  73.8 1.4 pad_maximum_fusion
  75.2 3.2 %collective-permute-start.1 = (bf16[2,3584,128]{2,1,0:T(8,128)(2,1)}, bf16[2,3584,128]{2,1,0:T(8,128)(2,1)}, u32[]{:S(2)}, u32[]{:S(2)}) collective-permute-start(bf16[2,3584,128]{2,1,0:T(8,128)(2,1)} %pad_maximum_fusion), channel_id=1, source_target_pairs={{0,1},{1,0},{2,3},{3,2},{4,5},{5,4},{6,7},{7,6},{8,9},{9,8},{10,11... | collective-permute-start | bytes 5505032 | tf_op jit(solution)/shard_map/ppermute | solution.py:15
  78.6 4.2 %collective-permute-done = f32[2,320,128]{2,1,0:T(8,128)} collective-permute-done((f32[2,320,128]{2,1,0:T(8,128)S(1)}, f32[2,320,128]{2,1,0:T(8,128)}, u32[]{:S(2)}, u32[]{:S(2)}) %collective-permute-start) | collective-permute-done | bytes 327712 | tf_op jit(solution)/shard_map/ppermute | solution.py:15
  82.7 1.0 fusion.55
  83.8 50.8 %all_gather.13 = bf16[320,1024]{1,0:T(8,128)(2,1)S(1)} all-gather(bf16[320,128]{1,0:T(8,128)(2,1)S(1)} %fusion.37), channel_id=1, replica_groups=mesh['section'=8,'eg'=4,'q'=8,'dp'=2] {'q'}, dimensions={1}, use_global_device_ids=true | all-gather | bytes 737280 | tf_op jit(solution)/shard_map/all_gather | solution.py:66
  134.6 1.3 convolution_convert_fusion.2
  135.9 1.8 reshape.123
  137.7 1.2 copy.68
  138.9 1.4 reshape.124
  140.2 6.9 %all-to-all-start.2 = ((bf16[64,2,1120]{2,1,0:T(2,128)(2,1)}), bf16[64,2,1120]{2,1,0:T(2,128)(2,1)S(1)}, u32[]{:S(2)}, u32[]{:S(2)}) async-start(bf16[64,2,1120]{2,1,0:T(2,128)(2,1)} %reshape.124), calls=%async_computation.2 | async-start | bytes 589824 | tf_op jit(solution)/shard_map/all_to_all | solution.py:72
  147.2 1.1 copy_bitcast_fusion
  148.3 3.2 %collective-permute-start.2 = (bf16[448,1024]{1,0:T(8,128)(2,1)}, bf16[448,1024]{1,0:T(8,128)(2,1)}, u32[]{:S(2)}, u32[]{:S(2)}) collective-permute-start(bf16[448,1024]{1,0:T(8,128)(2,1)} %copy_bitcast_fusion), channel_id=1, source_target_pairs={{0,1},{1,0},{2,3},{3,2},{4,5},{5,4},{6,7},{7,6},{8,9},{9,8},{10,11... | collective-permute-start | bytes 2752520 | tf_op jit(solution)/shard_map/ppermute | solution.py:15
  151.5 9.5 %all-to-all-done.2 = bf16[64,2,1120]{2,1,0:T(2,128)(2,1)S(1)} async-done(((bf16[64,2,1120]{2,1,0:T(2,128)(2,1)}), bf16[64,2,1120]{2,1,0:T(2,128)(2,1)S(1)}, u32[]{:S(2)}, u32[]{:S(2)}) %all-to-all-start.2) | async-done | bytes 286752 | tf_op jit(solution)/shard_map/all_to_all | solution.py:72
  161.0 0.6 reshape.125
  161.9 0.4 reshape.126
  162.3 0.7 gather_fusion
  163.4 0.6 multiply_reduce_fusion.1
  164.1 10.2 %collective-permute-done.2 = bf16[448,1024]{1,0:T(8,128)(2,1)} collective-permute-done((bf16[448,1024]{1,0:T(8,128)(2,1)}, bf16[448,1024]{1,0:T(8,128)(2,1)}, u32[]{:S(2)}, u32[]{:S(2)}) %collective-permute-start.2) | collective-permute-done | bytes 917536 | tf_op jit(solution)/shard_map/ppermute | solution.py:15
  174.3 3.1 %collective-permute-start.3 = (bf16[8,7168]{1,0:T(8,128)(2,1)S(1)}, bf16[8,7168]{1,0:T(8,128)(2,1)S(1)}, u32[]{:S(2)}, u32[]{:S(2)}) collective-permute-start(bf16[8,7168]{1,0:T(8,128)(2,1)S(1)} %fusion.35), channel_id=1, source_target_pairs={{0,64},{64,128},{128,192},{192,256},{256,320},{320,384},{384,448},... | collective-permute-start | bytes 344072 | tf_op jit(solution)/shard_map/ppermute | solution.py:15
  177.5 3.5 %collective-permute-done.3 = bf16[8,7168]{1,0:T(8,128)(2,1)S(1)} collective-permute-done((bf16[8,7168]{1,0:T(8,128)(2,1)S(1)}, bf16[8,7168]{1,0:T(8,128)(2,1)S(1)}, u32[]{:S(2)}, u32[]{:S(2)}) %collective-permute-start.3) | collective-permute-done | bytes 114720 | tf_op jit(solution)/shard_map/ppermute | solution.py:15
  181.7 14.0 %all_to_all.26 = bf16[4,280,128]{2,1,0:T(8,128)(2,1)S(1)} all-to-all(bf16[4,280,128]{2,1,0:T(8,128)(2,1)S(1)} %reshape_reshape.7), channel_id=1, replica_groups=mesh['section'=8,'eg'=4,'q'=8,'dp'=2] {'eg'}, dimensions={0} | all-to-all | bytes 573440 | tf_op jit(solution)/shard_map/all_to_all | solution.py:94
  195.7 1.1 reshape.127
  196.9 2.5 slice_bitcast_fusion.1
  199.4 34.4 %all-gather.5.cloned.1.call-done = bf16[5,32,7168]{2,0,1:T(8,128)(2,1)} async-done(((bf16[5,4,7168]{2,0,1:T(8,128)(2,1)}), bf16[5,32,7168]{2,0,1:T(8,128)(2,1)}) %all-gather.5.cloned.1.call-update) | async-done | bytes 2293776 | tf_op jit(solution)/shard_map/all_gather | solution.py:96
  233.8 3.6 %copy.60 = bf16[5,32,7168]{2,1,0:T(8,128)(2,1)S(1)} copy(bf16[5,32,7168]{2,0,1:T(8,128)(2,1)} %all-gather.5.cloned.1.call-done) | data formatting | bytes 4587520 | tf_op jit(solution)/shard_map/all_gather | solution.py:96
  237.4 0.8 fusion
  238.2 0.8 fusion.23
  239.0 15.8 %all_gather.15 = bf16[160,1024]{1,0:T(8,128)(2,1)S(1)} all-gather(bf16[160,128]{1,0:T(8,128)(2,1)S(1)} %fusion.23), channel_id=1, replica_groups=mesh['section'=8,'eg'=4,'q'=8,'dp'=2] {'q'}, dimensions={1}, use_global_device_ids=true | all-gather | bytes 368640 | tf_op jit(solution)/shard_map/all_gather | solution.py:102
  254.8 2.9 %fusion.21 = bf16[160,896]{1,0:T(8,128)(2,1)S(1)} fusion(bf16[160,1024]{1,0:T(8,128)(2,1)S(1)} %all_gather.15, bf16[448,1024]{1,0:T(8,128)(2,1)} %collective-permute-done.2, bf16[448,1024]{1,0:T(8,128)(2,1)} %copy_bitcast_fusion, pred[]{:T(512)S(6)} %eq.75), kind=kOutput, calls=%fused_computation.30 | convolution fusion | flops 302002176 | bytes 2449409 | tf_op jit(solution)/shard_map/dot_general | solution.py:103
  257.9 1.1 reshape.130
  259.0 7.0 %all-to-all-start.4 = ((bf16[32,2,2240]{2,1,0:T(2,128)(2,1)}), bf16[32,2,2240]{2,1,0:T(2,128)(2,1)S(1)}, u32[]{:S(2)}, u32[]{:S(2)}) async-start(bf16[32,2,2240]{2,1,0:T(2,128)(2,1)} %reshape.130), calls=%async_computation.4 | async-start | bytes 589824 | tf_op jit(solution)/shard_map/all_to_all | solution.py:108
  266.1 13.4 %all-to-all-done.4 = bf16[32,2,2240]{2,1,0:T(2,128)(2,1)S(1)} async-done(((bf16[32,2,2240]{2,1,0:T(2,128)(2,1)}), bf16[32,2,2240]{2,1,0:T(2,128)(2,1)S(1)}, u32[]{:S(2)}, u32[]{:S(2)}) %all-to-all-start.4) | async-done | bytes 286752 | tf_op jit(solution)/shard_map/all_to_all | solution.py:108
  279.5 0.4 reshape.131
  280.0 0.4 reshape.132
  280.3 0.7 gather_fusion.1
  281.4 0.6 multiply_reduce_fusion
  282.1 0.7 fusion.39
  (60 shorter events, 3.9 us)
Async XLA Ops:
  6.5 61.8 %all-gather.3.cloned.1.call-start = ((), (), s32[]{:S(2)}) async-start(), calls=%async_computation.5 | async-start | bytes 2580480 | tf_op jit(solution)/shard_map/all_gather | solution.py:58
  11.5 56.9 %copy-start.2 = (bf16[1,3584,128]{2,1,0:T(8,128)(2,1)S(1)}, bf16[1,3584,128]{2,1,0:T(8,128)(2,1)}, u32[]{:S(2)}) copy-start(bf16[1,3584,128]{2,1,0:T(8,128)(2,1)} %param.12) | copy-start | bytes 2752516
  34.4 100.2 %all-to-all-start.1 = ((bf16[8,448,128]{2,1,0:T(8,128)(2,1)}), bf16[8,448,128]{2,1,0:T(8,128)(2,1)S(1)}, u32[]{:S(2)}, u32[]{:S(2)}) async-start(bf16[8,448,128]{2,1,0:T(8,128)(2,1)} %bitcast.100), calls=%async_computation.1 | async-start | bytes 1835008 | tf_op jit(solution)/shard_map/all_to_all | solution.py:132
  42.6 28.3 %copy-start.1 = (bf16[1,3584,128]{2,1,0:T(8,128)(2,1)S(1)}, bf16[1,3584,128]{2,1,0:T(8,128)(2,1)}, u32[]{:S(2)}) copy-start(bf16[1,3584,128]{2,1,0:T(8,128)(2,1)} %param.11) | copy-start | bytes 2752516
  68.4 2.6 copy-start
  71.7 6.7 %copy-start.6 = (f32[1,2,8,2]{2,3,1,0:T(2,128)S(1)}, f32[1,2,8,2]{2,3,1,0:T(2,128)}, u32[]{:S(2)}) copy-start(f32[1,2,8,2]{2,3,1,0:T(2,128)} %param.15) | copy-start | bytes 388
  71.8 11.0 %collective-permute-start = (f32[2,320,128]{2,1,0:T(8,128)S(1)}, f32[2,320,128]{2,1,0:T(8,128)}, u32[]{:S(2)}, u32[]{:S(2)}) collective-permute-start(f32[2,320,128]{2,1,0:T(8,128)S(1)} %pad_maximum_fusion.1), channel_id=1, source_target_pairs={{0,1},{1,0},{2,3},{3,2},{4,5},{5,4},{6,7},{7,6},{8,9},{9,8},{10,11... | collective-permute-start | bytes 983048 | tf_op jit(solution)/shard_map/ppermute | solution.py:15
  75.2 88.8 %collective-permute-start.1 = (bf16[2,3584,128]{2,1,0:T(8,128)(2,1)}, bf16[2,3584,128]{2,1,0:T(8,128)(2,1)}, u32[]{:S(2)}, u32[]{:S(2)}) collective-permute-start(bf16[2,3584,128]{2,1,0:T(8,128)(2,1)} %pad_maximum_fusion), channel_id=1, source_target_pairs={{0,1},{1,0},{2,3},{3,2},{4,5},{5,4},{6,7},{7,6},{8,9},{9,8},{10,11... | collective-permute-start | bytes 5505032 | tf_op jit(solution)/shard_map/ppermute | solution.py:15
  140.2 20.8 %all-to-all-start.2 = ((bf16[64,2,1120]{2,1,0:T(2,128)(2,1)}), bf16[64,2,1120]{2,1,0:T(2,128)(2,1)S(1)}, u32[]{:S(2)}, u32[]{:S(2)}) async-start(bf16[64,2,1120]{2,1,0:T(2,128)(2,1)} %reshape.124), calls=%async_computation.2 | async-start | bytes 589824 | tf_op jit(solution)/shard_map/all_to_all | solution.py:72
  147.1 86.7 %all-gather.5.cloned.1.call-start = ((), (), s32[]{:S(2)}) async-start(), calls=%async_computation.6 | async-start | bytes 4128768 | tf_op jit(solution)/shard_map/all_gather | solution.py:96
  148.3 26.0 %collective-permute-start.2 = (bf16[448,1024]{1,0:T(8,128)(2,1)}, bf16[448,1024]{1,0:T(8,128)(2,1)}, u32[]{:S(2)}, u32[]{:S(2)}) collective-permute-start(bf16[448,1024]{1,0:T(8,128)(2,1)} %copy_bitcast_fusion), channel_id=1, source_target_pairs={{0,1},{1,0},{2,3},{3,2},{4,5},{5,4},{6,7},{7,6},{8,9},{9,8},{10,11... | collective-permute-start | bytes 2752520 | tf_op jit(solution)/shard_map/ppermute | solution.py:15
  162.3 1.7 copy-start.3
  162.3 18.9 %copy-start.5 = (f32[1,7168]{1,0:T(1,128)S(1)}, f32[1,7168]{1,0:T(1,128)}, u32[]{:S(2)}) copy-start(f32[1,7168]{1,0:T(1,128)} %param.10) | copy-start | bytes 86020
  174.3 6.7 %collective-permute-start.3 = (bf16[8,7168]{1,0:T(8,128)(2,1)S(1)}, bf16[8,7168]{1,0:T(8,128)(2,1)S(1)}, u32[]{:S(2)}, u32[]{:S(2)}) collective-permute-start(bf16[8,7168]{1,0:T(8,128)(2,1)S(1)} %fusion.35), channel_id=1, source_target_pairs={{0,64},{64,128},{128,192},{192,256},{256,320},{320,384},{384,448},... | collective-permute-start | bytes 344072 | tf_op jit(solution)/shard_map/ppermute | solution.py:15
  233.8 3.6 %copy-start.4 = (bf16[3584,128]{1,0:T(8,128)(2,1)S(1)}, bf16[3584,128]{1,0:T(8,128)(2,1)}, u32[]{:S(2)}) copy-start(bf16[3584,128]{1,0:T(8,128)(2,1)} %get-tuple-element.16) | copy-start | bytes 2752516
  259.0 20.5 %all-to-all-start.4 = ((bf16[32,2,2240]{2,1,0:T(2,128)(2,1)}), bf16[32,2,2240]{2,1,0:T(2,128)(2,1)S(1)}, u32[]{:S(2)}, u32[]{:S(2)}) async-start(bf16[32,2,2240]{2,1,0:T(2,128)(2,1)} %reshape.130), calls=%async_computation.4 | async-start | bytes 589824 | tf_op jit(solution)/shard_map/all_to_all | solution.py:108
Sparse Core Ops, SparseCore 0:
  34.6 33.7 all-gather.2
  197.0 36.7 all-gather.4

commit v10 on v8

--- a/solution.py
+++ b/solution.py
@@ -61,7 +61,7 @@
     gate_part = jnp.dot(rows, gate_w, preferred_element_type=jnp.float32)
     up_part = jnp.dot(rows, up_w, preferred_element_type=jnp.float32)
     mine = jnp.stack([gate_part, up_part])
-    both = mine + passed_along(mine, "dp", 1)
+    both = mine + passed_along(mine.astype(jnp.bfloat16), "dp", 1).astype(jnp.float32)
     hidden = (jax.nn.silu(both[0]) * both[1]).astype(jnp.bfloat16)
     hidden_all = lax.all_gather(hidden, "q", axis=1, tiled=True)
     out = lax.dot_general(

time: 248 us -> 240 us (0.968)
  waiting for transfers between devices: 106 us -> 99.1 us
    ppermute x3, waiting for transfers between devices: 22.1 us -> 15.1 us  [passed_along(): lax.ppermute(array, axis, [(i, (i + by) % length) for i in range(length)])]
  transfers between devices with their start and end apart: 8 -> 8, of which waited for: 7 -> 7; matrix products, arithmetic and copies ran while one was open for 1% -> 2% of each run, Pallas kernels for 0% -> 0%
where the time goes in v10:
time: 240 us
  waiting for transfers between devices  99.1 us (41%)
  blocking collectives  69.7 us (29%)
  starting transfers between devices  29.7 us (12%)
  between operations  13.8 us (6%)
  local copies, waits for them, and re-layouts  12.9 us (5%)
  matrix products  10.2 us (4%)
  other arithmetic  4.58 us (2%)
    all_gather x2, waiting for transfers between devices, moe_layer(): arrived = lax.all_gather(arrived, 'q', axis=1, tiled=True)  56.3 us
    all_gather x2, blocking collectives, moe_layer(): hidden_all = lax.all_gather(hidden, 'q', axis=1, tiled=True)  35.4 us
    all_to_all x2, blocking collectives, moe_layer(): lax.all_to_all(send, ('eg', 'dp'), split_axis=0, concat_axis=0, tiled=True)  34.3 us
    all_to_all x2, waiting for transfers between devices, moe_layer(): lax.all_to_all(out.reshape(sources, 2, capacity * piece // 2), ALL, split...  27.6 us
    ppermute x3, waiting for transfers between devices, passed_along(): lax.ppermute(array, axis, [(i, (i + by) % length) for i in range(length)])  15.1 us
    all_to_all x2, starting transfers between devices, moe_layer(): lax.all_to_all(out.reshape(sources, 2, capacity * piece // 2), ALL, split...  14.1 us
    all_to_all x1, starting transfers between devices, on_device(): lax.all_to_all(down_local.reshape(n_blocks, piece, width), 'q', split_axi...  8.2 us
    ppermute x3, starting transfers between devices, passed_along(): lax.ppermute(array, axis, [(i, (i + by) % length) for i in range(length)])  7.36 us
  transfers between devices with their start and end apart: 8, of which 7 were waited for; matrix products, arithmetic and copies ran while one was open for 2% of the time, Pallas kernels for 0%

profile of v10, /device:TPU:1, one launch (start us, length us, event | category | flops | bytes accessed | tf_op | source)
XLA Modules:
  0.0 239.9 jit_solution(4905169620555228530)
XLA Ops:
  6.5 0.8 fusion.38
  8.3 0.7 bitcast_add_fusion.1
  9.1 1.1 fusion.18
  10.2 1.2 convolution_convert_fusion.1
  11.4 0.2 reshape_reshape.6
  11.9 21.8 %all_to_all.25 = bf16[8,140,128]{2,1,0:T(8,128)(2,1)S(1)} all-to-all(bf16[8,140,128]{2,1,0:T(8,128)(2,1)S(1)} %copy.54), channel_id=1, replica_groups=mesh['section'=8,'eg'=4,'q'=8,'dp'=2] {'eg','dp'}, dimensions={0} | all-to-all | bytes 573440 | tf_op jit(solution)/shard_map/all_to_all | solution.py:56
  33.7 0.8 copy.55
  34.5 8.2 %all-to-all-start.1 = ((bf16[8,448,128]{2,1,0:T(8,128)(2,1)}), bf16[8,448,128]{2,1,0:T(8,128)(2,1)S(1)}, u32[]{:S(2)}, u32[]{:S(2)}) async-start(bf16[8,448,128]{2,1,0:T(8,128)(2,1)} %bitcast.16), calls=%async_computation.1 | async-start | bytes 1835008 | tf_op jit(solution)/shard_map/all_to_all | solution.py:90
  42.7 25.7 %all-gather.3.cloned.1.call-done = bf16[5,64,3584]{2,1,0:T(8,128)(2,1)} async-done(((bf16[5,8,3584]{2,1,0:T(8,128)(2,1)}), bf16[5,64,3584]{2,1,0:T(8,128)(2,1)}) %all-gather.3.cloned.1.call-update) | async-done | bytes 2293776 | tf_op jit(solution)/shard_map/all_gather | solution.py:58
  68.5 2.5 %convolution_bitcast_fusion.2 = f32[1,320,128]{2,1,0:T(8,128)S(1)} fusion(bf16[320,3584]{1,0:T(8,128)(2,1)} %bitcast.107, bf16[1,3584,128]{2,1,0:T(8,128)(2,1)S(1)} %copy-done), kind=kOutput, calls=%fused_computation.8 | convolution fusion | flops 293601280 | bytes 3375104 | tf_op jit(solution)/shard_map/dot_general | solution.py:62
  71.0 0.8 convolution_bitcast_fusion.3
  71.8 2.1 collective-permute-start
  73.9 5.3 %collective-permute-done = bf16[2,320,128]{2,1,0:T(8,128)(2,1)S(1)} collective-permute-done((bf16[2,320,128]{2,1,0:T(8,128)(2,1)S(1)}, bf16[2,320,128]{2,1,0:T(8,128)(2,1)S(1)}, u32[]{:S(2)}, u32[]{:S(2)}) %collective-permute-start) | collective-permute-done | bytes 163872 | tf_op jit(solution)/shard_map/ppermute | solution.py:15
  79.3 17.7 %all_gather.13 = bf16[320,1024]{1,0:T(8,128)(2,1)S(1)} all-gather(bf16[320,128]{1,0:T(8,128)(2,1)S(1)} %fusion.25), channel_id=1, replica_groups=mesh['section'=8,'eg'=4,'q'=8,'dp'=2] {'q'}, dimensions={1}, use_global_device_ids=true | all-gather | bytes 737280 | tf_op jit(solution)/shard_map/all_gather | solution.py:66
  97.0 1.3 convolution_convert_fusion.3
  98.2 1.1 reshape.126
  99.5 1.4 reshape.127
  100.9 6.1 %all-to-all-start.2 = ((bf16[64,2,1120]{2,1,0:T(2,128)(2,1)}), bf16[64,2,1120]{2,1,0:T(2,128)(2,1)S(1)}, u32[]{:S(2)}, u32[]{:S(2)}) async-start(bf16[64,2,1120]{2,1,0:T(2,128)(2,1)} %reshape.127), calls=%async_computation.2 | async-start | bytes 589824 | tf_op jit(solution)/shard_map/all_to_all | solution.py:72
  107.2 13.8 %all-to-all-done.2 = bf16[64,2,1120]{2,1,0:T(2,128)(2,1)S(1)} async-done(((bf16[64,2,1120]{2,1,0:T(2,128)(2,1)}), bf16[64,2,1120]{2,1,0:T(2,128)(2,1)S(1)}, u32[]{:S(2)}, u32[]{:S(2)}) %all-to-all-start.2) | async-done | bytes 286752 | tf_op jit(solution)/shard_map/all_to_all | solution.py:72
  121.0 0.6 reshape.128
  121.6 0.2 copy.58
  121.8 0.4 reshape.129
  122.2 0.7 gather_fusion
  123.0 0.3 reshape.138
  123.3 0.6 multiply_reduce_fusion.1
  124.0 3.1 %collective-permute-start.1 = (bf16[8,7168]{1,0:T(8,128)(2,1)S(1)}, bf16[8,7168]{1,0:T(8,128)(2,1)S(1)}, u32[]{:S(2)}, u32[]{:S(2)}) collective-permute-start(bf16[8,7168]{1,0:T(8,128)(2,1)S(1)} %fusion.21), channel_id=1, source_target_pairs={{0,64},{64,128},{128,192},{192,256},{256,320},{320,384},{384,448},... | collective-permute-start | bytes 344072 | tf_op jit(solution)/shard_map/ppermute | solution.py:15
  127.2 4.7 %collective-permute-done.1 = bf16[8,7168]{1,0:T(8,128)(2,1)S(1)} collective-permute-done((bf16[8,7168]{1,0:T(8,128)(2,1)S(1)}, bf16[8,7168]{1,0:T(8,128)(2,1)S(1)}, u32[]{:S(2)}, u32[]{:S(2)}) %collective-permute-start.1) | collective-permute-done | bytes 114720 | tf_op jit(solution)/shard_map/ppermute | solution.py:15
  132.0 0.3 convolution_convert_fusion
  132.3 0.2 reshape_reshape.7
  132.8 12.5 %all_to_all.26 = bf16[8,140,128]{2,1,0:T(8,128)(2,1)S(1)} all-to-all(bf16[8,140,128]{2,1,0:T(8,128)(2,1)S(1)} %copy.63), channel_id=1, replica_groups=mesh['section'=8,'eg'=4,'q'=8,'dp'=2] {'eg','dp'}, dimensions={0} | all-to-all | bytes 573440 | tf_op jit(solution)/shard_map/all_to_all | solution.py:56
  145.3 0.8 copy.64
  146.1 30.6 %all-gather.5.cloned.1.call-done = bf16[5,64,3584]{2,1,0:T(8,128)(2,1)} async-done(((bf16[5,8,3584]{2,1,0:T(8,128)(2,1)}), bf16[5,64,3584]{2,1,0:T(8,128)(2,1)}) %all-gather.5.cloned.1.call-update) | async-done | bytes 2293776 | tf_op jit(solution)/shard_map/all_gather | solution.py:58
  176.7 2.5 %convolution_bitcast_fusion = f32[1,320,128]{2,1,0:T(8,128)S(1)} fusion(bf16[320,3584]{1,0:T(8,128)(2,1)} %bitcast.109, bf16[1,3584,128]{2,1,0:T(8,128)(2,1)S(1)} %copy-done), kind=kOutput, calls=%fused_computation.6 | convolution fusion | flops 293601280 | bytes 3375104 | tf_op jit(solution)/shard_map/dot_general | solution.py:62
  179.3 0.8 convolution_bitcast_fusion.1
  180.1 2.2 collective-permute-start.2
  182.3 5.2 %collective-permute-done.2 = bf16[2,320,128]{2,1,0:T(8,128)(2,1)S(1)} collective-permute-done((bf16[2,320,128]{2,1,0:T(8,128)(2,1)S(1)}, bf16[2,320,128]{2,1,0:T(8,128)(2,1)S(1)}, u32[]{:S(2)}, u32[]{:S(2)}) %collective-permute-start.2) | collective-permute-done | bytes 163872 | tf_op jit(solution)/shard_map/ppermute | solution.py:15
  187.6 17.7 %all_gather.15 = bf16[320,1024]{1,0:T(8,128)(2,1)S(1)} all-gather(bf16[320,128]{1,0:T(8,128)(2,1)S(1)} %fusion.23), channel_id=1, replica_groups=mesh['section'=8,'eg'=4,'q'=8,'dp'=2] {'q'}, dimensions={1}, use_global_device_ids=true | all-gather | bytes 737280 | tf_op jit(solution)/shard_map/all_gather | solution.py:66
  205.3 0.5 convolution_convert_fusion.2
  206.2 1.4 reshape.134
  207.5 8.0 %all-to-all-start.4 = ((bf16[64,2,1120]{2,1,0:T(2,128)(2,1)}), bf16[64,2,1120]{2,1,0:T(2,128)(2,1)S(1)}, u32[]{:S(2)}, u32[]{:S(2)}) async-start(bf16[64,2,1120]{2,1,0:T(2,128)(2,1)} %reshape.134), calls=%async_computation.4 | async-start | bytes 589824 | tf_op jit(solution)/shard_map/all_to_all | solution.py:72
  215.6 13.8 %all-to-all-done.4 = bf16[64,2,1120]{2,1,0:T(2,128)(2,1)S(1)} async-done(((bf16[64,2,1120]{2,1,0:T(2,128)(2,1)}), bf16[64,2,1120]{2,1,0:T(2,128)(2,1)S(1)}, u32[]{:S(2)}, u32[]{:S(2)}) %all-to-all-start.4) | async-done | bytes 286752 | tf_op jit(solution)/shard_map/all_to_all | solution.py:72
  229.4 0.6 reshape.135
  230.1 0.2 copy.66
  230.3 0.4 reshape.136
  230.7 0.7 gather_fusion.1
  231.5 0.3 reshape.139
  231.7 0.6 multiply_reduce_fusion
  232.4 0.7 fusion.27
  (63 shorter events, 3.1 us)
Async XLA Ops:
  6.5 61.9 %copy-start = (bf16[1,3584,128]{2,1,0:T(8,128)(2,1)S(1)}, bf16[1,3584,128]{2,1,0:T(8,128)(2,1)}, u32[]{:S(2)}) copy-start(bf16[1,3584,128]{2,1,0:T(8,128)(2,1)} %param.12) | copy-start | bytes 2752516
  6.5 61.9 %all-gather.3.cloned.1.call-start = ((), (), s32[]{:S(2)}) async-start(), calls=%async_computation.5 | async-start | bytes 2580480 | tf_op jit(solution)/shard_map/all_gather | solution.py:58
  34.5 62.5 %all-to-all-start.1 = ((bf16[8,448,128]{2,1,0:T(8,128)(2,1)}), bf16[8,448,128]{2,1,0:T(8,128)(2,1)S(1)}, u32[]{:S(2)}, u32[]{:S(2)}) async-start(bf16[8,448,128]{2,1,0:T(8,128)(2,1)} %bitcast.16), calls=%async_computation.1 | async-start | bytes 1835008 | tf_op jit(solution)/shard_map/all_to_all | solution.py:90
  42.7 28.3 %copy-start.3 = (bf16[1,3584,128]{2,1,0:T(8,128)(2,1)S(1)}, bf16[1,3584,128]{2,1,0:T(8,128)(2,1)}, u32[]{:S(2)}) copy-start(bf16[1,3584,128]{2,1,0:T(8,128)(2,1)} %param.11) | copy-start | bytes 2752516
  68.5 2.6 %copy-start.1 = (bf16[5,64,3584]{2,1,0:T(8,128)(2,1)S(1)}, bf16[5,64,3584]{2,1,0:T(8,128)(2,1)}, u32[]{:S(2)}) copy-start(bf16[5,64,3584]{2,1,0:T(8,128)(2,1)} %all-gather.3.cloned.1.call-done) | copy-start | bytes 6881284
  71.8 7.4 %collective-permute-start = (bf16[2,320,128]{2,1,0:T(8,128)(2,1)S(1)}, bf16[2,320,128]{2,1,0:T(8,128)(2,1)S(1)}, u32[]{:S(2)}, u32[]{:S(2)}) collective-permute-start(bf16[2,320,128]{2,1,0:T(8,128)(2,1)S(1)} %fusion.13), channel_id=1, source_target_pairs={{0,1},{1,0},{2,3},{3,2},{4,5},{5,4},{6,7},{7,6},{8,9},{9,8},{10,11... | collective-permute-start | bytes 491528 | tf_op jit(solution)/shard_map/ppermute | solution.py:15
  97.0 10.1 %copy-start.8 = (f32[1,2,8,2]{2,3,1,0:T(2,128)S(1)}, f32[1,2,8,2]{2,3,1,0:T(2,128)}, u32[]{:S(2)}) copy-start(f32[1,2,8,2]{2,3,1,0:T(2,128)} %param.15) | copy-start | bytes 388
  97.0 1.3 copy-start.5
  100.9 20.0 %all-to-all-start.2 = ((bf16[64,2,1120]{2,1,0:T(2,128)(2,1)}), bf16[64,2,1120]{2,1,0:T(2,128)(2,1)S(1)}, u32[]{:S(2)}, u32[]{:S(2)}) async-start(bf16[64,2,1120]{2,1,0:T(2,128)(2,1)} %reshape.127), calls=%async_computation.2 | async-start | bytes 589824 | tf_op jit(solution)/shard_map/all_to_all | solution.py:72
  107.0 69.7 %all-gather.5.cloned.1.call-start = ((), (), s32[]{:S(2)}) async-start(), calls=%async_computation.6 | async-start | bytes 2580480 | tf_op jit(solution)/shard_map/all_gather | solution.py:58
  122.2 1.7 copy-start.4
  122.2 9.8 %copy-start.7 = (f32[1,7168]{1,0:T(1,128)S(1)}, f32[1,7168]{1,0:T(1,128)}, u32[]{:S(2)}) copy-start(f32[1,7168]{1,0:T(1,128)} %param.10) | copy-start | bytes 86020
  124.0 7.9 %collective-permute-start.1 = (bf16[8,7168]{1,0:T(8,128)(2,1)S(1)}, bf16[8,7168]{1,0:T(8,128)(2,1)S(1)}, u32[]{:S(2)}, u32[]{:S(2)}) collective-permute-start(bf16[8,7168]{1,0:T(8,128)(2,1)S(1)} %fusion.21), channel_id=1, source_target_pairs={{0,64},{64,128},{128,192},{192,256},{256,320},{320,384},{384,448},... | collective-permute-start | bytes 344072 | tf_op jit(solution)/shard_map/ppermute | solution.py:15
  176.7 2.6 %copy-start.2 = (bf16[5,64,3584]{2,1,0:T(8,128)(2,1)S(1)}, bf16[5,64,3584]{2,1,0:T(8,128)(2,1)}, u32[]{:S(2)}) copy-start(bf16[5,64,3584]{2,1,0:T(8,128)(2,1)} %all-gather.5.cloned.1.call-done) | copy-start | bytes 6881284
  179.3 26.0 %copy-start.6 = (bf16[8,448,128]{2,1,0:T(8,128)(2,1)S(1)}, bf16[8,448,128]{2,1,0:T(8,128)(2,1)}, u32[]{:S(2)}) copy-start(bf16[8,448,128]{2,1,0:T(8,128)(2,1)} %copy-done.5) | copy-start | bytes 2752516
  180.1 7.4 %collective-permute-start.2 = (bf16[2,320,128]{2,1,0:T(8,128)(2,1)S(1)}, bf16[2,320,128]{2,1,0:T(8,128)(2,1)S(1)}, u32[]{:S(2)}, u32[]{:S(2)}) collective-permute-start(bf16[2,320,128]{2,1,0:T(8,128)(2,1)S(1)} %fusion.12), channel_id=1, source_target_pairs={{0,1},{1,0},{2,3},{3,2},{4,5},{5,4},{6,7},{7,6},{8,9},{9,8},{10,11... | collective-permute-start | bytes 491528 | tf_op jit(solution)/shard_map/ppermute | solution.py:15
  207.5 21.9 %all-to-all-start.4 = ((bf16[64,2,1120]{2,1,0:T(2,128)(2,1)}), bf16[64,2,1120]{2,1,0:T(2,128)(2,1)S(1)}, u32[]{:S(2)}, u32[]{:S(2)}) async-start(bf16[64,2,1120]{2,1,0:T(2,128)(2,1)} %reshape.134), calls=%async_computation.4 | async-start | bytes 589824 | tf_op jit(solution)/shard_map/all_to_all | solution.py:72
Sparse Core Ops, SparseCore 0:
  34.6 33.7 all-gather.2
  146.3 30.4 all-gather.4

commit v11 on v10

--- a/solution.py
+++ b/solution.py
@@ -63,7 +63,10 @@
     mine = jnp.stack([gate_part, up_part])
     both = mine + passed_along(mine.astype(jnp.bfloat16), "dp", 1).astype(jnp.float32)
     hidden = (jax.nn.silu(both[0]) * both[1]).astype(jnp.bfloat16)
-    hidden_all = lax.all_gather(hidden, "q", axis=1, tiled=True)
+    units = hidden.shape[1]
+    hidden_all = lax.all_gather(hidden.reshape(capacity, sources, units), "q", axis=1, tiled=True)
+    hidden_all = hidden_all.reshape(capacity, blocks, sources, units).transpose(0, 2, 1, 3)
+    hidden_all = hidden_all.reshape(capacity * sources, blocks * units)
     out = lax.dot_general(
         hidden_all, down_mine, (((1,), (1,)), ((), ())), preferred_element_type=jnp.float32
     ).astype(jnp.bfloat16)

time: 240 us -> 243 us (1.012)
  starting transfers between devices: 29.7 us -> 32.5 us
    all_to_all x2, starting transfers between devices: 14.1 us -> 16.8 us  [moe_layer(): lax.all_to_all(out.reshape(sources, 2, capacity * piece // 2), ALL, split...]
where the time goes in v11:
time: 243 us
  waiting for transfers between devices  99.1 us (41%)
  blocking collectives  68.8 us (28%)
  starting transfers between devices  32.5 us (13%)
  between operations  13.9 us (6%)
  local copies, waits for them, and re-layouts  13.8 us (6%)
  matrix products  10.2 us (4%)
  other arithmetic  4.58 us (2%)
    all_gather x2, waiting for transfers between devices, moe_layer(): arrived = lax.all_gather(arrived, 'q', axis=1, tiled=True)  56.3 us
    all_gather x2, blocking collectives, moe_layer(): lax.all_gather(hidden.reshape(capacity, sources, units), 'q', axis=1, til...  34.4 us
    all_to_all x2, blocking collectives, moe_layer(): lax.all_to_all(send, ('eg', 'dp'), split_axis=0, concat_axis=0, tiled=True)  34.3 us
    all_to_all x2, waiting for transfers between devices, moe_layer(): lax.all_to_all(out.reshape(sources, 2, capacity * piece // 2), ALL, split...  27.6 us
    all_to_all x2, starting transfers between devices, moe_layer(): lax.all_to_all(out.reshape(sources, 2, capacity * piece // 2), ALL, split...  16.8 us
    ppermute x3, waiting for transfers between devices, passed_along(): lax.ppermute(array, axis, [(i, (i + by) % length) for i in range(length)])  15.1 us
    all_to_all x1, starting transfers between devices, on_device(): lax.all_to_all(down_local.reshape(n_blocks, piece, width), 'q', split_axi...  8.2 us
    ppermute x3, starting transfers between devices, passed_along(): lax.ppermute(array, axis, [(i, (i + by) % length) for i in range(length)])  7.5 us
  transfers between devices with their start and end apart: 8, of which 7 were waited for; matrix products, arithmetic and copies ran while one was open for 2% of the time, Pallas kernels for 0%

profile of v11, /device:TPU:1, one launch (start us, length us, event | category | flops | bytes accessed | tf_op | source)
XLA Modules:
  0.0 242.7 jit_solution(7055242202661505565)
XLA Ops:
  6.5 0.8 fusion.40
  8.3 0.7 bitcast_add_fusion.1
  9.1 1.1 fusion.22
  10.2 1.2 convolution_convert_fusion.1
  11.4 0.2 reshape_reshape.6
  11.9 21.8 %all_to_all.25 = bf16[8,140,128]{2,1,0:T(8,128)(2,1)S(1)} all-to-all(bf16[8,140,128]{2,1,0:T(8,128)(2,1)S(1)} %copy.73), channel_id=1, replica_groups=mesh['section'=8,'eg'=4,'q'=8,'dp'=2] {'eg','dp'}, dimensions={0} | all-to-all | bytes 573440 | tf_op jit(solution)/shard_map/all_to_all | solution.py:56
  33.7 0.8 copy.74
  34.5 8.2 %all-to-all-start.1 = ((bf16[8,448,128]{2,1,0:T(8,128)(2,1)}), bf16[8,448,128]{2,1,0:T(8,128)(2,1)S(1)}, u32[]{:S(2)}, u32[]{:S(2)}) async-start(bf16[8,448,128]{2,1,0:T(8,128)(2,1)} %bitcast.18), calls=%async_computation.1 | async-start | bytes 1835008 | tf_op jit(solution)/shard_map/all_to_all | solution.py:93
  42.7 25.7 %all-gather.3.cloned.1.call-done = bf16[5,64,3584]{2,1,0:T(8,128)(2,1)} async-done(((bf16[5,8,3584]{2,1,0:T(8,128)(2,1)}), bf16[5,64,3584]{2,1,0:T(8,128)(2,1)}) %all-gather.3.cloned.1.call-update) | async-done | bytes 2293776 | tf_op jit(solution)/shard_map/all_gather | solution.py:58
  68.5 2.5 %convolution_bitcast_fusion.2 = f32[1,320,128]{2,1,0:T(8,128)S(1)} fusion(bf16[320,3584]{1,0:T(8,128)(2,1)} %bitcast.105, bf16[1,3584,128]{2,1,0:T(8,128)(2,1)S(1)} %copy-done), kind=kOutput, calls=%fused_computation.8 | convolution fusion | flops 293601280 | bytes 3375104 | tf_op jit(solution)/shard_map/dot_general | solution.py:62
  71.0 0.8 convolution_bitcast_fusion.3
  71.8 2.1 collective-permute-start
  73.9 5.3 %collective-permute-done = bf16[2,320,128]{2,1,0:T(8,128)(2,1)S(1)} collective-permute-done((bf16[2,320,128]{2,1,0:T(8,128)(2,1)S(1)}, bf16[2,320,128]{2,1,0:T(8,128)(2,1)S(1)}, u32[]{:S(2)}, u32[]{:S(2)}) %collective-permute-start) | collective-permute-done | bytes 163872 | tf_op jit(solution)/shard_map/ppermute | solution.py:15
  79.3 17.1 %all_gather.13 = bf16[5,512,128]{2,1,0:T(8,128)(2,1)S(1)} all-gather(bf16[5,64,128]{2,1,0:T(8,128)(2,1)S(1)} %multiply_convert_fusion.1), channel_id=1, replica_groups=mesh['section'=8,'eg'=4,'q'=8,'dp'=2] {'q'}, dimensions={1}, use_global_device_ids=true | all-gather | bytes 737280 | tf_op jit(solution)/shard_map/all_gather | solution.py:67
  96.4 0.4 copy.75
  96.9 1.3 convolution_convert_fusion.3
  98.1 1.1 reshape.146
  99.4 1.4 reshape.147
  100.8 7.6 %all-to-all-start.2 = ((bf16[64,2,1120]{2,1,0:T(2,128)(2,1)}), bf16[64,2,1120]{2,1,0:T(2,128)(2,1)S(1)}, u32[]{:S(2)}, u32[]{:S(2)}) async-start(bf16[64,2,1120]{2,1,0:T(2,128)(2,1)} %reshape.147), calls=%async_computation.2 | async-start | bytes 589824 | tf_op jit(solution)/shard_map/all_to_all | solution.py:75
  108.6 13.8 %all-to-all-done.2 = bf16[64,2,1120]{2,1,0:T(2,128)(2,1)S(1)} async-done(((bf16[64,2,1120]{2,1,0:T(2,128)(2,1)}), bf16[64,2,1120]{2,1,0:T(2,128)(2,1)S(1)}, u32[]{:S(2)}, u32[]{:S(2)}) %all-to-all-start.2) | async-done | bytes 286752 | tf_op jit(solution)/shard_map/all_to_all | solution.py:75
  122.3 0.6 reshape.148
  123.2 0.4 reshape.149
  123.6 0.7 gather_fusion
  124.4 0.3 reshape.160
  124.6 0.6 multiply_reduce_fusion.1
  125.3 3.1 %collective-permute-start.1 = (bf16[8,7168]{1,0:T(8,128)(2,1)S(1)}, bf16[8,7168]{1,0:T(8,128)(2,1)S(1)}, u32[]{:S(2)}, u32[]{:S(2)}) collective-permute-start(bf16[8,7168]{1,0:T(8,128)(2,1)S(1)} %fusion.25), channel_id=1, source_target_pairs={{0,64},{64,128},{128,192},{192,256},{256,320},{320,384},{384,448},... | collective-permute-start | bytes 344072 | tf_op jit(solution)/shard_map/ppermute | solution.py:15
  128.5 4.7 %collective-permute-done.1 = bf16[8,7168]{1,0:T(8,128)(2,1)S(1)} collective-permute-done((bf16[8,7168]{1,0:T(8,128)(2,1)S(1)}, bf16[8,7168]{1,0:T(8,128)(2,1)S(1)}, u32[]{:S(2)}, u32[]{:S(2)}) %collective-permute-start.1) | collective-permute-done | bytes 114720 | tf_op jit(solution)/shard_map/ppermute | solution.py:15
  133.4 0.3 convolution_convert_fusion
  133.7 0.2 reshape_reshape.7
  134.2 12.5 %all_to_all.26 = bf16[8,140,128]{2,1,0:T(8,128)(2,1)S(1)} all-to-all(bf16[8,140,128]{2,1,0:T(8,128)(2,1)S(1)} %copy.83), channel_id=1, replica_groups=mesh['section'=8,'eg'=4,'q'=8,'dp'=2] {'eg','dp'}, dimensions={0} | all-to-all | bytes 573440 | tf_op jit(solution)/shard_map/all_to_all | solution.py:56
  146.7 0.8 copy.84
  147.5 30.6 %all-gather.5.cloned.1.call-done = bf16[5,64,3584]{2,1,0:T(8,128)(2,1)} async-done(((bf16[5,8,3584]{2,1,0:T(8,128)(2,1)}), bf16[5,64,3584]{2,1,0:T(8,128)(2,1)}) %all-gather.5.cloned.1.call-update) | async-done | bytes 2293776 | tf_op jit(solution)/shard_map/all_gather | solution.py:58
  178.1 2.5 %convolution_bitcast_fusion = f32[1,320,128]{2,1,0:T(8,128)S(1)} fusion(bf16[320,3584]{1,0:T(8,128)(2,1)} %bitcast.107, bf16[1,3584,128]{2,1,0:T(8,128)(2,1)S(1)} %copy-done), kind=kOutput, calls=%fused_computation.6 | convolution fusion | flops 293601280 | bytes 3375104 | tf_op jit(solution)/shard_map/dot_general | solution.py:62
  180.7 0.8 convolution_bitcast_fusion.1
  181.5 2.3 collective-permute-start.2
  183.8 5.2 %collective-permute-done.2 = bf16[2,320,128]{2,1,0:T(8,128)(2,1)S(1)} collective-permute-done((bf16[2,320,128]{2,1,0:T(8,128)(2,1)S(1)}, bf16[2,320,128]{2,1,0:T(8,128)(2,1)S(1)}, u32[]{:S(2)}, u32[]{:S(2)}) %collective-permute-start.2) | collective-permute-done | bytes 163872 | tf_op jit(solution)/shard_map/ppermute | solution.py:15
  189.1 17.4 %all_gather.15 = bf16[5,512,128]{2,1,0:T(8,128)(2,1)S(1)} all-gather(bf16[5,64,128]{2,1,0:T(8,128)(2,1)S(1)} %multiply_convert_fusion), channel_id=1, replica_groups=mesh['section'=8,'eg'=4,'q'=8,'dp'=2] {'q'}, dimensions={1}, use_global_device_ids=true | all-gather | bytes 737280 | tf_op jit(solution)/shard_map/all_gather | solution.py:67
  206.5 0.4 copy.85
  206.9 0.5 convolution_convert_fusion.2
  207.8 1.4 reshape.156
  209.2 9.2 %all-to-all-start.4 = ((bf16[64,2,1120]{2,1,0:T(2,128)(2,1)}), bf16[64,2,1120]{2,1,0:T(2,128)(2,1)S(1)}, u32[]{:S(2)}, u32[]{:S(2)}) async-start(bf16[64,2,1120]{2,1,0:T(2,128)(2,1)} %reshape.156), calls=%async_computation.4 | async-start | bytes 589824 | tf_op jit(solution)/shard_map/all_to_all | solution.py:75
  218.5 13.8 %all-to-all-done.4 = bf16[64,2,1120]{2,1,0:T(2,128)(2,1)S(1)} async-done(((bf16[64,2,1120]{2,1,0:T(2,128)(2,1)}), bf16[64,2,1120]{2,1,0:T(2,128)(2,1)S(1)}, u32[]{:S(2)}, u32[]{:S(2)}) %all-to-all-start.4) | async-done | bytes 286752 | tf_op jit(solution)/shard_map/all_to_all | solution.py:75
  232.3 0.6 reshape.157
  233.1 0.4 reshape.158
  233.5 0.7 gather_fusion.1
  234.3 0.3 reshape.161
  234.6 0.6 multiply_reduce_fusion
  235.2 0.7 fusion.27
  (67 shorter events, 3.6 us)
Async XLA Ops:
  6.5 61.9 %copy-start = (bf16[1,3584,128]{2,1,0:T(8,128)(2,1)S(1)}, bf16[1,3584,128]{2,1,0:T(8,128)(2,1)}, u32[]{:S(2)}) copy-start(bf16[1,3584,128]{2,1,0:T(8,128)(2,1)} %param.12) | copy-start | bytes 2752516
  6.5 61.9 %all-gather.3.cloned.1.call-start = ((), (), s32[]{:S(2)}) async-start(), calls=%async_computation.5 | async-start | bytes 2580480 | tf_op jit(solution)/shard_map/all_gather | solution.py:58
  34.5 62.3 %all-to-all-start.1 = ((bf16[8,448,128]{2,1,0:T(8,128)(2,1)}), bf16[8,448,128]{2,1,0:T(8,128)(2,1)S(1)}, u32[]{:S(2)}, u32[]{:S(2)}) async-start(bf16[8,448,128]{2,1,0:T(8,128)(2,1)} %bitcast.18), calls=%async_computation.1 | async-start | bytes 1835008 | tf_op jit(solution)/shard_map/all_to_all | solution.py:93
  42.7 28.3 %copy-start.3 = (bf16[1,3584,128]{2,1,0:T(8,128)(2,1)S(1)}, bf16[1,3584,128]{2,1,0:T(8,128)(2,1)}, u32[]{:S(2)}) copy-start(bf16[1,3584,128]{2,1,0:T(8,128)(2,1)} %param.11) | copy-start | bytes 2752516
  68.5 2.6 %copy-start.1 = (bf16[5,64,3584]{2,1,0:T(8,128)(2,1)S(1)}, bf16[5,64,3584]{2,1,0:T(8,128)(2,1)}, u32[]{:S(2)}) copy-start(bf16[5,64,3584]{2,1,0:T(8,128)(2,1)} %all-gather.3.cloned.1.call-done) | copy-start | bytes 6881284
  71.8 7.4 %collective-permute-start = (bf16[2,320,128]{2,1,0:T(8,128)(2,1)S(1)}, bf16[2,320,128]{2,1,0:T(8,128)(2,1)S(1)}, u32[]{:S(2)}, u32[]{:S(2)}) collective-permute-start(bf16[2,320,128]{2,1,0:T(8,128)(2,1)S(1)} %fusion.17), channel_id=1, source_target_pairs={{0,1},{1,0},{2,3},{3,2},{4,5},{5,4},{6,7},{7,6},{8,9},{9,8},{10,11... | collective-permute-start | bytes 491528 | tf_op jit(solution)/shard_map/ppermute | solution.py:15
  96.8 1.3 copy-start.5
  96.8 11.6 %copy-start.8 = (f32[1,2,8,2]{2,3,1,0:T(2,128)S(1)}, f32[1,2,8,2]{2,3,1,0:T(2,128)}, u32[]{:S(2)}) copy-start(f32[1,2,8,2]{2,3,1,0:T(2,128)} %param.15) | copy-start | bytes 388
  100.8 21.5 %all-to-all-start.2 = ((bf16[64,2,1120]{2,1,0:T(2,128)(2,1)}), bf16[64,2,1120]{2,1,0:T(2,128)(2,1)S(1)}, u32[]{:S(2)}, u32[]{:S(2)}) async-start(bf16[64,2,1120]{2,1,0:T(2,128)(2,1)} %reshape.147), calls=%async_computation.2 | async-start | bytes 589824 | tf_op jit(solution)/shard_map/all_to_all | solution.py:75
  108.4 69.7 %all-gather.5.cloned.1.call-start = ((), (), s32[]{:S(2)}) async-start(), calls=%async_computation.6 | async-start | bytes 2580480 | tf_op jit(solution)/shard_map/all_gather | solution.py:58
  123.5 1.7 copy-start.4
  123.5 9.8 %copy-start.7 = (f32[1,7168]{1,0:T(1,128)S(1)}, f32[1,7168]{1,0:T(1,128)}, u32[]{:S(2)}) copy-start(f32[1,7168]{1,0:T(1,128)} %param.10) | copy-start | bytes 86020
  125.3 7.9 %collective-permute-start.1 = (bf16[8,7168]{1,0:T(8,128)(2,1)S(1)}, bf16[8,7168]{1,0:T(8,128)(2,1)S(1)}, u32[]{:S(2)}, u32[]{:S(2)}) collective-permute-start(bf16[8,7168]{1,0:T(8,128)(2,1)S(1)} %fusion.25), channel_id=1, source_target_pairs={{0,64},{64,128},{128,192},{192,256},{256,320},{320,384},{384,448},... | collective-permute-start | bytes 344072 | tf_op jit(solution)/shard_map/ppermute | solution.py:15
  178.1 2.6 %copy-start.2 = (bf16[5,64,3584]{2,1,0:T(8,128)(2,1)S(1)}, bf16[5,64,3584]{2,1,0:T(8,128)(2,1)}, u32[]{:S(2)}) copy-start(bf16[5,64,3584]{2,1,0:T(8,128)(2,1)} %all-gather.5.cloned.1.call-done) | copy-start | bytes 6881284
  181.4 25.5 %copy-start.6 = (bf16[8,448,128]{2,1,0:T(8,128)(2,1)S(1)}, bf16[8,448,128]{2,1,0:T(8,128)(2,1)}, u32[]{:S(2)}) copy-start(bf16[8,448,128]{2,1,0:T(8,128)(2,1)} %copy-done.5) | copy-start | bytes 2752516
  181.5 7.5 %collective-permute-start.2 = (bf16[2,320,128]{2,1,0:T(8,128)(2,1)S(1)}, bf16[2,320,128]{2,1,0:T(8,128)(2,1)S(1)}, u32[]{:S(2)}, u32[]{:S(2)}) collective-permute-start(bf16[2,320,128]{2,1,0:T(8,128)(2,1)S(1)} %fusion.16), channel_id=1, source_target_pairs={{0,1},{1,0},{2,3},{3,2},{4,5},{5,4},{6,7},{7,6},{8,9},{9,8},{10,11... | collective-permute-start | bytes 491528 | tf_op jit(solution)/shard_map/ppermute | solution.py:15
  209.2 23.1 %all-to-all-start.4 = ((bf16[64,2,1120]{2,1,0:T(2,128)(2,1)}), bf16[64,2,1120]{2,1,0:T(2,128)(2,1)S(1)}, u32[]{:S(2)}, u32[]{:S(2)}) async-start(bf16[64,2,1120]{2,1,0:T(2,128)(2,1)} %reshape.156), calls=%async_computation.4 | async-start | bytes 589824 | tf_op jit(solution)/shard_map/all_to_all | solution.py:75
Sparse Core Ops, SparseCore 0:
  34.6 33.7 all-gather.2
  147.7 30.4 all-gather.4

commit v12 on v10

--- a/solution.py
+++ b/solution.py
@@ -52,15 +52,16 @@
     lanes = 128
     tiles = half // lanes
     send = outgoing.reshape(experts, capacity, halves, tiles, lanes).transpose(0, 2, 1, 3, 4)
-    send = send.reshape(experts * halves, capacity * tiles, lanes)
+    send = send.reshape(experts * halves, 2, capacity * half // 2)
     arrived = lax.all_to_all(send, ("eg", "dp"), split_axis=0, concat_axis=0, tiled=True)
     arrived = arrived.reshape(experts * halves, capacity, half).transpose(1, 0, 2)
     arrived = lax.all_gather(arrived, "q", axis=1, tiled=True)
     sources = blocks * experts * halves
     rows = arrived.reshape(capacity * sources, half)
-    gate_part = jnp.dot(rows, gate_w, preferred_element_type=jnp.float32)
-    up_part = jnp.dot(rows, up_w, preferred_element_type=jnp.float32)
-    mine = jnp.stack([gate_part, up_part])
+    units = gate_w.shape[1]
+    both_w = jnp.concatenate([gate_w, up_w], axis=1)
+    gate_up = jnp.dot(rows, both_w, preferred_element_type=jnp.float32)
+    mine = gate_up.reshape(rows.shape[0], 2, units).transpose(1, 0, 2)
     both = mine + passed_along(mine.astype(jnp.bfloat16), "dp", 1).astype(jnp.float32)
     hidden = (jax.nn.silu(both[0]) * both[1]).astype(jnp.bfloat16)
     hidden_all = lax.all_gather(hidden, "q", axis=1, tiled=True)

time: 240 us -> 240 us (level)
  waiting for transfers between devices: 99.1 us -> 94.7 us
    all_gather x2, waiting for transfers between devices: 56.3 us -> 52.1 us  [moe_layer(): arrived = lax.all_gather(arrived, 'q', axis=1, tiled=True)]
    dot_general x0 -> x1, local copies, waits for them, and re-layouts: none -> 2.65 us  [moe_layer(): gate_up = jnp.dot(rows, both_w, preferred_element_type=jnp.float32)]
    dot_general x4 -> x2, matrix products: 6.59 us -> 5.41 us  [moe_layer(): gate_up = jnp.dot(rows, both_w, preferred_element_type=jnp.float32)]
  transfers between devices with their start and end apart: 8 -> 8, of which waited for: 7 -> 7; matrix products, arithmetic and copies ran while one was open for 2% -> 3% of each run, Pallas kernels for 0% -> 0%
where the time goes in v12:
time: 240 us; the launch traced here: 239 us
  waiting for transfers between devices  94.7 us (39%)
  blocking collectives  69.8 us (29%)
  starting transfers between devices  29.6 us (12%)
  local copies, waits for them, and re-layouts  14.7 us (6%)
  between operations  13.8 us (6%)
  matrix products  10.6 us (4%)
  other arithmetic  5.94 us (2%)
    all_gather x2, waiting for transfers between devices, moe_layer(): arrived = lax.all_gather(arrived, 'q', axis=1, tiled=True)  52.1 us
    all_gather x2, blocking collectives, moe_layer(): hidden_all = lax.all_gather(hidden, 'q', axis=1, tiled=True)  35.3 us
    all_to_all x2, blocking collectives, moe_layer(): lax.all_to_all(send, ('eg', 'dp'), split_axis=0, concat_axis=0, tiled=True)  34.5 us
    all_to_all x2, waiting for transfers between devices, moe_layer(): lax.all_to_all(out.reshape(sources, 2, capacity * piece // 2), ALL, split...  27.6 us
    ppermute x3, waiting for transfers between devices, passed_along(): lax.ppermute(array, axis, [(i, (i + by) % length) for i in range(length)])  14.9 us
    all_to_all x2, starting transfers between devices, moe_layer(): lax.all_to_all(out.reshape(sources, 2, capacity * piece // 2), ALL, split...  13.9 us
    all_to_all x1, starting transfers between devices, on_device(): lax.all_to_all(down_local.reshape(n_blocks, piece, width), 'q', split_axi...  8.1 us
    ppermute x3, starting transfers between devices, passed_along(): lax.ppermute(array, axis, [(i, (i + by) % length) for i in range(length)])  7.57 us
  transfers between devices with their start and end apart: 8, of which 7 were waited for; matrix products, arithmetic and copies ran while one was open for 3% of the time, Pallas kernels for 0%

profile of v12, /device:TPU:1, one launch (start us, length us, event | category | flops | bytes accessed | tf_op | source)
XLA Modules:
  0.0 239.2 jit_solution(17253363982797982586)
XLA Ops:
  6.5 0.7 fusion.32
  8.2 0.7 bitcast_add_fusion.1
  9.0 1.1 fusion.12
  10.1 1.2 convolution_convert_fusion.1
  11.3 0.2 reshape_reshape.6
  11.7 21.9 %all_to_all.25 = bf16[8,2,8960]{2,1,0:T(2,128)(2,1)S(1)} all-to-all(bf16[8,2,8960]{2,1,0:T(2,128)(2,1)S(1)} %reshape.126), channel_id=1, replica_groups=mesh['section'=8,'eg'=4,'q'=8,'dp'=2] {'eg','dp'}, dimensions={0} | all-to-all | bytes 573440 | tf_op jit(solution)/shard_map/all_to_all | solution.py:56
  33.6 0.2 reshape.127
  33.8 0.8 copy.57
  34.6 8.1 %all-to-all-start.1 = ((bf16[8,448,128]{2,1,0:T(8,128)(2,1)}), bf16[8,448,128]{2,1,0:T(8,128)(2,1)}, u32[]{:S(2)}, u32[]{:S(2)}) async-start(bf16[8,448,128]{2,1,0:T(8,128)(2,1)} %bitcast.16), calls=%async_computation.1 | async-start | bytes 1835008 | tf_op jit(solution)/shard_map/all_to_all | solution.py:91
  42.7 1.4 maximum_bitcast_fusion
  44.1 2.7 %copy.58 = bf16[256,3584]{1,0:T(8,128)(2,1)} copy(bf16[256,3584]{0,1:T(8,128)(2,1)S(1)} %maximum_bitcast_fusion) | data formatting | bytes 3670016 | tf_op jit(solution)/shard_map/dot_general | solution.py:63
  46.8 21.7 %all-gather.3.cloned.1.call-done = bf16[5,64,3584]{2,1,0:T(8,128)(2,1)} async-done(((bf16[5,8,3584]{2,1,0:T(8,128)(2,1)}), bf16[5,64,3584]{2,1,0:T(8,128)(2,1)}) %all-gather.3.cloned.1.call-update) | async-done | bytes 2293776 | tf_op jit(solution)/shard_map/all_gather | solution.py:58
  68.5 3.0 %fusion.33 = (bf16[2,320,128]{2,1,0:T(8,128)(2,1)S(1)}, f32[2,320,128]{2,1,0:T(8,128)S(1)}) fusion(bf16[320,3584,1]{1,0,2:T(8,128)(2,1)} %bitcast.110, bf16[2,128,3584]{2,1,0:T(8,128)(2,1)} %bitcast.100), kind=kOutput, calls=%fused_computation.77 | convolution fusion | flops 587284480 | bytes 4620288 | tf_op jit(solution)/shard_map/dot_general | solution.py:63
  71.5 2.3 collective-permute-start
  73.8 5.1 %collective-permute-done = bf16[2,320,128]{2,1,0:T(8,128)(2,1)S(1)} collective-permute-done((bf16[2,320,128]{2,1,0:T(8,128)(2,1)S(1)}, bf16[2,320,128]{2,1,0:T(8,128)(2,1)S(1)}, u32[]{:S(2)}, u32[]{:S(2)}) %collective-permute-start) | collective-permute-done | bytes 163872 | tf_op jit(solution)/shard_map/ppermute | solution.py:15
  79.0 17.6 %all_gather.13 = bf16[320,1024]{1,0:T(8,128)(2,1)S(1)} all-gather(bf16[320,128]{1,0:T(8,128)(2,1)S(1)} %fusion.19), channel_id=1, replica_groups=mesh['section'=8,'eg'=4,'q'=8,'dp'=2] {'q'}, dimensions={1}, use_global_device_ids=true | all-gather | bytes 737280 | tf_op jit(solution)/shard_map/all_gather | solution.py:67
  96.6 1.7 convolution_convert_fusion.3
  98.7 1.4 reshape.131
  100.1 6.1 %all-to-all-start.2 = ((bf16[64,2,1120]{2,1,0:T(2,128)(2,1)}), bf16[64,2,1120]{2,1,0:T(2,128)(2,1)S(1)}, u32[]{:S(2)}, u32[]{:S(2)}) async-start(bf16[64,2,1120]{2,1,0:T(2,128)(2,1)} %reshape.131), calls=%async_computation.2 | async-start | bytes 589824 | tf_op jit(solution)/shard_map/all_to_all | solution.py:73
  106.4 13.8 %all-to-all-done.2 = bf16[64,2,1120]{2,1,0:T(2,128)(2,1)S(1)} async-done(((bf16[64,2,1120]{2,1,0:T(2,128)(2,1)}), bf16[64,2,1120]{2,1,0:T(2,128)(2,1)S(1)}, u32[]{:S(2)}, u32[]{:S(2)}) %all-to-all-start.2) | async-done | bytes 286752 | tf_op jit(solution)/shard_map/all_to_all | solution.py:73
  120.1 0.6 reshape.132
  120.7 0.2 copy.61
  121.0 0.4 reshape.133
  121.4 0.7 gather_fusion
  122.2 0.3 reshape.142
  122.4 0.6 multiply_reduce_fusion.1
  123.1 3.1 %collective-permute-start.1 = (bf16[8,7168]{1,0:T(8,128)(2,1)S(1)}, bf16[8,7168]{1,0:T(8,128)(2,1)S(1)}, u32[]{:S(2)}, u32[]{:S(2)}) collective-permute-start(bf16[8,7168]{1,0:T(8,128)(2,1)S(1)} %fusion.15), channel_id=1, source_target_pairs={{0,64},{64,128},{128,192},{192,256},{256,320},{320,384},{384,448},... | collective-permute-start | bytes 344072 | tf_op jit(solution)/shard_map/ppermute | solution.py:15
  126.3 4.7 %collective-permute-done.1 = bf16[8,7168]{1,0:T(8,128)(2,1)S(1)} collective-permute-done((bf16[8,7168]{1,0:T(8,128)(2,1)S(1)}, bf16[8,7168]{1,0:T(8,128)(2,1)S(1)}, u32[]{:S(2)}, u32[]{:S(2)}) %collective-permute-start.1) | collective-permute-done | bytes 114720 | tf_op jit(solution)/shard_map/ppermute | solution.py:15
  131.2 0.3 convolution_convert_fusion
  131.5 0.2 reshape_reshape.7
  131.9 12.6 %all_to_all.26 = bf16[8,2,8960]{2,1,0:T(2,128)(2,1)S(1)} all-to-all(bf16[8,2,8960]{2,1,0:T(2,128)(2,1)S(1)} %reshape.134), channel_id=1, replica_groups=mesh['section'=8,'eg'=4,'q'=8,'dp'=2] {'eg','dp'}, dimensions={0} | all-to-all | bytes 573440 | tf_op jit(solution)/shard_map/all_to_all | solution.py:56
  144.7 0.8 copy.66
  145.5 30.4 %all-gather.5.cloned.1.call-done = bf16[5,64,3584]{2,1,0:T(8,128)(2,1)} async-done(((bf16[5,8,3584]{2,1,0:T(8,128)(2,1)}), bf16[5,64,3584]{2,1,0:T(8,128)(2,1)}) %all-gather.5.cloned.1.call-update) | async-done | bytes 2293776 | tf_op jit(solution)/shard_map/all_gather | solution.py:58
  175.9 2.4 %fusion.34 = (bf16[2,320,128]{2,1,0:T(8,128)(2,1)S(1)}, f32[2,320,128]{2,1,0:T(8,128)S(1)}) fusion(bf16[320,3584,1]{1,0,2:T(8,128)(2,1)} %bitcast.111, bf16[2,128,3584]{2,1,0:T(8,128)(2,1)S(1)} %bitcast.101), kind=kOutput, calls=%fused_computation.78 | convolution fusion | flops 587284480 | bytes 4620288 | tf_op jit(solution)/shard_map/dot_general | solution.py:63
  178.3 2.2 collective-permute-start.2
  180.5 5.2 %collective-permute-done.2 = bf16[2,320,128]{2,1,0:T(8,128)(2,1)S(1)} collective-permute-done((bf16[2,320,128]{2,1,0:T(8,128)(2,1)S(1)}, bf16[2,320,128]{2,1,0:T(8,128)(2,1)S(1)}, u32[]{:S(2)}, u32[]{:S(2)}) %collective-permute-start.2) | collective-permute-done | bytes 163872 | tf_op jit(solution)/shard_map/ppermute | solution.py:15
  185.8 17.7 %all_gather.15 = bf16[320,1024]{1,0:T(8,128)(2,1)S(1)} all-gather(bf16[320,128]{1,0:T(8,128)(2,1)S(1)} %fusion.17), channel_id=1, replica_groups=mesh['section'=8,'eg'=4,'q'=8,'dp'=2] {'q'}, dimensions={1}, use_global_device_ids=true | all-gather | bytes 737280 | tf_op jit(solution)/shard_map/all_gather | solution.py:67
  203.5 1.7 convolution_convert_fusion.2
  205.6 1.4 reshape.138
  207.0 7.8 %all-to-all-start.4 = ((bf16[64,2,1120]{2,1,0:T(2,128)(2,1)}), bf16[64,2,1120]{2,1,0:T(2,128)(2,1)S(1)}, u32[]{:S(2)}, u32[]{:S(2)}) async-start(bf16[64,2,1120]{2,1,0:T(2,128)(2,1)} %reshape.138), calls=%async_computation.4 | async-start | bytes 589824 | tf_op jit(solution)/shard_map/all_to_all | solution.py:73
  214.9 13.8 %all-to-all-done.4 = bf16[64,2,1120]{2,1,0:T(2,128)(2,1)S(1)} async-done(((bf16[64,2,1120]{2,1,0:T(2,128)(2,1)}), bf16[64,2,1120]{2,1,0:T(2,128)(2,1)S(1)}, u32[]{:S(2)}, u32[]{:S(2)}) %all-to-all-start.4) | async-done | bytes 286752 | tf_op jit(solution)/shard_map/all_to_all | solution.py:73
  228.7 0.6 reshape.139
  229.3 0.2 copy.68
  229.5 0.4 reshape.140
  229.9 0.7 gather_fusion.1
  230.7 0.3 reshape.143
  231.0 0.6 multiply_reduce_fusion
  231.6 0.7 fusion.21
  (55 shorter events, 3.2 us)
Async XLA Ops:
  6.5 62.0 %all-gather.3.cloned.1.call-start = ((), (), s32[]{:S(2)}) async-start(), calls=%async_computation.5 | async-start | bytes 2580480 | tf_op jit(solution)/shard_map/all_gather | solution.py:58
  11.6 31.2 %copy-start.2 = (bf16[1,3584,128]{2,1,0:T(8,128)(2,1)S(1)}, bf16[1,3584,128]{2,1,0:T(8,128)(2,1)}, u32[]{:S(2)}) copy-start(bf16[1,3584,128]{2,1,0:T(8,128)(2,1)} %param.12) | copy-start | bytes 2752516
  34.6 62.0 %all-to-all-start.1 = ((bf16[8,448,128]{2,1,0:T(8,128)(2,1)}), bf16[8,448,128]{2,1,0:T(8,128)(2,1)}, u32[]{:S(2)}, u32[]{:S(2)}) async-start(bf16[8,448,128]{2,1,0:T(8,128)(2,1)} %bitcast.16), calls=%async_computation.1 | async-start | bytes 1835008 | tf_op jit(solution)/shard_map/all_to_all | solution.py:91
  71.5 7.4 %collective-permute-start = (bf16[2,320,128]{2,1,0:T(8,128)(2,1)S(1)}, bf16[2,320,128]{2,1,0:T(8,128)(2,1)S(1)}, u32[]{:S(2)}, u32[]{:S(2)}) collective-permute-start(bf16[2,320,128]{2,1,0:T(8,128)(2,1)S(1)} %get-tuple-element.16), channel_id=1, source_target_pairs={{0,1},{1,0},{2,3},{3,2},{4,5},{5,4},{6,7},{7,6},{8,9},{9,8},{10,11... | collective-permute-start | bytes 491528 | tf_op jit(solution)/shard_map/ppermute | solution.py:15
  96.6 9.6 %copy-start.4 = (f32[1,2,8,2]{2,3,1,0:T(2,128)S(1)}, f32[1,2,8,2]{2,3,1,0:T(2,128)}, u32[]{:S(2)}) copy-start(f32[1,2,8,2]{2,3,1,0:T(2,128)} %param.15) | copy-start | bytes 388
  100.1 20.1 %all-to-all-start.2 = ((bf16[64,2,1120]{2,1,0:T(2,128)(2,1)}), bf16[64,2,1120]{2,1,0:T(2,128)(2,1)S(1)}, u32[]{:S(2)}, u32[]{:S(2)}) async-start(bf16[64,2,1120]{2,1,0:T(2,128)(2,1)} %reshape.131), calls=%async_computation.2 | async-start | bytes 589824 | tf_op jit(solution)/shard_map/all_to_all | solution.py:73
  106.2 69.7 %all-gather.5.cloned.1.call-start = ((), (), s32[]{:S(2)}) async-start(), calls=%async_computation.6 | async-start | bytes 2580480 | tf_op jit(solution)/shard_map/all_gather | solution.py:58
  121.3 1.7 copy-start.1
  121.3 9.8 %copy-start.3 = (f32[1,7168]{1,0:T(1,128)S(1)}, f32[1,7168]{1,0:T(1,128)}, u32[]{:S(2)}) copy-start(f32[1,7168]{1,0:T(1,128)} %param.10) | copy-start | bytes 86020
  123.1 7.9 %collective-permute-start.1 = (bf16[8,7168]{1,0:T(8,128)(2,1)S(1)}, bf16[8,7168]{1,0:T(8,128)(2,1)S(1)}, u32[]{:S(2)}, u32[]{:S(2)}) collective-permute-start(bf16[8,7168]{1,0:T(8,128)(2,1)S(1)} %fusion.15), channel_id=1, source_target_pairs={{0,64},{64,128},{128,192},{192,256},{256,320},{320,384},{384,448},... | collective-permute-start | bytes 344072 | tf_op jit(solution)/shard_map/ppermute | solution.py:15
  131.2 44.7 %copy-start = (bf16[256,3584]{1,0:T(8,128)(2,1)S(1)}, bf16[256,3584]{1,0:T(8,128)(2,1)}, u32[]{:S(2)}) copy-start(bf16[256,3584]{1,0:T(8,128)(2,1)} %copy.58) | copy-start | bytes 5505028
  178.3 7.4 %collective-permute-start.2 = (bf16[2,320,128]{2,1,0:T(8,128)(2,1)S(1)}, bf16[2,320,128]{2,1,0:T(8,128)(2,1)S(1)}, u32[]{:S(2)}, u32[]{:S(2)}) collective-permute-start(bf16[2,320,128]{2,1,0:T(8,128)(2,1)S(1)} %get-tuple-element.18), channel_id=1, source_target_pairs={{0,1},{1,0},{2,3},{3,2},{4,5},{5,4},{6,7},{7,6},{8,9},{9,8},{10,11... | collective-permute-start | bytes 491528 | tf_op jit(solution)/shard_map/ppermute | solution.py:15
  207.0 21.7 %all-to-all-start.4 = ((bf16[64,2,1120]{2,1,0:T(2,128)(2,1)}), bf16[64,2,1120]{2,1,0:T(2,128)(2,1)S(1)}, u32[]{:S(2)}, u32[]{:S(2)}) async-start(bf16[64,2,1120]{2,1,0:T(2,128)(2,1)} %reshape.138), calls=%async_computation.4 | async-start | bytes 589824 | tf_op jit(solution)/shard_map/all_to_all | solution.py:73
Sparse Core Ops, SparseCore 0:
  34.8 33.7 all-gather.2
  145.6 30.2 all-gather.4

commit v13 on v12

--- a/solution.py
+++ b/solution.py
@@ -52,7 +52,7 @@
     lanes = 128
     tiles = half // lanes
     send = outgoing.reshape(experts, capacity, halves, tiles, lanes).transpose(0, 2, 1, 3, 4)
-    send = send.reshape(experts * halves, 2, capacity * half // 2)
+    send = send.reshape(experts * halves, capacity * tiles, lanes)
     arrived = lax.all_to_all(send, ("eg", "dp"), split_axis=0, concat_axis=0, tiled=True)
     arrived = arrived.reshape(experts * halves, capacity, half).transpose(1, 0, 2)
     arrived = lax.all_gather(arrived, "q", axis=1, tiled=True)

time: 240 us -> 240 us (level)
  no operation moved by 1% of the time
where the time goes in v13:
time: 240 us; the launch traced here: 239 us
  waiting for transfers between devices  94.7 us (39%)
  blocking collectives  69.7 us (29%)
  starting transfers between devices  29.9 us (12%)
  local copies, waits for them, and re-layouts  14.5 us (6%)
  between operations  13.8 us (6%)
  matrix products  10.6 us (4%)
  other arithmetic  5.96 us (2%)
    all_gather x2, waiting for transfers between devices, moe_layer(): arrived = lax.all_gather(arrived, 'q', axis=1, tiled=True)  52.3 us
    all_gather x2, blocking collectives, moe_layer(): hidden_all = lax.all_gather(hidden, 'q', axis=1, tiled=True)  35.4 us
    all_to_all x2, blocking collectives, moe_layer(): lax.all_to_all(send, ('eg', 'dp'), split_axis=0, concat_axis=0, tiled=True)  34.3 us
    all_to_all x2, waiting for transfers between devices, moe_layer(): lax.all_to_all(out.reshape(sources, 2, capacity * piece // 2), ALL, split...  27.6 us
    ppermute x3, waiting for transfers between devices, passed_along(): lax.ppermute(array, axis, [(i, (i + by) % length) for i in range(length)])  14.8 us
    all_to_all x2, starting transfers between devices, moe_layer(): lax.all_to_all(out.reshape(sources, 2, capacity * piece // 2), ALL, split...  13.9 us
    all_to_all x1, starting transfers between devices, on_device(): lax.all_to_all(down_local.reshape(n_blocks, piece, width), 'q', split_axi...  8.2 us
    ppermute x3, starting transfers between devices, passed_along(): lax.ppermute(array, axis, [(i, (i + by) % length) for i in range(length)])  7.77 us
  transfers between devices with their start and end apart: 8, of which 7 were waited for; matrix products, arithmetic and copies ran while one was open for 3% of the time, Pallas kernels for 0%

profile of v13, /device:TPU:1, one launch (start us, length us, event | category | flops | bytes accessed | tf_op | source)
XLA Modules:
  0.0 239.2 jit_solution(13683018786179740672)
XLA Ops:
  6.5 0.7 fusion.32
  8.2 0.7 bitcast_add_fusion.1
  9.0 1.1 fusion.12
  10.1 1.2 convolution_convert_fusion.1
  11.3 0.2 reshape_reshape.6
  11.5 0.2 copy.56
  11.8 21.8 %all_to_all.25 = bf16[8,140,128]{2,1,0:T(8,128)(2,1)S(1)} all-to-all(bf16[8,140,128]{2,1,0:T(8,128)(2,1)S(1)} %copy.57), channel_id=1, replica_groups=mesh['section'=8,'eg'=4,'q'=8,'dp'=2] {'eg','dp'}, dimensions={0} | all-to-all | bytes 573440 | tf_op jit(solution)/shard_map/all_to_all | solution.py:56
  33.6 0.8 copy.58
  34.4 8.2 %all-to-all-start.1 = ((bf16[8,448,128]{2,1,0:T(8,128)(2,1)}), bf16[8,448,128]{2,1,0:T(8,128)(2,1)}, u32[]{:S(2)}, u32[]{:S(2)}) async-start(bf16[8,448,128]{2,1,0:T(8,128)(2,1)} %bitcast.18), calls=%async_computation.1 | async-start | bytes 1835008 | tf_op jit(solution)/shard_map/all_to_all | solution.py:91
  42.6 1.4 maximum_bitcast_fusion
  44.0 2.7 %copy.59 = bf16[256,3584]{1,0:T(8,128)(2,1)} copy(bf16[256,3584]{0,1:T(8,128)(2,1)S(1)} %maximum_bitcast_fusion) | data formatting | bytes 3670016 | tf_op jit(solution)/shard_map/dot_general | solution.py:63
  46.7 21.7 %all-gather.3.cloned.1.call-done = bf16[5,64,3584]{2,1,0:T(8,128)(2,1)} async-done(((bf16[5,8,3584]{2,1,0:T(8,128)(2,1)}), bf16[5,64,3584]{2,1,0:T(8,128)(2,1)}) %all-gather.3.cloned.1.call-update) | async-done | bytes 2293776 | tf_op jit(solution)/shard_map/all_gather | solution.py:58
  68.4 3.0 %fusion.33 = (bf16[2,320,128]{2,1,0:T(8,128)(2,1)S(1)}, f32[2,320,128]{2,1,0:T(8,128)S(1)}) fusion(bf16[320,3584,1]{1,0,2:T(8,128)(2,1)} %bitcast.118, bf16[2,128,3584]{2,1,0:T(8,128)(2,1)} %bitcast.106), kind=kOutput, calls=%fused_computation.77 | convolution fusion | flops 587284480 | bytes 4620288 | tf_op jit(solution)/shard_map/dot_general | solution.py:63
  71.3 2.3 collective-permute-start
  73.7 5.0 %collective-permute-done = bf16[2,320,128]{2,1,0:T(8,128)(2,1)S(1)} collective-permute-done((bf16[2,320,128]{2,1,0:T(8,128)(2,1)S(1)}, bf16[2,320,128]{2,1,0:T(8,128)(2,1)S(1)}, u32[]{:S(2)}, u32[]{:S(2)}) %collective-permute-start) | collective-permute-done | bytes 163872 | tf_op jit(solution)/shard_map/ppermute | solution.py:15
  78.8 17.7 %all_gather.13 = bf16[320,1024]{1,0:T(8,128)(2,1)S(1)} all-gather(bf16[320,128]{1,0:T(8,128)(2,1)S(1)} %fusion.19), channel_id=1, replica_groups=mesh['section'=8,'eg'=4,'q'=8,'dp'=2] {'q'}, dimensions={1}, use_global_device_ids=true | all-gather | bytes 737280 | tf_op jit(solution)/shard_map/all_gather | solution.py:67
  96.5 1.7 convolution_convert_fusion.3
  98.6 1.4 reshape.131
  100.0 6.1 %all-to-all-start.2 = ((bf16[64,2,1120]{2,1,0:T(2,128)(2,1)}), bf16[64,2,1120]{2,1,0:T(2,128)(2,1)S(1)}, u32[]{:S(2)}, u32[]{:S(2)}) async-start(bf16[64,2,1120]{2,1,0:T(2,128)(2,1)} %reshape.131), calls=%async_computation.2 | async-start | bytes 589824 | tf_op jit(solution)/shard_map/all_to_all | solution.py:73
  106.3 13.8 %all-to-all-done.2 = bf16[64,2,1120]{2,1,0:T(2,128)(2,1)S(1)} async-done(((bf16[64,2,1120]{2,1,0:T(2,128)(2,1)}), bf16[64,2,1120]{2,1,0:T(2,128)(2,1)S(1)}, u32[]{:S(2)}, u32[]{:S(2)}) %all-to-all-start.2) | async-done | bytes 286752 | tf_op jit(solution)/shard_map/all_to_all | solution.py:73
  120.0 0.6 reshape.132
  120.6 0.2 copy.62
  120.9 0.4 reshape.133
  121.3 0.7 gather_fusion
  122.1 0.3 reshape.142
  122.4 0.6 multiply_reduce_fusion.1
  123.1 3.2 %collective-permute-start.1 = (bf16[8,7168]{1,0:T(8,128)(2,1)S(1)}, bf16[8,7168]{1,0:T(8,128)(2,1)S(1)}, u32[]{:S(2)}, u32[]{:S(2)}) collective-permute-start(bf16[8,7168]{1,0:T(8,128)(2,1)S(1)} %fusion.15), channel_id=1, source_target_pairs={{0,64},{64,128},{128,192},{192,256},{256,320},{320,384},{384,448},... | collective-permute-start | bytes 344072 | tf_op jit(solution)/shard_map/ppermute | solution.py:15
  126.4 4.7 %collective-permute-done.1 = bf16[8,7168]{1,0:T(8,128)(2,1)S(1)} collective-permute-done((bf16[8,7168]{1,0:T(8,128)(2,1)S(1)}, bf16[8,7168]{1,0:T(8,128)(2,1)S(1)}, u32[]{:S(2)}, u32[]{:S(2)}) %collective-permute-start.1) | collective-permute-done | bytes 114720 | tf_op jit(solution)/shard_map/ppermute | solution.py:15
  131.2 0.3 convolution_convert_fusion
  131.5 0.2 reshape_reshape.7
  132.1 12.5 %all_to_all.26 = bf16[8,140,128]{2,1,0:T(8,128)(2,1)S(1)} all-to-all(bf16[8,140,128]{2,1,0:T(8,128)(2,1)S(1)} %copy.67), channel_id=1, replica_groups=mesh['section'=8,'eg'=4,'q'=8,'dp'=2] {'eg','dp'}, dimensions={0} | all-to-all | bytes 573440 | tf_op jit(solution)/shard_map/all_to_all | solution.py:56
  144.6 0.8 copy.68
  145.4 30.6 %all-gather.5.cloned.1.call-done = bf16[5,64,3584]{2,1,0:T(8,128)(2,1)} async-done(((bf16[5,8,3584]{2,1,0:T(8,128)(2,1)}), bf16[5,64,3584]{2,1,0:T(8,128)(2,1)}) %all-gather.5.cloned.1.call-update) | async-done | bytes 2293776 | tf_op jit(solution)/shard_map/all_gather | solution.py:58
  176.0 2.4 %fusion.34 = (bf16[2,320,128]{2,1,0:T(8,128)(2,1)S(1)}, f32[2,320,128]{2,1,0:T(8,128)S(1)}) fusion(bf16[320,3584,1]{1,0,2:T(8,128)(2,1)} %bitcast.119, bf16[2,128,3584]{2,1,0:T(8,128)(2,1)S(1)} %bitcast.107), kind=kOutput, calls=%fused_computation.78 | convolution fusion | flops 587284480 | bytes 4620288 | tf_op jit(solution)/shard_map/dot_general | solution.py:63
  178.4 2.2 collective-permute-start.2
  180.6 5.2 %collective-permute-done.2 = bf16[2,320,128]{2,1,0:T(8,128)(2,1)S(1)} collective-permute-done((bf16[2,320,128]{2,1,0:T(8,128)(2,1)S(1)}, bf16[2,320,128]{2,1,0:T(8,128)(2,1)S(1)}, u32[]{:S(2)}, u32[]{:S(2)}) %collective-permute-start.2) | collective-permute-done | bytes 163872 | tf_op jit(solution)/shard_map/ppermute | solution.py:15
  185.9 17.7 %all_gather.15 = bf16[320,1024]{1,0:T(8,128)(2,1)S(1)} all-gather(bf16[320,128]{1,0:T(8,128)(2,1)S(1)} %fusion.17), channel_id=1, replica_groups=mesh['section'=8,'eg'=4,'q'=8,'dp'=2] {'q'}, dimensions={1}, use_global_device_ids=true | all-gather | bytes 737280 | tf_op jit(solution)/shard_map/all_gather | solution.py:67
  203.6 1.7 convolution_convert_fusion.2
  205.6 1.4 reshape.138
  207.0 7.8 %all-to-all-start.4 = ((bf16[64,2,1120]{2,1,0:T(2,128)(2,1)}), bf16[64,2,1120]{2,1,0:T(2,128)(2,1)S(1)}, u32[]{:S(2)}, u32[]{:S(2)}) async-start(bf16[64,2,1120]{2,1,0:T(2,128)(2,1)} %reshape.138), calls=%async_computation.4 | async-start | bytes 589824 | tf_op jit(solution)/shard_map/all_to_all | solution.py:73
  214.9 13.8 %all-to-all-done.4 = bf16[64,2,1120]{2,1,0:T(2,128)(2,1)S(1)} async-done(((bf16[64,2,1120]{2,1,0:T(2,128)(2,1)}), bf16[64,2,1120]{2,1,0:T(2,128)(2,1)S(1)}, u32[]{:S(2)}, u32[]{:S(2)}) %all-to-all-start.4) | async-done | bytes 286752 | tf_op jit(solution)/shard_map/all_to_all | solution.py:73
  228.7 0.6 reshape.139
  229.3 0.2 copy.70
  229.6 0.4 reshape.140
  229.9 0.7 gather_fusion.1
  230.8 0.3 reshape.143
  231.0 0.6 multiply_reduce_fusion
  231.7 0.7 fusion.21
  (53 shorter events, 3.0 us)
Async XLA Ops:
  6.5 61.8 %all-gather.3.cloned.1.call-start = ((), (), s32[]{:S(2)}) async-start(), calls=%async_computation.5 | async-start | bytes 2580480 | tf_op jit(solution)/shard_map/all_gather | solution.py:58
  11.5 31.1 %copy-start.2 = (bf16[1,3584,128]{2,1,0:T(8,128)(2,1)S(1)}, bf16[1,3584,128]{2,1,0:T(8,128)(2,1)}, u32[]{:S(2)}) copy-start(bf16[1,3584,128]{2,1,0:T(8,128)(2,1)} %param.12) | copy-start | bytes 2752516
  34.4 62.1 %all-to-all-start.1 = ((bf16[8,448,128]{2,1,0:T(8,128)(2,1)}), bf16[8,448,128]{2,1,0:T(8,128)(2,1)}, u32[]{:S(2)}, u32[]{:S(2)}) async-start(bf16[8,448,128]{2,1,0:T(8,128)(2,1)} %bitcast.18), calls=%async_computation.1 | async-start | bytes 1835008 | tf_op jit(solution)/shard_map/all_to_all | solution.py:91
  71.3 7.4 %collective-permute-start = (bf16[2,320,128]{2,1,0:T(8,128)(2,1)S(1)}, bf16[2,320,128]{2,1,0:T(8,128)(2,1)S(1)}, u32[]{:S(2)}, u32[]{:S(2)}) collective-permute-start(bf16[2,320,128]{2,1,0:T(8,128)(2,1)S(1)} %get-tuple-element.16), channel_id=1, source_target_pairs={{0,1},{1,0},{2,3},{3,2},{4,5},{5,4},{6,7},{7,6},{8,9},{9,8},{10,11... | collective-permute-start | bytes 491528 | tf_op jit(solution)/shard_map/ppermute | solution.py:15
  96.5 9.7 %copy-start.4 = (f32[1,2,8,2]{2,3,1,0:T(2,128)S(1)}, f32[1,2,8,2]{2,3,1,0:T(2,128)}, u32[]{:S(2)}) copy-start(f32[1,2,8,2]{2,3,1,0:T(2,128)} %param.15) | copy-start | bytes 388
  100.0 20.1 %all-to-all-start.2 = ((bf16[64,2,1120]{2,1,0:T(2,128)(2,1)}), bf16[64,2,1120]{2,1,0:T(2,128)(2,1)S(1)}, u32[]{:S(2)}, u32[]{:S(2)}) async-start(bf16[64,2,1120]{2,1,0:T(2,128)(2,1)} %reshape.131), calls=%async_computation.2 | async-start | bytes 589824 | tf_op jit(solution)/shard_map/all_to_all | solution.py:73
  106.1 69.8 %all-gather.5.cloned.1.call-start = ((), (), s32[]{:S(2)}) async-start(), calls=%async_computation.6 | async-start | bytes 2580480 | tf_op jit(solution)/shard_map/all_gather | solution.py:58
  121.3 1.8 copy-start.1
  121.3 10.0 %copy-start.3 = (f32[1,7168]{1,0:T(1,128)S(1)}, f32[1,7168]{1,0:T(1,128)}, u32[]{:S(2)}) copy-start(f32[1,7168]{1,0:T(1,128)} %param.10) | copy-start | bytes 86020
  123.0 52.9 %copy-start = (bf16[256,3584]{1,0:T(8,128)(2,1)S(1)}, bf16[256,3584]{1,0:T(8,128)(2,1)}, u32[]{:S(2)}) copy-start(bf16[256,3584]{1,0:T(8,128)(2,1)} %copy.59) | copy-start | bytes 5505028
  123.1 8.0 %collective-permute-start.1 = (bf16[8,7168]{1,0:T(8,128)(2,1)S(1)}, bf16[8,7168]{1,0:T(8,128)(2,1)S(1)}, u32[]{:S(2)}, u32[]{:S(2)}) collective-permute-start(bf16[8,7168]{1,0:T(8,128)(2,1)S(1)} %fusion.15), channel_id=1, source_target_pairs={{0,64},{64,128},{128,192},{192,256},{256,320},{320,384},{384,448},... | collective-permute-start | bytes 344072 | tf_op jit(solution)/shard_map/ppermute | solution.py:15
  178.4 7.4 %collective-permute-start.2 = (bf16[2,320,128]{2,1,0:T(8,128)(2,1)S(1)}, bf16[2,320,128]{2,1,0:T(8,128)(2,1)S(1)}, u32[]{:S(2)}, u32[]{:S(2)}) collective-permute-start(bf16[2,320,128]{2,1,0:T(8,128)(2,1)S(1)} %get-tuple-element.18), channel_id=1, source_target_pairs={{0,1},{1,0},{2,3},{3,2},{4,5},{5,4},{6,7},{7,6},{8,9},{9,8},{10,11... | collective-permute-start | bytes 491528 | tf_op jit(solution)/shard_map/ppermute | solution.py:15
  207.0 21.7 %all-to-all-start.4 = ((bf16[64,2,1120]{2,1,0:T(2,128)(2,1)}), bf16[64,2,1120]{2,1,0:T(2,128)(2,1)S(1)}, u32[]{:S(2)}, u32[]{:S(2)}) async-start(bf16[64,2,1120]{2,1,0:T(2,128)(2,1)} %reshape.138), calls=%async_computation.4 | async-start | bytes 589824 | tf_op jit(solution)/shard_map/all_to_all | solution.py:73
Sparse Core Ops, SparseCore 0:
  34.5 33.7 all-gather.2
  145.5 30.4 all-gather.4
